TPU v7x, 256 devices: a whole 4x4x8 slice. The times are simulated.
256 devices in a mesh: wide: 32 (over x, z), narrow: 8 (over y, core).
Axes of the slice: x: 4, y: 4, z: 8, core: 2. Of those that a mesh axis runs over, the one named last changes fastest.
Arguments:
- embeddings: bfloat16 [524288, 1024], P(('wide', 'narrow')), may hold values from -6 to 6
- level1_ids: int32 [524288], P(('wide', 'narrow')), may hold values from 0 to 32767, as said below
- block_counts: int32 [8192], P(('wide', 'narrow')), may hold values from 1 to 64, as said below
- level1_old: bfloat16 [32768, 1024], P('wide'), may hold values from -6 to 6
- level2_old: bfloat16 [4096, 1024], P('narrow'), may hold values from -6 to 6
- level2_ids: int32 [32768], P('wide'), may hold values from 0 to 4095
Outputs:
- level1_new: bfloat16 [32768, 1024], P('wide')
- level2_new: bfloat16 [4096, 1024], P('narrow')
- split_weights: float32 [4096], P('narrow')
Inputs may be any that keep to these rules, and one draw needn't show every extreme that they name: `level1_ids`: in every device's rows, the slots of block b (slot index divided by 64, modulo 32) name level-1 centroids b * 1024 to (b + 1) * 1024 - 1. `block_counts`: at most 64 live slots a block; every device has a block with exactly 64.
All inputs are finite; a program needn't handle non-finite values.
Results may differ from a plain program's by a relative error of at most 0.013.
Values may be sent and summed in bfloat16 or wider, within the bound.
No kernel may reach another device: no remote copies, remote signals or barrier semaphores. Data moves between devices by JAX's collectives and lax.ppermute only.
A program may use at most 64 MiB of HBM per device.

v0:
```python
import jax
import jax.numpy as jnp
from jax import lax
from jax.sharding import PartitionSpec as P


def owner_sums(rows_flat, ids_flat, owner_base, owner_size):
    owner_index = ids_flat - owner_base
    owner_table = owner_index[:, None] == lax.broadcasted_iota(jnp.int32, (1, owner_size), 1)
    row_sums = lax.dot_general(
        owner_table.astype(jnp.bfloat16),
        rows_flat,
        (((0,), (0,)), ((), ())),
        preferred_element_type=jnp.float32,
    )
    row_counts = jnp.sum(owner_table.astype(jnp.float32), axis=0)
    return (row_sums, row_counts)


def blocked_sums(rows_grouped, ids_grouped, owner_base, owner_size):
    groups = rows_grouped.shape[0]
    steps = 4
    width = rows_grouped.shape[-1]
    rows_steps = rows_grouped.reshape(steps, -1, width)
    ids_steps = ids_grouped.reshape(steps, -1)

    def accumulate(carry, items):
        part_sums, part_counts = owner_sums(items[0], items[1], owner_base, owner_size)
        return ((carry[0] + part_sums, carry[1] + part_counts), None)

    start = (jnp.zeros((owner_size, width), jnp.float32), jnp.zeros((owner_size,), jnp.float32))
    totals, _ = lax.scan(accumulate, start, (rows_steps, ids_steps))
    return totals


def local(embeddings, level1_ids, block_counts, level1_old, level2_old, level2_ids):
    wide_count = lax.axis_size("wide")
    narrow_count = lax.axis_size("narrow")
    slot_count = embeddings.shape[0] // wide_count
    feature_dim = embeddings.shape[1]
    owner_size = level1_old.shape[0]
    owner_base = lax.axis_index("wide") * owner_size
    block_rows = embeddings.reshape(wide_count, slot_count, feature_dim)
    position = lax.broadcasted_iota(jnp.int32, (wide_count, slot_count), 1)
    live_slots = position < block_counts[:, None]
    sent_ids = jnp.where(live_slots, level1_ids.reshape(wide_count, slot_count), -1)
    got_rows, got_ids = (
        lax.all_to_all(block_rows, "wide", split_axis=0, concat_axis=0, tiled=True),
        lax.all_to_all(sent_ids, "wide", split_axis=0, concat_axis=0, tiled=True),
    )
    row_sums, row_counts = blocked_sums(got_rows, got_ids, owner_base, owner_size)
    full_sums, full_counts = (
        lax.psum(row_sums.astype(jnp.bfloat16), "narrow").astype(jnp.float32),
        lax.psum(row_counts.astype(jnp.bfloat16), "narrow").astype(jnp.float32),
    )
    level1_new = (
        (4.0 * level1_old.astype(jnp.float32) + full_sums) / (4.0 + full_counts)[:, None]
    ).astype(jnp.bfloat16)
    group_size = level2_old.shape[0]
    group_index = level2_ids - lax.axis_index("narrow") * group_size
    group_table = group_index[:, None] == lax.broadcasted_iota(jnp.int32, (1, group_size), 1)
    group_sums = lax.dot_general(
        group_table.astype(jnp.bfloat16),
        level1_new,
        (((0,), (0,)), ((), ())),
        preferred_element_type=jnp.float32,
    )
    group_float = group_table.astype(jnp.float32)
    group_counts = jnp.sum(group_float, axis=0)
    level1_float = level1_new.astype(jnp.float32)
    squares = jnp.sum(level1_float * level1_float, axis=1)
    group_squares = jnp.dot(squares, group_float, precision=lax.Precision.HIGHEST)
    sums_two, counts_two, squares_two = (
        lax.psum(group_sums.astype(jnp.bfloat16), "wide").astype(jnp.float32),
        lax.psum(group_counts.astype(jnp.bfloat16), "wide").astype(jnp.float32),
        lax.psum(group_squares.astype(jnp.bfloat16), "wide").astype(jnp.float32),
    )
    means_two = (4.0 * level2_old.astype(jnp.float32) + sums_two) / (4.0 + counts_two)[:, None]
    inertia = (
        squares_two
        - 2.0 * jnp.sum(means_two * sums_two, axis=1)
        + counts_two * jnp.sum(means_two * means_two, axis=1)
    )
    inertia_sum = lax.psum(jnp.sum(inertia), "narrow")
    centroid_total = float(group_size * narrow_count)
    split_weights = centroid_total * inertia / inertia_sum
    return (level1_new, means_two.astype(jnp.bfloat16), split_weights)


def solution(mesh):
    return jax.shard_map(
        local,
        mesh=mesh,
        in_specs=(
            P(("wide", "narrow"), None),
            P(("wide", "narrow")),
            P(("wide", "narrow")),
            P("wide", None),
            P("narrow", None),
            P("wide"),
        ),
        out_specs=(P("wide", None), P("narrow", None), P("narrow")),
        check_vma=False,
    )
```

profile of v0, /device:TPU:1, one launch (start us, length us, event | category | flops | bytes accessed | tf_op | source)
XLA Modules:
  0.0 406.6 jit_solution(5804267014183993663)
XLA Ops:
  7.2 0.8 reshape.66
  7.9 0.8 compare_select_fusion
  8.7 20.3 %all_to_all.11 = s32[32,1,64]{2,1,0:T(1,128)S(1)} all-to-all(s32[32,1,64]{2,1,0:T(1,128)S(1)} %compare_select_fusion), channel_id=1, replica_groups=mesh['wide'=32,'narrow'=8] {'wide'}, dimensions={0} | all-to-all | bytes 16384 | tf_op jit(solution)/shard_map/all_to_all | solution.py:49
  29.0 4.9 %all-to-all-start.1 = ((bf16[32,64,1024]{2,1,0:T(8,128)(2,1)}), bf16[32,64,1024]{2,1,0:T(8,128)(2,1)}, u32[]{:S(2)}, u32[]{:S(2)}) async-start(bf16[32,64,1024]{2,1,0:T(8,128)(2,1)} %bitcast.14), calls=%async_computation.1 | async-start | bytes 8388608 | tf_op jit(solution)/shard_map/all_to_all | solution.py:48
  33.9 0.0 all-reduce.4.cloned.1.call-start
  33.9 0.5 broadcast.46
  34.5 0.7 reduce.3
  35.2 0.1 reshape.67
  35.2 95.2 %all-to-all-done.1 = bf16[32,64,1024]{2,1,0:T(8,128)(2,1)} async-done(((bf16[32,64,1024]{2,1,0:T(8,128)(2,1)}), bf16[32,64,1024]{2,1,0:T(8,128)(2,1)}, u32[]{:S(2)}, u32[]{:S(2)}) %all-to-all-start.1) | async-done | bytes 4194336 | tf_op jit(solution)/shard_map/all_to_all | solution.py:48
  130.4 23.5 %while.13 = (s32[]{:T(128)}, f32[1024,1024]{1,0:T(8,128)}, f32[1024]{0:T(1024)S(1)}, s32[4,512]{1,0:T(4,128)S(1)}, s32[]{:T(128)}, /*index=5*/bf16[4,512,1024]{2,1,0:T(8,128)(2,1)}, s32[]{:T(128)}, s32[]{:T(128)}) while((s32[]{:T(128)}, f32[1024,1024]{1,0:T(8,128)}, f32[1024]{0:T(1024)S(1)}, s32[4,512]{1,0:T(4,128)S(1)}, ...), condition=%wide.region_2.3_spmd.clone, body=%wide.region_0.2_spmd.clone.sunk | while | flops 1077937664 | bytes 9462376 | solution.py:32
  130.4 4.6 %select_add_fusion.4 = f32[1024,1024]{1,0:T(8,128)} fusion(f32[1024,1024]{1,0:T(8,128)} %get-tuple-element.124, pred[]{:T(512)S(6)} %compare.3, bf16[4,512,1024]{2,1,0:T(8,128)(2,1)} %get-tuple-element.136, s32[]{:T(128)} %get-tuple-element.123, s32[512]{0:T(512)S(1)} %bitcast.15), kind=kOutput, calls=%fused_computation.clone.1 | convolution fusion | flops 1076363264 | bytes 9439745 | tf_op jit(solution)/shard_map/while/body/eval_jaxpr/dot_general | solution.py:10
  135.0 0.3 convert_reduce_fusion.3
  135.3 5.9 %select_add_fusion.4 = f32[1024,1024]{1,0:T(8,128)} fusion(f32[1024,1024]{1,0:T(8,128)} %get-tuple-element.124, pred[]{:T(512)S(6)} %compare.3, bf16[4,512,1024]{2,1,0:T(8,128)(2,1)} %get-tuple-element.136, s32[]{:T(128)} %get-tuple-element.123, s32[512]{0:T(512)S(1)} %bitcast.15), kind=kOutput, calls=%fused_computation.clone.1 | convolution fusion | flops 1076363264 | bytes 9439745 | tf_op jit(solution)/shard_map/while/body/eval_jaxpr/dot_general | solution.py:10
  141.2 0.3 convert_reduce_fusion.3
  141.5 5.9 %select_add_fusion.4 = f32[1024,1024]{1,0:T(8,128)} fusion(f32[1024,1024]{1,0:T(8,128)} %get-tuple-element.124, pred[]{:T(512)S(6)} %compare.3, bf16[4,512,1024]{2,1,0:T(8,128)(2,1)} %get-tuple-element.136, s32[]{:T(128)} %get-tuple-element.123, s32[512]{0:T(512)S(1)} %bitcast.15), kind=kOutput, calls=%fused_computation.clone.1 | convolution fusion | flops 1076363264 | bytes 9439745 | tf_op jit(solution)/shard_map/while/body/eval_jaxpr/dot_general | solution.py:10
  147.4 0.3 convert_reduce_fusion.3
  147.7 5.9 %select_add_fusion.4 = f32[1024,1024]{1,0:T(8,128)} fusion(f32[1024,1024]{1,0:T(8,128)} %get-tuple-element.124, pred[]{:T(512)S(6)} %compare.3, bf16[4,512,1024]{2,1,0:T(8,128)(2,1)} %get-tuple-element.136, s32[]{:T(128)} %get-tuple-element.123, s32[512]{0:T(512)S(1)} %bitcast.15), kind=kOutput, calls=%fused_computation.clone.1 | convolution fusion | flops 1076363264 | bytes 9439745 | tf_op jit(solution)/shard_map/while/body/eval_jaxpr/dot_general | solution.py:10
  153.6 0.3 convert_reduce_fusion.3
  153.9 3.8 convert_element_type.54
  157.7 0.0 copy-start.3
  157.7 0.0 copy-start
  157.7 0.0 all-reduce.4.cloned.1.call-update
  157.7 0.0 all-reduce.6.cloned.1.call-start
  157.8 0.6 copy-done.3
  158.4 13.5 %psum.43 = bf16[1024]{0:T(1024)(128)(2,1)S(1)} all-reduce(bf16[1024]{0:T(1024)(128)(2,1)S(1)} %convert_element_type.56), channel_id=1, replica_groups=mesh['wide'=32,'narrow'=8] {'narrow'}, use_global_device_ids=true, to_apply=%region_4.5 | all-reduce | flops 1024 | bytes 4096 | tf_op jit(solution)/shard_map/psum | solution.py:54
  171.9 52.4 %all-reduce.4.cloned.1.call-done = bf16[1024,1024]{1,0:T(8,128)(2,1)} async-done(((bf16[1024,1024]{1,0:T(8,128)(2,1)}), bf16[1024,1024]{1,0:T(8,128)(2,1)}) %all-reduce.4.cloned.1.call-update) | async-done | bytes 2097168 | tf_op jit(solution)/shard_map/psum | solution.py:53
  224.3 0.0 copy-done
  224.3 2.7 multiply_reduce_fusion
  227.0 0.0 copy-start.1
  227.1 1.3 copy-done.1
  228.4 2.3 fusion.8
  230.7 0.0 copy-start.2
  230.7 0.0 all-reduce.6.cloned.1.call-update
  230.7 0.3 convert_reduce_fusion.1
  231.0 0.8 fusion.6
  231.8 61.0 %all-reduce = (bf16[512]{0:T(512)(128)(2,1)S(1)}, bf16[512]{0:T(512)(128)(2,1)S(1)}) all-reduce(bf16[512]{0:T(512)(128)(2,1)S(1)} %convert_reduce_fusion.1, bf16[512]{0:T(512)(128)(2,1)S(1)} %convert_element_type.67), channel_id=1, replica_groups=mesh['wide'=32,'narrow'=8] {'wide'}, use_global_device_ids=true, to_apply=%region_7.8 | all-reduce | flops 1024 | bytes 4096 | tf_op jit(solution)/shard_map/psum | solution.py:75
  292.9 84.4 %all-reduce.6.cloned.1.call-done = bf16[512,1024]{1,0:T(8,128)(2,1)} async-done(((bf16[512,1024]{1,0:T(8,128)(2,1)}), bf16[512,1024]{1,0:T(8,128)(2,1)}) %all-reduce.6.cloned.1.call-update) | async-done | bytes 1048592 | tf_op jit(solution)/shard_map/psum | solution.py:74
  377.2 0.0 copy-done.2
  377.2 2.9 fusion.5
  380.2 0.6 fusion.12
  380.8 17.7 %psum.47 = f32[]{:T(128)} all-reduce(f32[]{:T(128)} %fusion.12), channel_id=1, replica_groups=mesh['wide'=32,'narrow'=8] {'narrow'}, use_global_device_ids=true, to_apply=%region_13.14 | all-reduce | flops 1 | bytes 8 | tf_op jit(solution)/shard_map/psum | solution.py:84
  398.5 1.3 multiply_divide_fusion
  (15 shorter events, 0.1 us)
Async XLA Ops:
  29.0 101.4 %all-to-all-start.1 = ((bf16[32,64,1024]{2,1,0:T(8,128)(2,1)}), bf16[32,64,1024]{2,1,0:T(8,128)(2,1)}, u32[]{:S(2)}, u32[]{:S(2)}) async-start(bf16[32,64,1024]{2,1,0:T(8,128)(2,1)} %bitcast.14), calls=%async_computation.1 | async-start | bytes 8388608 | tf_op jit(solution)/shard_map/all_to_all | solution.py:48
  33.9 190.5 %all-reduce.4.cloned.1.call-start = ((), (), s32[]{:S(2)}) async-start(), calls=%async_computation.2 | async-start | bytes 4194304 | tf_op jit(solution)/shard_map/psum | solution.py:53
  157.7 0.7 copy-start.3
  157.7 66.6 %copy-start = (bf16[1024,1024]{1,0:T(8,128)(2,1)S(1)}, bf16[1024,1024]{1,0:T(8,128)(2,1)}, u32[]{:S(2)}) copy-start(bf16[1024,1024]{1,0:T(8,128)(2,1)} %param.11) | copy-start | bytes 6291460
  157.7 219.5 %all-reduce.6.cloned.1.call-start = ((), (), s32[]{:S(2)}) async-start(), calls=%async_computation.3 | async-start | bytes 2097152 | tf_op jit(solution)/shard_map/psum | solution.py:74
  227.0 1.3 copy-start.1
  230.7 146.5 %copy-start.2 = (bf16[512,1024]{1,0:T(8,128)(2,1)S(1)}, bf16[512,1024]{1,0:T(8,128)(2,1)}, u32[]{:S(2)}) copy-start(bf16[512,1024]{1,0:T(8,128)(2,1)} %param.12) | copy-start | bytes 3145732
Sparse Core Ops, SparseCore 0:
  157.9 66.4 all-reduce.3
  230.8 146.3 all-reduce.5
where the time goes:
time: 407 us
  waiting for transfers between devices  232 us (57%)
  blocking collectives  113 us (28%)
  matrix products  25.3 us (6%)
  other arithmetic  14.3 us (4%)
  between operations  14.1 us (3%)
  starting transfers between devices  4.93 us (1%)
    all_to_all x1, waiting for transfers between devices, local(): lax.all_to_all(block_rows, 'wide', split_axis=0, concat_axis=0, tiled=True)  95.2 us
    psum x1, waiting for transfers between devices, local(): lax.psum(group_sums.astype(jnp.bfloat16), 'wide').astype(jnp.float32)  84.4 us
    psum x1, blocking collectives, local(): lax.psum(group_counts.astype(jnp.bfloat16), 'wide').astype(jnp.float32)  61 us
    psum x1, waiting for transfers between devices, local(): lax.psum(row_sums.astype(jnp.bfloat16), 'narrow').astype(jnp.float32)  52.4 us
    dot_general x4, matrix products, owner_sums(): lax.dot_general(owner_table.astype(jnp.bfloat16), rows_flat, (((0,), (0,)...  22.2 us
    all_to_all x1, blocking collectives, local(): lax.all_to_all(sent_ids, 'wide', split_axis=0, concat_axis=0, tiled=True)  20.3 us
    psum x1, blocking collectives, local(): inertia_sum = lax.psum(jnp.sum(inertia), 'narrow')  17.7 us
    psum x1, blocking collectives, local(): lax.psum(row_counts.astype(jnp.bfloat16), 'narrow').astype(jnp.float32)  13.5 us
  transfers between devices with their start and end apart: 3, of which 3 were waited for; matrix products, arithmetic and copies ran while one was open for 1% of the time, Pallas kernels for 0%

commit v1 on v0

v1 whole, which is shorter than its diff:
```python
import jax
import jax.numpy as jnp
from jax import lax
from jax.sharding import PartitionSpec as P


def split_whole(values, step):
    high = jnp.floor(values / step)
    return high, values - step * high


def split_float(values, pieces):
    out = []
    rest = values
    for _ in range(pieces):
        piece = rest.astype(jnp.bfloat16)
        out.append(piece)
        rest = rest - piece.astype(jnp.float32)
    return out


def pack_rows(body, extras, groups):
    rows, width = body.shape
    per = rows // groups
    flat_body = body.astype(jnp.bfloat16).reshape(groups, per * width)
    tail = jnp.stack([e.astype(jnp.bfloat16).reshape(groups, per) for e in extras], axis=1).reshape(groups, -1)
    pad = (-tail.shape[1]) % 128
    tail = jnp.pad(tail, ((0, 0), (0, pad)))
    return jnp.concatenate([flat_body, tail], axis=1)


def unpack_rows(packed, per, width, n_extras):
    body = packed[:, : per * width].reshape(-1, per, width)
    tail = packed[:, per * width : per * width + n_extras * per].reshape(-1, n_extras, per)
    return body, tail


def local(embeddings, level1_ids, block_counts, level1_old, level2_old, level2_ids):
    wide_count = lax.axis_size("wide")
    narrow_count = lax.axis_size("narrow")
    wide_index = lax.axis_index("wide")
    narrow_index = lax.axis_index("narrow")
    slot_count = embeddings.shape[0] // wide_count
    feature_dim = embeddings.shape[1]
    owner_size = level1_old.shape[0]
    owner_base = wide_index * owner_size
    block_rows = embeddings.reshape(wide_count, slot_count, feature_dim)
    position = lax.broadcasted_iota(jnp.int32, (wide_count, slot_count), 1)
    live_slots = position < block_counts[:, None]
    sent_ids = jnp.where(live_slots, level1_ids.reshape(wide_count, slot_count), -1)
    got_rows = lax.all_to_all(block_rows, "wide", split_axis=0, concat_axis=0, tiled=True)
    got_ids = lax.all_to_all(sent_ids, "wide", split_axis=0, concat_axis=0, tiled=True)

    owner_index = got_ids.reshape(-1) - owner_base
    owner_table = lax.broadcasted_iota(jnp.int32, (owner_size, 1), 0) == owner_index[None, :]
    row_sums = jnp.dot(
        owner_table.astype(jnp.bfloat16),
        got_rows.reshape(-1, feature_dim),
        preferred_element_type=jnp.float32,
    )
    row_counts = jnp.sum(owner_table.astype(jnp.float32), axis=1)

    sub_size = owner_size // narrow_count
    count_high, count_low = split_whole(row_counts, 16.0)
    sent_one = pack_rows(row_sums, [count_high, count_low], narrow_count)
    got_one = lax.all_to_all(sent_one, "narrow", split_axis=0, concat_axis=0, tiled=True)
    body_one, tail_one = unpack_rows(got_one, sub_size, feature_dim, 2)
    sub_sums = jnp.sum(body_one.astype(jnp.float32), axis=0)
    tail_sum = jnp.sum(tail_one.astype(jnp.float32), axis=0)
    sub_counts = 16.0 * tail_sum[0] + tail_sum[1]
    sub_old = lax.dynamic_slice_in_dim(level1_old, narrow_index * sub_size, sub_size, axis=0)
    sub_new = ((4.0 * sub_old.astype(jnp.float32) + sub_sums) / (4.0 + sub_counts)[:, None]).astype(jnp.bfloat16)
    sent_sub = jnp.broadcast_to(sub_new[None], (narrow_count,) + sub_new.shape)
    level1_new = lax.all_to_all(sent_sub, "narrow", split_axis=0, concat_axis=0, tiled=True).reshape(owner_size, feature_dim)

    group_size = level2_old.shape[0]
    group_index = level2_ids - narrow_index * group_size
    group_table = lax.broadcasted_iota(jnp.int32, (group_size, 1), 0) == group_index[None, :]
    group_sums = jnp.dot(group_table.astype(jnp.bfloat16), level1_new, preferred_element_type=jnp.float32)
    group_float = group_table.astype(jnp.float32)
    group_counts = jnp.sum(group_float, axis=1)
    level1_float = level1_new.astype(jnp.float32)
    squares = jnp.sum(level1_float * level1_float, axis=1)
    group_squares = jnp.sum(jnp.where(group_table, squares[None, :], 0.0), axis=1)

    part_size = group_size // wide_count
    squares_high, squares_low = split_float(group_squares, 2)
    counts_high, counts_low = split_whole(group_counts, 16.0)
    sent_two = pack_rows(group_sums, [squares_high, squares_low, counts_high, counts_low], wide_count)
    got_two = lax.all_to_all(sent_two, "wide", split_axis=0, concat_axis=0, tiled=True)
    body_two, tail_two = unpack_rows(got_two, part_size, feature_dim, 4)
    sums_two = jnp.sum(body_two.astype(jnp.float32), axis=0)
    tail_two = jnp.sum(tail_two.astype(jnp.float32), axis=0)
    squares_two = tail_two[0] + tail_two[1]
    counts_two = 16.0 * tail_two[2] + tail_two[3]
    old_two = lax.dynamic_slice_in_dim(level2_old, wide_index * part_size, part_size, axis=0)
    means_two = (4.0 * old_two.astype(jnp.float32) + sums_two) / (4.0 + counts_two)[:, None]
    inertia = (
        squares_two
        - 2.0 * jnp.sum(means_two * sums_two, axis=1)
        + counts_two * jnp.sum(means_two * means_two, axis=1)
    )

    inertia_pieces = split_float(inertia, 3)
    sent_three = pack_rows(means_two, inertia_pieces, 1)
    sent_three = jnp.broadcast_to(sent_three, (wide_count, sent_three.shape[1]))
    got_three = lax.all_to_all(sent_three, "wide", split_axis=0, concat_axis=0, tiled=True)
    body_three, tail_three = unpack_rows(got_three, part_size, feature_dim, 3)
    level2_new = body_three.reshape(group_size, feature_dim)
    tail_three = tail_three.astype(jnp.float32)
    inertia_all = ((tail_three[:, 0] + tail_three[:, 1]) + tail_three[:, 2]).reshape(group_size)
    inertia_sum = lax.psum(jnp.sum(inertia_all), "narrow")
    centroid_total = float(group_size * narrow_count)
    split_weights = centroid_total * inertia_all / inertia_sum
    return (level1_new, level2_new, split_weights)


def solution(mesh):
    return jax.shard_map(
        local,
        mesh=mesh,
        in_specs=(
            P(("wide", "narrow"), None),
            P(("wide", "narrow")),
            P(("wide", "narrow")),
            P("wide", None),
            P("narrow", None),
            P("wide"),
        ),
        out_specs=(P("wide", None), P("narrow", None), P("narrow")),
        check_vma=False,
    )
```

time: 407 us -> 367 us (0.902)
  waiting for transfers between devices: 232 us -> 173 us
  local copies, waits for them, and re-layouts: 3.3 us -> 59.6 us
  blocking collectives: 113 us -> 72.9 us
  matrix products: 25.3 us -> 9.1 us
  other arithmetic: 14.3 us -> 29.7 us
  starting transfers between devices: 4.93 us -> 20.3 us
  between operations: 14.1 us -> 0.82 us
    psum x2 -> x0, waiting for transfers between devices: 137 us -> none  [the longest x1 84.4 us: local(): lax.psum(group_sums.astype(jnp.bfloat16), 'wide').astype(jnp.float32)]
    all_to_all x0 -> x3, waiting for transfers between devices: none -> 77.6 us  [the longest x1 26.5 us: local(): lax.all_to_all(sent_one, 'narrow', split_axis=0, concat_axis=0, tiled=True)]
    psum x3 -> x1, blocking collectives: 92.3 us -> 15.9 us  [local(): inertia_sum = lax.psum(jnp.sum(inertia_all), 'narrow')]
    all_to_all x0 -> x1, blocking collectives: none -> 36.8 us  [local(): lax.all_to_all(sent_three, 'wide', split_axis=0, concat_axis=0, tiled=True)]
    unnamed x8 -> x13, local copies, waits for them, and re-layouts: 1.93 us -> 32.5 us
    dot_general x6 -> x2, matrix products: 25.3 us -> 9.1 us  [the longest x1 7.83 us: local(): jnp.dot(owner_table.astype(jnp.bfloat16), got_rows.reshape(-1, feature_di...]
    all_to_all x0 -> x3, starting transfers between devices: none -> 15.5 us  [the longest x1 6.02 us: local(): lax.all_to_all(sent_one, 'narrow', split_axis=0, concat_axis=0, tiled=True)]
    all_to_all x1 -> x4, other arithmetic: 0.69 us -> 12.5 us  [the longest x2 9.09 us: local(): lax.all_to_all(sent_one, 'narrow', split_axis=0, concat_axis=0, tiled=True)]
  transfers between devices with their start and end apart: 3 -> 4, of which waited for: 3 -> 4; matrix products, arithmetic and copies ran while one was open for 1% -> 0% of each run, Pallas kernels for 0% -> 0%
where the time goes in v1:
time: 367 us; the launch traced here: 365 us
  waiting for transfers between devices  173 us (47%)
  blocking collectives  72.9 us (20%)
  local copies, waits for them, and re-layouts  59.6 us (16%)
  other arithmetic  29.7 us (8%)
  starting transfers between devices  20.3 us (6%)
  matrix products  9.1 us (2%)
    all_to_all x1, waiting for transfers between devices, local(): lax.all_to_all(block_rows, 'wide', split_axis=0, concat_axis=0, tiled=True)  95.5 us
    all_to_all x1, blocking collectives, local(): lax.all_to_all(sent_three, 'wide', split_axis=0, concat_axis=0, tiled=True)  36.8 us
    unnamed x13, local copies, waits for them, and re-layouts  32.5 us
    all_to_all x1, waiting for transfers between devices, local(): lax.all_to_all(sent_one, 'narrow', split_axis=0, concat_axis=0, tiled=True)  26.5 us
    all_to_all x1, waiting for transfers between devices, local(): lax.all_to_all(sent_sub, 'narrow', split_axis=0, concat_axis=0, tiled=True)  26.3 us
    all_to_all x1, waiting for transfers between devices, local(): lax.all_to_all(sent_two, 'wide', split_axis=0, concat_axis=0, tiled=True)  24.7 us
    all_to_all x1, blocking collectives, local(): lax.all_to_all(sent_ids, 'wide', split_axis=0, concat_axis=0, tiled=True)  20.3 us
    psum x1, blocking collectives, local(): inertia_sum = lax.psum(jnp.sum(inertia_all), 'narrow')  15.9 us
  transfers between devices with their start and end apart: 4, of which 4 were waited for; matrix products, arithmetic and copies ran while one was open for 0% of the time, Pallas kernels for 0%

profile of v1, /device:TPU:1, one launch (start us, length us, event | category | flops | bytes accessed | tf_op | source)
XLA Modules:
  0.0 365.5 jit_solution(13682946781479271805)
XLA Ops:
  0.6 0.8 reshape.283
  1.4 0.8 compare_select_fusion.1
  2.2 20.3 %all_to_all.49 = s32[32,1,64]{2,1,0:T(1,128)S(1)} all-to-all(s32[32,1,64]{2,1,0:T(1,128)S(1)} %compare_select_fusion.1), channel_id=1, replica_groups=mesh['wide'=32,'narrow'=8] {'wide'}, dimensions={0} | all-to-all | bytes 16384 | tf_op jit(solution)/shard_map/all_to_all | solution.py:52
  22.5 4.9 %all-to-all-start.1 = ((bf16[32,64,1024]{2,1,0:T(8,128)(2,1)}), bf16[32,64,1024]{2,1,0:T(8,128)(2,1)}, u32[]{:S(2)}, u32[]{:S(2)}) async-start(bf16[32,64,1024]{2,1,0:T(8,128)(2,1)} %bitcast.53), calls=%async_computation.1 | async-start | bytes 8388608 | tf_op jit(solution)/shard_map/all_to_all | solution.py:51
  27.4 0.1 sub.69
  27.5 0.9 convert_reduce_fusion
  28.4 95.5 %all-to-all-done.1 = bf16[32,64,1024]{2,1,0:T(8,128)(2,1)} async-done(((bf16[32,64,1024]{2,1,0:T(8,128)(2,1)}), bf16[32,64,1024]{2,1,0:T(8,128)(2,1)}, u32[]{:S(2)}, u32[]{:S(2)}) %all-to-all-start.1) | async-done | bytes 4194336 | tf_op jit(solution)/shard_map/all_to_all | solution.py:51
  123.9 7.8 %fusion.4 = bf16[1024,1024]{1,0:T(8,128)(2,1)} fusion(bf16[2048,1024]{1,0:T(8,128)(2,1)} %bitcast.1, s32[2048]{0:T(1024)S(1)} %sub.69), kind=kOutput, calls=%fused_computation.15 | convolution fusion | flops 4298113024 | bytes 6299648 | tf_op jit(solution)/shard_map/dot_general | solution.py:56
  131.7 2.5 reshape.286
  134.3 4.8 %maximum_bitcast_fusion = bf16[8,1,131328]{2,0,1:T(8,128)(2,1)} fusion(bf16[8,256]{1,0:T(8,128)(2,1)S(1)} %maximum_bitcast_fusion.1, bf16[8,131072]{1,0:T(8,128)(2,1)S(1)} %reshape.286), kind=kLoop, calls=%fused_computation.8 | loop fusion | flops 4202496 | bytes 4202496 | tf_op jit(solution)/shard_map/all_to_all | solution.py:66
  139.1 0.5 broadcast.151
  139.6 4.3 %reduce.12 = bf16[8,131328]{1,0:T(8,128)(2,1)} reduce(bf16[8,1,131328]{2,0,1:T(8,128)(2,1)} %maximum_bitcast_fusion, bf16[]{:T(256)} %broadcast.151), dimensions={1}, to_apply=%copy.28.reduce_sub_computation | reduce | bytes 4202498 | tf_op jit(solution)/shard_map/all_to_all | solution.py:66
  143.9 3.5 reshape.302
  147.4 6.0 %all-to-all-start.2 = ((bf16[8,2,65664]{2,1,0:T(2,128)(2,1)}), bf16[8,2,65664]{2,1,0:T(2,128)(2,1)}, u32[]{:S(2)}, u32[]{:S(2)}) async-start(bf16[8,2,65664]{2,1,0:T(2,128)(2,1)} %reshape.302), calls=%async_computation.2 | async-start | bytes 4202496 | tf_op jit(solution)/shard_map/all_to_all | solution.py:66
  153.4 26.5 %all-to-all-done.2 = bf16[8,2,65664]{2,1,0:T(2,128)(2,1)} async-done(((bf16[8,2,65664]{2,1,0:T(2,128)(2,1)}), bf16[8,2,65664]{2,1,0:T(2,128)(2,1)}, u32[]{:S(2)}, u32[]{:S(2)}) %all-to-all-start.2) | async-done | bytes 2101280 | tf_op jit(solution)/shard_map/all_to_all | solution.py:66
  179.9 9.1 %reshape.303 = bf16[8,1,131328]{2,1,0:T(2,128)(2,1)} reshape(bf16[8,2,65664]{2,1,0:T(2,128)(2,1)} %all-to-all-done.2) | data formatting | bytes 4202496
  189.0 2.8 copy.41
  191.8 1.4 convert_reduce_fusion.1
  193.2 0.1 reduce_sum.112
  193.3 1.1 divide_convert_fusion
  194.3 1.6 broadcast_in_dim.36
  195.9 0.0 copy-start
  195.9 4.5 %all-to-all-start.3 = ((bf16[8,128,1024]{2,1,0:T(8,128)(2,1)}), bf16[8,128,1024]{2,1,0:T(8,128)(2,1)S(1)}, u32[]{:S(2)}, u32[]{:S(2)}) async-start(bf16[8,128,1024]{2,1,0:T(8,128)(2,1)} %broadcast_in_dim.36), calls=%async_computation.3 | async-start | bytes 4194304 | tf_op jit(solution)/shard_map/all_to_all | solution.py:74
  200.4 0.0 copy-done
  200.4 26.3 %all-to-all-done.3 = bf16[8,128,1024]{2,1,0:T(8,128)(2,1)S(1)} async-done(((bf16[8,128,1024]{2,1,0:T(8,128)(2,1)}), bf16[8,128,1024]{2,1,0:T(8,128)(2,1)S(1)}, u32[]{:S(2)}, u32[]{:S(2)}) %all-to-all-start.3) | async-done | bytes 2097184 | tf_op jit(solution)/shard_map/all_to_all | solution.py:74
  226.8 0.5 multiply_reduce_fusion
  227.3 0.6 select_reduce_fusion
  227.9 0.1 reduce_sum.116
  228.0 0.1 reduce_sum.118
  228.1 0.1 copy.29
  228.2 0.1 copy.37
  228.2 1.3 fusion.5
  229.5 1.3 reshape.289
  230.8 1.3 fusion.7
  232.1 2.1 reduce.13
  234.2 2.6 reshape.304
  236.9 4.9 %all-to-all-start.4 = ((bf16[32,2,8256]{2,1,0:T(2,128)(2,1)}), bf16[32,2,8256]{2,1,0:T(2,128)(2,1)S(1)}, u32[]{:S(2)}, u32[]{:S(2)}) async-start(bf16[32,2,8256]{2,1,0:T(2,128)(2,1)} %reshape.304), calls=%async_computation.4 | async-start | bytes 2129920 | tf_op jit(solution)/shard_map/all_to_all | solution.py:90
  241.8 24.7 %all-to-all-done.4 = bf16[32,2,8256]{2,1,0:T(2,128)(2,1)S(1)} async-done(((bf16[32,2,8256]{2,1,0:T(2,128)(2,1)}), bf16[32,2,8256]{2,1,0:T(2,128)(2,1)S(1)}, u32[]{:S(2)}, u32[]{:S(2)}) %all-to-all-start.4) | async-done | bytes 1056800 | tf_op jit(solution)/shard_map/all_to_all | solution.py:90
  266.5 3.6 reshape.305
  270.1 1.7 copy.42
  271.9 0.2 convert_reduce_fusion.2
  272.1 0.1 broadcast_add_fusion
  272.2 1.0 multiply_reduce_fusion.2
  273.2 0.1 copy.38
  273.2 0.1 convert_bitcast_fusion.3
  273.3 0.1 reshape.292
  273.4 0.2 fusion.10
  273.6 2.4 broadcast_in_dim.40
  276.1 9.1 %reduce.14 = bf16[32,16512]{1,0:T(8,128)(2,1)} reduce(bf16[32,1,16512]{2,1,0:T(2,128)(2,1)} %broadcast_in_dim.40, bf16[]{:T(256)} %broadcast.151), dimensions={1}, to_apply=%broadcast_in_dim.40.reduce_sub_computation | reduce | bytes 2113538 | tf_op jit(solution)/shard_map/broadcast_in_dim | solution.py:106
  285.1 1.8 reshape.306
  287.0 36.8 %all_to_all.50 = bf16[32,2,8256]{2,1,0:T(2,128)(2,1)} all-to-all(bf16[32,2,8256]{2,1,0:T(2,128)(2,1)S(1)} %reshape.306), channel_id=1, replica_groups=mesh['wide'=32,'narrow'=8] {'wide'}, dimensions={0} | all-to-all | bytes 2113536 | tf_op jit(solution)/shard_map/all_to_all | solution.py:107
  323.7 5.9 %reshape.307 = bf16[32,1,16512]{2,1,0:T(2,128)(2,1)} reshape(bf16[32,2,8256]{2,1,0:T(2,128)(2,1)} %all_to_all.50) | data formatting | bytes 2113536
  329.6 7.5 %copy.32 = bf16[32,1,16512]{0,2,1:T(8,128)(2,1)} copy(bf16[32,1,16512]{2,1,0:T(2,128)(2,1)} %reshape.307) | data formatting | bytes 2113536 | tf_op jit(solution)/shard_map/all_to_all | solution.py:107
  337.1 0.7 slice.71
  337.8 0.6 fusion.15
  338.4 3.7 %slice.70 = bf16[32,16384]{0,1:T(8,128)(2,1)} slice(bf16[32,16512]{0,1:T(8,128)(2,1)} %bitcast.48), slice={[0:32], [0:16384]} | slice | bytes 2097152 | tf_op jit(solution)/shard_map/slice | solution.py:33
  342.1 15.9 %psum.7 = f32[]{:T(128)} all-reduce(f32[]{:T(128)} %fusion.15), channel_id=1, replica_groups=mesh['wide'=32,'narrow'=8] {'narrow'}, use_global_device_ids=true, to_apply=%region_11.12 | all-reduce | flops 1 | bytes 8 | tf_op jit(solution)/shard_map/psum | solution.py:112
  358.0 0.7 multiply_divide_fusion
  358.6 0.1 copy.34
  358.7 0.7 div.39
  359.4 3.5 copy.33
  362.9 1.3 reshape_reshape.3
  364.2 1.3 copy.46
  (13 shorter events, 0.2 us)
Async XLA Ops:
  22.5 101.4 %all-to-all-start.1 = ((bf16[32,64,1024]{2,1,0:T(8,128)(2,1)}), bf16[32,64,1024]{2,1,0:T(8,128)(2,1)}, u32[]{:S(2)}, u32[]{:S(2)}) async-start(bf16[32,64,1024]{2,1,0:T(8,128)(2,1)} %bitcast.53), calls=%async_computation.1 | async-start | bytes 8388608 | tf_op jit(solution)/shard_map/all_to_all | solution.py:51
  147.4 32.5 %all-to-all-start.2 = ((bf16[8,2,65664]{2,1,0:T(2,128)(2,1)}), bf16[8,2,65664]{2,1,0:T(2,128)(2,1)}, u32[]{:S(2)}, u32[]{:S(2)}) async-start(bf16[8,2,65664]{2,1,0:T(2,128)(2,1)} %reshape.302), calls=%async_computation.2 | async-start | bytes 4202496 | tf_op jit(solution)/shard_map/all_to_all | solution.py:66
  195.9 4.5 %copy-start = (s32[1024]{0:T(1024)S(1)}, s32[1024]{0:T(1024)}, u32[]{:S(2)}) copy-start(s32[1024]{0:T(1024)} %param.11) | copy-start | bytes 12292
  195.9 30.9 %all-to-all-start.3 = ((bf16[8,128,1024]{2,1,0:T(8,128)(2,1)}), bf16[8,128,1024]{2,1,0:T(8,128)(2,1)S(1)}, u32[]{:S(2)}, u32[]{:S(2)}) async-start(bf16[8,128,1024]{2,1,0:T(8,128)(2,1)} %broadcast_in_dim.36), calls=%async_computation.3 | async-start | bytes 4194304 | tf_op jit(solution)/shard_map/all_to_all | solution.py:74
  236.9 29.7 %all-to-all-start.4 = ((bf16[32,2,8256]{2,1,0:T(2,128)(2,1)}), bf16[32,2,8256]{2,1,0:T(2,128)(2,1)S(1)}, u32[]{:S(2)}, u32[]{:S(2)}) async-start(bf16[32,2,8256]{2,1,0:T(2,128)(2,1)} %reshape.304), calls=%async_computation.4 | async-start | bytes 2129920 | tf_op jit(solution)/shard_map/all_to_all | solution.py:90

commit v2 on v1

--- a/solution.py
+++ b/solution.py
@@ -19,20 +19,13 @@
     return out
 
 
-def pack_rows(body, extras, groups):
-    rows, width = body.shape
-    per = rows // groups
-    flat_body = body.astype(jnp.bfloat16).reshape(groups, per * width)
-    tail = jnp.stack([e.astype(jnp.bfloat16).reshape(groups, per) for e in extras], axis=1).reshape(groups, -1)
-    pad = (-tail.shape[1]) % 128
-    tail = jnp.pad(tail, ((0, 0), (0, pad)))
-    return jnp.concatenate([flat_body, tail], axis=1)
-
-
-def unpack_rows(packed, per, width, n_extras):
-    body = packed[:, : per * width].reshape(-1, per, width)
-    tail = packed[:, per * width : per * width + n_extras * per].reshape(-1, n_extras, per)
-    return body, tail
+def pack_columns(body, extras):
+    rows = body.shape[0]
+    lane = lax.broadcasted_iota(jnp.int32, (rows, 128), 1)
+    tail = jnp.zeros((rows, 128), jnp.float32)
+    for place, extra in enumerate(extras):
+        tail = jnp.where(lane == place, extra.astype(jnp.float32)[:, None], tail)
+    return jnp.concatenate([body.astype(jnp.bfloat16), tail.astype(jnp.bfloat16)], axis=1)
 
 
 def local(embeddings, level1_ids, block_counts, level1_old, level2_old, level2_ids):
@@ -58,16 +51,19 @@
         got_rows.reshape(-1, feature_dim),
         preferred_element_type=jnp.float32,
     )
-    row_counts = jnp.sum(owner_table.astype(jnp.float32), axis=1)
+    row_counts = jnp.dot(
+        owner_table.astype(jnp.bfloat16),
+        jnp.ones((owner_index.shape[0], 128), jnp.bfloat16),
+        preferred_element_type=jnp.float32,
+    )[:, 0]
 
     sub_size = owner_size // narrow_count
     count_high, count_low = split_whole(row_counts, 16.0)
-    sent_one = pack_rows(row_sums, [count_high, count_low], narrow_count)
+    sent_one = pack_columns(row_sums, [count_high, count_low]).reshape(narrow_count, sub_size, -1)
     got_one = lax.all_to_all(sent_one, "narrow", split_axis=0, concat_axis=0, tiled=True)
-    body_one, tail_one = unpack_rows(got_one, sub_size, feature_dim, 2)
-    sub_sums = jnp.sum(body_one.astype(jnp.float32), axis=0)
-    tail_sum = jnp.sum(tail_one.astype(jnp.float32), axis=0)
-    sub_counts = 16.0 * tail_sum[0] + tail_sum[1]
+    sub_sums = jnp.sum(got_one[:, :, :feature_dim].astype(jnp.float32), axis=0)
+    tail_sum = jnp.sum(got_one[:, :, feature_dim : feature_dim + 2].astype(jnp.float32), axis=0)
+    sub_counts = 16.0 * tail_sum[:, 0] + tail_sum[:, 1]
     sub_old = lax.dynamic_slice_in_dim(level1_old, narrow_index * sub_size, sub_size, axis=0)
     sub_new = ((4.0 * sub_old.astype(jnp.float32) + sub_sums) / (4.0 + sub_counts)[:, None]).astype(jnp.bfloat16)
     sent_sub = jnp.broadcast_to(sub_new[None], (narrow_count,) + sub_new.shape)
@@ -77,8 +73,11 @@
     group_index = level2_ids - narrow_index * group_size
     group_table = lax.broadcasted_iota(jnp.int32, (group_size, 1), 0) == group_index[None, :]
     group_sums = jnp.dot(group_table.astype(jnp.bfloat16), level1_new, preferred_element_type=jnp.float32)
-    group_float = group_table.astype(jnp.float32)
-    group_counts = jnp.sum(group_float, axis=1)
+    group_counts = jnp.dot(
+        group_table.astype(jnp.bfloat16),
+        jnp.ones((group_index.shape[0], 128), jnp.bfloat16),
+        preferred_element_type=jnp.float32,
+    )[:, 0]
     level1_float = level1_new.astype(jnp.float32)
     squares = jnp.sum(level1_float * level1_float, axis=1)
     group_squares = jnp.sum(jnp.where(group_table, squares[None, :], 0.0), axis=1)
@@ -86,13 +85,13 @@
     part_size = group_size // wide_count
     squares_high, squares_low = split_float(group_squares, 2)
     counts_high, counts_low = split_whole(group_counts, 16.0)
-    sent_two = pack_rows(group_sums, [squares_high, squares_low, counts_high, counts_low], wide_count)
+    sent_two = pack_columns(group_sums, [squares_high, squares_low, counts_high, counts_low])
+    sent_two = sent_two.reshape(wide_count, part_size, -1)
     got_two = lax.all_to_all(sent_two, "wide", split_axis=0, concat_axis=0, tiled=True)
-    body_two, tail_two = unpack_rows(got_two, part_size, feature_dim, 4)
-    sums_two = jnp.sum(body_two.astype(jnp.float32), axis=0)
-    tail_two = jnp.sum(tail_two.astype(jnp.float32), axis=0)
-    squares_two = tail_two[0] + tail_two[1]
-    counts_two = 16.0 * tail_two[2] + tail_two[3]
+    sums_two = jnp.sum(got_two[:, :, :feature_dim].astype(jnp.float32), axis=0)
+    tail_two = jnp.sum(got_two[:, :, feature_dim : feature_dim + 4].astype(jnp.float32), axis=0)
+    squares_two = tail_two[:, 0] + tail_two[:, 1]
+    counts_two = 16.0 * tail_two[:, 2] + tail_two[:, 3]
     old_two = lax.dynamic_slice_in_dim(level2_old, wide_index * part_size, part_size, axis=0)
     means_two = (4.0 * old_two.astype(jnp.float32) + sums_two) / (4.0 + counts_two)[:, None]
     inertia = (
@@ -102,13 +101,12 @@
     )
 
     inertia_pieces = split_float(inertia, 3)
-    sent_three = pack_rows(means_two, inertia_pieces, 1)
-    sent_three = jnp.broadcast_to(sent_three, (wide_count, sent_three.shape[1]))
+    sent_three = pack_columns(means_two, inertia_pieces)
+    sent_three = jnp.broadcast_to(sent_three[None], (wide_count,) + sent_three.shape)
     got_three = lax.all_to_all(sent_three, "wide", split_axis=0, concat_axis=0, tiled=True)
-    body_three, tail_three = unpack_rows(got_three, part_size, feature_dim, 3)
-    level2_new = body_three.reshape(group_size, feature_dim)
-    tail_three = tail_three.astype(jnp.float32)
-    inertia_all = ((tail_three[:, 0] + tail_three[:, 1]) + tail_three[:, 2]).reshape(group_size)
+    level2_new = got_three[:, :, :feature_dim].reshape(group_size, feature_dim)
+    tail_three = got_three[:, :, feature_dim : feature_dim + 3].astype(jnp.float32)
+    inertia_all = ((tail_three[:, :, 0] + tail_three[:, :, 1]) + tail_three[:, :, 2]).reshape(group_size)
     inertia_sum = lax.psum(jnp.sum(inertia_all), "narrow")
     centroid_total = float(group_size * narrow_count)
     split_weights = centroid_total * inertia_all / inertia_sum

time: 367 us -> 307 us (0.84)
  local copies, waits for them, and re-layouts: 59.6 us -> 8.03 us
  other arithmetic: 29.7 us -> 12.8 us
  waiting for transfers between devices: 173 us -> 177 us
    unnamed x13 -> x6, local copies, waits for them, and re-layouts: 32.5 us -> 3.26 us
    all_to_all x4 -> x0, other arithmetic: 12.5 us -> none  [the longest x2 9.09 us: local(): lax.all_to_all(sent_one, 'narrow', split_axis=0, concat_axis=0, tiled=True)]
    broadcast_in_dim x1, other arithmetic: 9.06 us -> 0.23 us  [pack_columns(): tail = jnp.where(lane == place, extra.astype(jnp.float32)[:, None], tail)]
    all_to_all x2 -> x0, local copies, waits for them, and re-layouts: 7.99 us -> none  [the longest x1 7.48 us: local(): lax.all_to_all(sent_three, 'wide', split_axis=0, concat_axis=0, tiled=True)]
    slice x3 -> x1, local copies, waits for them, and re-layouts: 7.88 us -> 1.11 us  [local(): level2_new = got_three[:, :, :feature_dim].reshape(group_size, feature_dim)]
    reshape x3 -> x0, local copies, waits for them, and re-layouts: 3.94 us -> none  [the longest x2 3.85 us: pack_rows(): flat_body = body.astype(jnp.bfloat16).reshape(groups, per * width)]
  transfers between devices with their start and end apart: 4 -> 4, of which waited for: 4 -> 4; matrix products, arithmetic and copies ran while one was open for 0% -> 1% of each run, Pallas kernels for 0% -> 0%
where the time goes in v2:
time: 307 us; the launch traced here: 306 us
  waiting for transfers between devices  177 us (58%)
  blocking collectives  74.8 us (24%)
  starting transfers between devices  20.8 us (7%)
  other arithmetic  12.8 us (4%)
  matrix products  11.9 us (4%)
  local copies, waits for them, and re-layouts  8.03 us (3%)
    all_to_all x1, waiting for transfers between devices, local(): lax.all_to_all(block_rows, 'wide', split_axis=0, concat_axis=0, tiled=True)  94.7 us
    all_to_all x1, blocking collectives, local(): lax.all_to_all(sent_three, 'wide', split_axis=0, concat_axis=0, tiled=True)  37.4 us
    all_to_all x1, waiting for transfers between devices, local(): lax.all_to_all(sent_one, 'narrow', split_axis=0, concat_axis=0, tiled=True)  29 us
    all_to_all x1, waiting for transfers between devices, local(): lax.all_to_all(sent_two, 'wide', split_axis=0, concat_axis=0, tiled=True)  27.5 us
    all_to_all x1, waiting for transfers between devices, local(): lax.all_to_all(sent_sub, 'narrow', split_axis=0, concat_axis=0, tiled=True)  26 us
    all_to_all x1, blocking collectives, local(): lax.all_to_all(sent_ids, 'wide', split_axis=0, concat_axis=0, tiled=True)  20.3 us
    psum x1, blocking collectives, local(): inertia_sum = lax.psum(jnp.sum(inertia_all), 'narrow')  17 us
    dot_general x1, matrix products, local(): jnp.dot(owner_table.astype(jnp.bfloat16), got_rows.reshape(-1, feature_di...  7.07 us
  transfers between devices with their start and end apart: 4, of which 4 were waited for; matrix products, arithmetic and copies ran while one was open for 1% of the time, Pallas kernels for 0%

profile of v2, /device:TPU:1, one launch (start us, length us, event | category | flops | bytes accessed | tf_op | source)
XLA Modules:
  0.0 306.4 jit_solution(2913720922803310605)
XLA Ops:
  0.6 0.0 copy-start
  0.6 0.9 reshape.112
  1.6 0.8 compare_select_fusion
  2.3 20.3 %all_to_all.31 = s32[32,1,64]{2,1,0:T(1,128)S(1)} all-to-all(s32[32,1,64]{2,1,0:T(1,128)S(1)} %compare_select_fusion), channel_id=1, replica_groups=mesh['wide'=32,'narrow'=8] {'wide'}, dimensions={0} | all-to-all | bytes 16384 | tf_op jit(solution)/shard_map/all_to_all | solution.py:45
  22.6 4.9 %all-to-all-start.1 = ((bf16[32,64,1024]{2,1,0:T(8,128)(2,1)}), bf16[32,64,1024]{2,1,0:T(8,128)(2,1)}, u32[]{:S(2)}, u32[]{:S(2)}) async-start(bf16[32,64,1024]{2,1,0:T(8,128)(2,1)} %bitcast.23), calls=%async_computation.1 | async-start | bytes 8388608 | tf_op jit(solution)/shard_map/all_to_all | solution.py:44
  27.5 0.1 subtract_reduce_fusion
  27.6 0.1 sub.51
  27.6 1.5 multiply_subtract_fusion
  29.2 0.1 select_convert_fusion
  29.3 94.7 %all-to-all-done.1 = bf16[32,64,1024]{2,1,0:T(8,128)(2,1)} async-done(((bf16[32,64,1024]{2,1,0:T(8,128)(2,1)}), bf16[32,64,1024]{2,1,0:T(8,128)(2,1)}, u32[]{:S(2)}, u32[]{:S(2)}) %all-to-all-start.1) | async-done | bytes 4194336 | tf_op jit(solution)/shard_map/all_to_all | solution.py:44
  124.0 7.1 %fusion.6 = bf16[1024,1024]{0,1:T(8,128)(2,1)S(1)} fusion(bf16[2048,1024]{1,0:T(8,128)(2,1)} %bitcast.1, s32[2048]{0:T(1024)S(1)} %sub.51), kind=kOutput, calls=%fused_computation.14 | convolution fusion | flops 4298113024 | bytes 6299648 | tf_op jit(solution)/shard_map/dot_general | solution.py:49
  131.1 1.8 copy_bitcast_fusion
  132.9 6.0 %all-to-all-start.2 = ((bf16[8,128,1152]{1,2,0:T(8,128)(2,1)}), bf16[8,128,1152]{1,2,0:T(8,128)(2,1)}, u32[]{:S(2)}, u32[]{:S(2)}) async-start(bf16[8,128,1152]{1,2,0:T(8,128)(2,1)} %copy_bitcast_fusion), calls=%async_computation.2 | async-start | bytes 4718592 | tf_op jit(solution)/shard_map/all_to_all | solution.py:63
  139.0 0.0 copy-done
  139.0 0.2 copy.30
  139.2 29.0 %all-to-all-done.2 = bf16[8,128,1152]{1,2,0:T(8,128)(2,1)} async-done(((bf16[8,128,1152]{1,2,0:T(8,128)(2,1)}), bf16[8,128,1152]{1,2,0:T(8,128)(2,1)}, u32[]{:S(2)}, u32[]{:S(2)}) %all-to-all-start.2) | async-done | bytes 2359328 | tf_op jit(solution)/shard_map/all_to_all | solution.py:63
  168.2 0.7 convert_reduce_fusion.6
  169.0 1.9 convert_reduce_fusion
  170.9 0.1 divide_convert_fusion
  171.0 0.1 copy.26
  171.1 1.6 broadcast_in_dim.138
  172.7 0.0 copy-start.1
  172.7 5.2 %all-to-all-start.3 = ((bf16[8,128,1024]{2,1,0:T(8,128)(2,1)}), bf16[8,128,1024]{2,1,0:T(8,128)(2,1)}, u32[]{:S(2)}, u32[]{:S(2)}) async-start(bf16[8,128,1024]{2,1,0:T(8,128)(2,1)} %broadcast_in_dim.138), calls=%async_computation.3 | async-start | bytes 4194304 | tf_op jit(solution)/shard_map/all_to_all | solution.py:70
  177.9 0.0 copy-done.1
  178.0 0.5 multiply_subtract_fusion.1
  178.4 26.0 %all-to-all-done.3 = bf16[8,128,1024]{2,1,0:T(8,128)(2,1)} async-done(((bf16[8,128,1024]{2,1,0:T(8,128)(2,1)}), bf16[8,128,1024]{2,1,0:T(8,128)(2,1)}, u32[]{:S(2)}, u32[]{:S(2)}) %all-to-all-start.3) | async-done | bytes 2097184 | tf_op jit(solution)/shard_map/all_to_all | solution.py:70
  204.4 2.1 multiply_reduce_fusion
  206.5 0.3 select_reduce_fusion
  206.8 2.8 fusion.7
  209.6 0.3 select_convert_fusion.1
  210.0 1.1 pad_maximum_fusion
  211.1 4.7 %all-to-all-start.4 = ((bf16[32,16,1152]{2,1,0:T(8,128)(2,1)}), bf16[32,16,1152]{2,1,0:T(8,128)(2,1)S(1)}, u32[]{:S(2)}, u32[]{:S(2)}) async-start(bf16[32,16,1152]{2,1,0:T(8,128)(2,1)} %bitcast.22), calls=%async_computation.4 | async-start | bytes 2359296 | tf_op jit(solution)/shard_map/all_to_all | solution.py:90
  215.8 27.5 %all-to-all-done.4 = bf16[32,16,1152]{2,1,0:T(8,128)(2,1)S(1)} async-done(((bf16[32,16,1152]{2,1,0:T(8,128)(2,1)}), bf16[32,16,1152]{2,1,0:T(8,128)(2,1)S(1)}, u32[]{:S(2)}, u32[]{:S(2)}) %all-to-all-start.4) | async-done | bytes 1179680 | tf_op jit(solution)/shard_map/all_to_all | solution.py:90
  243.4 0.2 add_reduce_fusion
  243.6 0.2 convert_reduce_fusion.1
  243.7 1.0 multiply_reduce_fusion.1
  244.7 0.1 copy.27
  244.8 0.1 copy.28
  244.9 0.2 convert_reduce_fusion.5
  245.1 0.1 select_convert_fusion.2
  245.2 0.1 broadcast_in_dim.158
  245.3 37.4 %all_to_all.32 = bf16[32,16,1152]{2,1,0:T(8,128)(2,1)S(1)} all-to-all(bf16[32,16,1152]{2,1,0:T(8,128)(2,1)S(1)} %broadcast_in_dim.158), channel_id=1, replica_groups=mesh['wide'=32,'narrow'=8] {'wide'}, dimensions={0} | all-to-all | bytes 2359296 | tf_op jit(solution)/shard_map/all_to_all | solution.py:106
  282.7 0.8 fusion.20
  283.5 17.0 %psum.7 = f32[]{:T(128)} all-reduce(f32[]{:T(128)} %fusion.20), channel_id=1, replica_groups=mesh['wide'=32,'narrow'=8] {'narrow'}, use_global_device_ids=true, to_apply=%region_9.10 | all-reduce | flops 1 | bytes 8 | tf_op jit(solution)/shard_map/psum | solution.py:110
  300.6 0.9 fusion.10
  301.5 0.7 div.45
  302.2 1.1 slice.80
  303.3 3.1 %copy.34 = bf16[1024,1024]{1,0:T(8,128)(2,1)} copy(bf16[1024,1024]{1,0:T(8,128)(2,1)} %bitcast.5) | data formatting | bytes 4194304
  (10 shorter events, 0.1 us)
Async XLA Ops:
  0.6 138.3 %copy-start = (bf16[1024,1024]{1,0:T(8,128)(2,1)S(1)}, bf16[1024,1024]{1,0:T(8,128)(2,1)}, u32[]{:S(2)}) copy-start(bf16[1024,1024]{1,0:T(8,128)(2,1)} %param.9) | copy-start | bytes 6291460
  22.6 101.4 %all-to-all-start.1 = ((bf16[32,64,1024]{2,1,0:T(8,128)(2,1)}), bf16[32,64,1024]{2,1,0:T(8,128)(2,1)}, u32[]{:S(2)}, u32[]{:S(2)}) async-start(bf16[32,64,1024]{2,1,0:T(8,128)(2,1)} %bitcast.23), calls=%async_computation.1 | async-start | bytes 8388608 | tf_op jit(solution)/shard_map/all_to_all | solution.py:44
  132.9 35.3 %all-to-all-start.2 = ((bf16[8,128,1152]{1,2,0:T(8,128)(2,1)}), bf16[8,128,1152]{1,2,0:T(8,128)(2,1)}, u32[]{:S(2)}, u32[]{:S(2)}) async-start(bf16[8,128,1152]{1,2,0:T(8,128)(2,1)} %copy_bitcast_fusion), calls=%async_computation.2 | async-start | bytes 4718592 | tf_op jit(solution)/shard_map/all_to_all | solution.py:63
  172.7 5.2 %copy-start.1 = (s32[1024]{0:T(1024)S(1)}, s32[1024]{0:T(1024)}, u32[]{:S(2)}) copy-start(s32[1024]{0:T(1024)} %param.11) | copy-start | bytes 12292
  172.7 31.7 %all-to-all-start.3 = ((bf16[8,128,1024]{2,1,0:T(8,128)(2,1)}), bf16[8,128,1024]{2,1,0:T(8,128)(2,1)}, u32[]{:S(2)}, u32[]{:S(2)}) async-start(bf16[8,128,1024]{2,1,0:T(8,128)(2,1)} %broadcast_in_dim.138), calls=%async_computation.3 | async-start | bytes 4194304 | tf_op jit(solution)/shard_map/all_to_all | solution.py:70
  211.1 32.3 %all-to-all-start.4 = ((bf16[32,16,1152]{2,1,0:T(8,128)(2,1)}), bf16[32,16,1152]{2,1,0:T(8,128)(2,1)S(1)}, u32[]{:S(2)}, u32[]{:S(2)}) async-start(bf16[32,16,1152]{2,1,0:T(8,128)(2,1)} %bitcast.22), calls=%async_computation.4 | async-start | bytes 2359296 | tf_op jit(solution)/shard_map/all_to_all | solution.py:90

commit v3 on v2

--- a/solution.py
+++ b/solution.py
@@ -40,15 +40,29 @@
     block_rows = embeddings.reshape(wide_count, slot_count, feature_dim)
     position = lax.broadcasted_iota(jnp.int32, (wide_count, slot_count), 1)
     live_slots = position < block_counts[:, None]
-    sent_ids = jnp.where(live_slots, level1_ids.reshape(wide_count, slot_count), -1)
-    got_rows = lax.all_to_all(block_rows, "wide", split_axis=0, concat_axis=0, tiled=True)
-    got_ids = lax.all_to_all(sent_ids, "wide", split_axis=0, concat_axis=0, tiled=True)
+    lanes = 128
+    pieces = feature_dim // lanes
+    block_base = lax.broadcasted_iota(jnp.int32, (wide_count, 1), 0) * owner_size
+    local_ids = jnp.where(live_slots, level1_ids.reshape(wide_count, slot_count) - block_base, -32)
+    id_high = jnp.floor_divide(local_ids, 32)
+    id_low = local_ids - 32 * id_high
+    id_flat = jnp.concatenate([id_high, id_low], axis=1).astype(jnp.float32).astype(jnp.bfloat16)
+    tile_rows = -(-id_flat.shape[1] // lanes)
+    tile_pad = -(-tile_rows // 16) * 16
+    id_flat = jnp.pad(id_flat, ((0, 0), (0, tile_pad * lanes - id_flat.shape[1])))
+    id_tile = id_flat.reshape(wide_count, tile_pad, lanes)
+    body_rows = block_rows.reshape(wide_count, slot_count * pieces, lanes)
+    sent_rows = jnp.concatenate([body_rows, id_tile], axis=1)
+    got_all = lax.all_to_all(sent_rows, "wide", split_axis=0, concat_axis=0, tiled=True)
+    got_rows = got_all[:, : slot_count * pieces, :].reshape(wide_count * slot_count, feature_dim)
+    got_tile = got_all[:, slot_count * pieces :, :].reshape(wide_count, -1)[:, : 2 * slot_count].astype(jnp.float32)
+    got_local = (32.0 * got_tile[:, :slot_count] + got_tile[:, slot_count:]).astype(jnp.int32)
 
-    owner_index = got_ids.reshape(-1) - owner_base
+    owner_index = got_local.reshape(-1)
     owner_table = lax.broadcasted_iota(jnp.int32, (owner_size, 1), 0) == owner_index[None, :]
     row_sums = jnp.dot(
         owner_table.astype(jnp.bfloat16),
-        got_rows.reshape(-1, feature_dim),
+        got_rows,
         preferred_element_type=jnp.float32,
     )
     row_counts = jnp.dot(

time: 307 us -> 324 us (1.055)
  blocking collectives: 74.8 us -> 54.5 us
  local copies, waits for them, and re-layouts: 8.03 us -> 28.3 us
  starting transfers between devices: 20.8 us -> 32 us
  other arithmetic: 12.8 us -> 17.4 us
    all_to_all x1 -> x0, blocking collectives: 20.3 us -> none  [local(): lax.all_to_all(sent_ids, 'wide', split_axis=0, concat_axis=0, tiled=True)]
    another operation x0 -> x1, local copies, waits for them, and re-layouts: none -> 7.32 us  [local(): body_rows = block_rows.reshape(wide_count, slot_count * pieces, lanes)]
    reshape x1 -> x2, local copies, waits for them, and re-layouts: 0.93 us -> 8.23 us  [the longest x1 7.31 us: local(): got_all[:, :slot_count * pieces, :]]
    all_to_all x1, starting transfers between devices: 4.85 us -> 12 us  [local(): lax.all_to_all(sent_rows, 'wide', split_axis=0, concat_axis=0, tiled=True)]
    slice x0 -> x2, local copies, waits for them, and re-layouts: none -> 5.55 us  [the longest x1 4.63 us: local(): got_all[:, :slot_count * pieces, :]]
    concatenate x0 -> x1, other arithmetic: none -> 4.52 us  [local(): sent_rows = jnp.concatenate([body_rows, id_tile], axis=1)]
    all_to_all x1, starting transfers between devices: 6.02 us -> 9.88 us  [local(): lax.all_to_all(sent_one, 'narrow', split_axis=0, concat_axis=0, tiled=True)]
  transfers between devices with their start and end apart: 4 -> 4, of which waited for: 4 -> 4; matrix products, arithmetic and copies ran while one was open for 1% -> 0% of each run, Pallas kernels for 0% -> 0%
where the time goes in v3:
time: 324 us; the launch traced here: 323 us
  waiting for transfers between devices  178 us (55%)
  blocking collectives  54.5 us (17%)
  starting transfers between devices  32 us (10%)
  local copies, waits for them, and re-layouts  28.3 us (9%)
  other arithmetic  17.4 us (5%)
  matrix products  11.9 us (4%)
    all_to_all x1, waiting for transfers between devices, local(): lax.all_to_all(sent_rows, 'wide', split_axis=0, concat_axis=0, tiled=True)  95.5 us
    all_to_all x1, blocking collectives, local(): lax.all_to_all(sent_three, 'wide', split_axis=0, concat_axis=0, tiled=True)  37.4 us
    all_to_all x1, waiting for transfers between devices, local(): lax.all_to_all(sent_one, 'narrow', split_axis=0, concat_axis=0, tiled=True)  29 us
    all_to_all x1, waiting for transfers between devices, local(): lax.all_to_all(sent_two, 'wide', split_axis=0, concat_axis=0, tiled=True)  27.5 us
    all_to_all x1, waiting for transfers between devices, local(): lax.all_to_all(sent_sub, 'narrow', split_axis=0, concat_axis=0, tiled=True)  26 us
    psum x1, blocking collectives, local(): inertia_sum = lax.psum(jnp.sum(inertia_all), 'narrow')  17 us
    all_to_all x1, starting transfers between devices, local(): lax.all_to_all(sent_rows, 'wide', split_axis=0, concat_axis=0, tiled=True)  12 us
    all_to_all x1, starting transfers between devices, local(): lax.all_to_all(sent_one, 'narrow', split_axis=0, concat_axis=0, tiled=True)  9.88 us
  transfers between devices with their start and end apart: 4, of which 4 were waited for; matrix products, arithmetic and copies ran while one was open for 0% of the time, Pallas kernels for 0%

profile of v3, /device:TPU:1, one launch (start us, length us, event | category | flops | bytes accessed | tf_op | source)
XLA Modules:
  0.0 323.0 jit_solution(659665587077996165)
XLA Ops:
  0.6 0.0 copy-start
  0.7 0.9 reshape.76
  1.6 0.7 add_select_fusion
  2.3 0.1 fusion.15
  2.4 7.3 %reshape_reshape.3 = bf16[32,512,128]{2,1,0:T(8,128)(2,1)} reshape(bf16[2048,1024]{1,0:T(8,128)(2,1)} %param.6) | data formatting | bytes 8388608 | tf_op jit(solution)/shard_map/reshape;reshape | solution.py:54
  9.8 4.5 %pad_maximum_fusion = bf16[32,528,128]{2,1,0:T(8,128)(2,1)} fusion(bf16[32,16,128]{2,1,0:T(8,128)(2,1)S(1)} %bitcast.29, bf16[32,512,128]{2,1,0:T(8,128)(2,1)} %reshape_reshape.3), kind=kLoop, calls=%fused_computation.3 | loop fusion | flops 8650752 | bytes 8650752 | tf_op jit(solution)/shard_map/concatenate | solution.py:55
  14.3 12.0 %all-to-all-start = ((bf16[32,528,128]{2,1,0:T(8,128)(2,1)}), bf16[32,528,128]{2,1,0:T(8,128)(2,1)}, u32[]{:S(2)}, u32[]{:S(2)}) async-start(bf16[32,528,128]{2,1,0:T(8,128)(2,1)} %pad_maximum_fusion), calls=%async_computation | async-start | bytes 8650752 | tf_op jit(solution)/shard_map/all_to_all | solution.py:56
  26.3 95.5 %all-to-all-done = bf16[32,528,128]{2,1,0:T(8,128)(2,1)} async-done(((bf16[32,528,128]{2,1,0:T(8,128)(2,1)}), bf16[32,528,128]{2,1,0:T(8,128)(2,1)}, u32[]{:S(2)}, u32[]{:S(2)}) %all-to-all-start) | async-done | bytes 4325408 | tf_op jit(solution)/shard_map/all_to_all | solution.py:56
  121.8 0.9 slice.92
  122.8 0.1 fusion.14
  122.9 0.1 eq.82
  123.0 1.5 multiply_subtract_fusion.1
  124.5 4.6 %slice.96 = bf16[32,512,128]{2,1,0:T(8,128)(2,1)} slice(bf16[32,528,128]{2,1,0:T(8,128)(2,1)} %all-to-all-done), slice={[0:32], [0:512], [0:128]} | slice | bytes 8388608 | tf_op jit(solution)/shard_map/slice | solution.py:57
  129.1 7.3 %reshape.79 = bf16[2048,1024]{1,0:T(8,128)(2,1)} reshape(bf16[32,512,128]{2,1,0:T(8,128)(2,1)} %slice.96) | data formatting | bytes 8388608 | tf_op jit(solution)/shard_map/reshape | solution.py:57
  136.4 7.1 %fusion.6 = bf16[1024,1024]{0,1:T(8,128)(2,1)S(1)} fusion(bf16[2048,1024]{1,0:T(8,128)(2,1)} %reshape.79, s32[2048]{0:T(1024)S(1)} %eq.82), kind=kOutput, calls=%fused_computation.15 | convolution fusion | flops 4298113024 | bytes 6299648 | tf_op jit(solution)/shard_map/dot_general | solution.py:63
  143.5 0.1 select_convert_fusion
  143.6 1.8 copy_bitcast_fusion
  145.4 9.9 %all-to-all-start.1 = ((bf16[8,128,1152]{1,2,0:T(8,128)(2,1)}), bf16[8,128,1152]{1,2,0:T(8,128)(2,1)}, u32[]{:S(2)}, u32[]{:S(2)}) async-start(bf16[8,128,1152]{1,2,0:T(8,128)(2,1)} %copy_bitcast_fusion), calls=%async_computation.1 | async-start | bytes 4718592 | tf_op jit(solution)/shard_map/all_to_all | solution.py:77
  155.3 0.0 copy-done
  155.3 0.2 copy.30
  155.5 29.0 %all-to-all-done.1 = bf16[8,128,1152]{1,2,0:T(8,128)(2,1)} async-done(((bf16[8,128,1152]{1,2,0:T(8,128)(2,1)}), bf16[8,128,1152]{1,2,0:T(8,128)(2,1)}, u32[]{:S(2)}, u32[]{:S(2)}) %all-to-all-start.1) | async-done | bytes 2359328 | tf_op jit(solution)/shard_map/all_to_all | solution.py:77
  184.6 0.7 convert_reduce_fusion.6
  185.3 1.9 convert_reduce_fusion
  187.2 0.1 divide_convert_fusion
  187.3 0.1 copy.26
  187.5 1.6 broadcast_in_dim.137
  189.1 0.0 copy-start.1
  189.1 5.2 %all-to-all-start.2 = ((bf16[8,128,1024]{2,1,0:T(8,128)(2,1)}), bf16[8,128,1024]{2,1,0:T(8,128)(2,1)}, u32[]{:S(2)}, u32[]{:S(2)}) async-start(bf16[8,128,1024]{2,1,0:T(8,128)(2,1)} %broadcast_in_dim.137), calls=%async_computation.2 | async-start | bytes 4194304 | tf_op jit(solution)/shard_map/all_to_all | solution.py:84
  194.3 0.0 copy-done.1
  194.3 0.5 multiply_subtract_fusion.2
  194.8 26.0 %all-to-all-done.2 = bf16[8,128,1024]{2,1,0:T(8,128)(2,1)} async-done(((bf16[8,128,1024]{2,1,0:T(8,128)(2,1)}), bf16[8,128,1024]{2,1,0:T(8,128)(2,1)}, u32[]{:S(2)}, u32[]{:S(2)}) %all-to-all-start.2) | async-done | bytes 2097184 | tf_op jit(solution)/shard_map/all_to_all | solution.py:84
  220.8 2.1 multiply_reduce_fusion
  222.8 0.3 select_reduce_fusion
  223.1 2.8 fusion.7
  226.0 0.3 select_convert_fusion.1
  226.3 1.1 pad_maximum_fusion.1
  227.4 5.0 %all-to-all-start.3 = ((bf16[32,16,1152]{2,1,0:T(8,128)(2,1)}), bf16[32,16,1152]{2,1,0:T(8,128)(2,1)S(1)}, u32[]{:S(2)}, u32[]{:S(2)}) async-start(bf16[32,16,1152]{2,1,0:T(8,128)(2,1)} %bitcast.27), calls=%async_computation.3 | async-start | bytes 2359296 | tf_op jit(solution)/shard_map/all_to_all | solution.py:104
  232.4 27.5 %all-to-all-done.3 = bf16[32,16,1152]{2,1,0:T(8,128)(2,1)S(1)} async-done(((bf16[32,16,1152]{2,1,0:T(8,128)(2,1)}), bf16[32,16,1152]{2,1,0:T(8,128)(2,1)S(1)}, u32[]{:S(2)}, u32[]{:S(2)}) %all-to-all-start.3) | async-done | bytes 1179680 | tf_op jit(solution)/shard_map/all_to_all | solution.py:104
  260.0 0.2 add_reduce_fusion
  260.2 0.2 convert_reduce_fusion.1
  260.3 1.0 multiply_reduce_fusion.1
  261.3 0.1 copy.27
  261.4 0.1 copy.28
  261.5 0.2 convert_reduce_fusion.5
  261.7 0.1 select_convert_fusion.2
  261.8 0.1 broadcast_in_dim.157
  261.9 37.4 %all_to_all.25 = bf16[32,16,1152]{2,1,0:T(8,128)(2,1)S(1)} all-to-all(bf16[32,16,1152]{2,1,0:T(8,128)(2,1)S(1)} %broadcast_in_dim.157), channel_id=1, replica_groups=mesh['wide'=32,'narrow'=8] {'wide'}, dimensions={0} | all-to-all | bytes 2359296 | tf_op jit(solution)/shard_map/all_to_all | solution.py:120
  299.4 0.8 fusion.24
  300.2 17.0 %psum.7 = f32[]{:T(128)} all-reduce(f32[]{:T(128)} %fusion.24), channel_id=1, replica_groups=mesh['wide'=32,'narrow'=8] {'narrow'}, use_global_device_ids=true, to_apply=%region_9.10 | all-reduce | flops 1 | bytes 8 | tf_op jit(solution)/shard_map/psum | solution.py:124
  317.2 0.9 fusion.10
  318.1 0.7 div.61
  318.8 1.1 slice.105
  319.9 3.1 copy.38
  (15 shorter events, 0.2 us)
Async XLA Ops:
  0.6 154.7 %copy-start = (bf16[1024,1024]{1,0:T(8,128)(2,1)S(1)}, bf16[1024,1024]{1,0:T(8,128)(2,1)}, u32[]{:S(2)}) copy-start(bf16[1024,1024]{1,0:T(8,128)(2,1)} %param.9) | copy-start | bytes 6291460
  14.3 107.5 %all-to-all-start = ((bf16[32,528,128]{2,1,0:T(8,128)(2,1)}), bf16[32,528,128]{2,1,0:T(8,128)(2,1)}, u32[]{:S(2)}, u32[]{:S(2)}) async-start(bf16[32,528,128]{2,1,0:T(8,128)(2,1)} %pad_maximum_fusion), calls=%async_computation | async-start | bytes 8650752 | tf_op jit(solution)/shard_map/all_to_all | solution.py:56
  145.4 39.1 %all-to-all-start.1 = ((bf16[8,128,1152]{1,2,0:T(8,128)(2,1)}), bf16[8,128,1152]{1,2,0:T(8,128)(2,1)}, u32[]{:S(2)}, u32[]{:S(2)}) async-start(bf16[8,128,1152]{1,2,0:T(8,128)(2,1)} %copy_bitcast_fusion), calls=%async_computation.1 | async-start | bytes 4718592 | tf_op jit(solution)/shard_map/all_to_all | solution.py:77
  189.1 5.2 %copy-start.1 = (s32[1024]{0:T(1024)S(1)}, s32[1024]{0:T(1024)}, u32[]{:S(2)}) copy-start(s32[1024]{0:T(1024)} %param.11) | copy-start | bytes 12292
  189.1 31.7 %all-to-all-start.2 = ((bf16[8,128,1024]{2,1,0:T(8,128)(2,1)}), bf16[8,128,1024]{2,1,0:T(8,128)(2,1)}, u32[]{:S(2)}, u32[]{:S(2)}) async-start(bf16[8,128,1024]{2,1,0:T(8,128)(2,1)} %broadcast_in_dim.137), calls=%async_computation.2 | async-start | bytes 4194304 | tf_op jit(solution)/shard_map/all_to_all | solution.py:84
  227.4 32.5 %all-to-all-start.3 = ((bf16[32,16,1152]{2,1,0:T(8,128)(2,1)}), bf16[32,16,1152]{2,1,0:T(8,128)(2,1)S(1)}, u32[]{:S(2)}, u32[]{:S(2)}) async-start(bf16[32,16,1152]{2,1,0:T(8,128)(2,1)} %bitcast.27), calls=%async_computation.3 | async-start | bytes 2359296 | tf_op jit(solution)/shard_map/all_to_all | solution.py:104

commit v4 on v2

--- a/solution.py
+++ b/solution.py
@@ -57,17 +57,35 @@
         preferred_element_type=jnp.float32,
     )[:, 0]
 
-    sub_size = owner_size // narrow_count
+    core_count = 2
+    chip_count = narrow_count // core_count
+    core = narrow_index % core_count
+    chip = narrow_index // core_count
+    half_size = owner_size // core_count
+    sub_size = half_size // chip_count
     count_high, count_low = split_whole(row_counts, 16.0)
-    sent_one = pack_columns(row_sums, [count_high, count_low]).reshape(narrow_count, sub_size, -1)
-    got_one = lax.all_to_all(sent_one, "narrow", split_axis=0, concat_axis=0, tiled=True)
+    packed = pack_columns(row_sums, [count_high, count_low]).reshape(core_count, half_size, -1)
+    kept = jnp.where(core == 0, packed[0], packed[1])
+    given = jnp.where(core == 0, packed[1], packed[0])
+    partner = [(i, i ^ 1) for i in range(narrow_count)]
+    chip_part = kept.astype(jnp.float32) + lax.ppermute(given, "narrow", partner).astype(jnp.float32)
+    rings = [[c + core_count * y for y in range(chip_count)] for c in range(core_count)]
+    sent_one = chip_part.astype(jnp.bfloat16).reshape(chip_count, sub_size, -1)
+    got_one = lax.all_to_all(sent_one, "narrow", 0, 0, axis_index_groups=rings, tiled=True)
     sub_sums = jnp.sum(got_one[:, :, :feature_dim].astype(jnp.float32), axis=0)
     tail_sum = jnp.sum(got_one[:, :, feature_dim : feature_dim + 2].astype(jnp.float32), axis=0)
     sub_counts = 16.0 * tail_sum[:, 0] + tail_sum[:, 1]
-    sub_old = lax.dynamic_slice_in_dim(level1_old, narrow_index * sub_size, sub_size, axis=0)
+    sub_start = core * half_size + chip * sub_size
+    sub_old = lax.dynamic_slice_in_dim(level1_old, sub_start, sub_size, axis=0)
     sub_new = ((4.0 * sub_old.astype(jnp.float32) + sub_sums) / (4.0 + sub_counts)[:, None]).astype(jnp.bfloat16)
-    sent_sub = jnp.broadcast_to(sub_new[None], (narrow_count,) + sub_new.shape)
-    level1_new = lax.all_to_all(sent_sub, "narrow", split_axis=0, concat_axis=0, tiled=True).reshape(owner_size, feature_dim)
+    sent_sub = jnp.broadcast_to(sub_new[None], (chip_count,) + sub_new.shape)
+    half_new = lax.all_to_all(sent_sub, "narrow", 0, 0, axis_index_groups=rings, tiled=True).reshape(half_size, feature_dim)
+    other_half = lax.ppermute(half_new, "narrow", partner)
+    level1_new = jnp.where(
+        core == 0,
+        jnp.concatenate([half_new, other_half], axis=0),
+        jnp.concatenate([other_half, half_new], axis=0),
+    )
 
     group_size = level2_old.shape[0]
     group_index = level2_ids - narrow_index * group_size

time: 307 us -> 278 us (0.906)
  waiting for transfers between devices: 177 us -> 142 us
  blocking collectives: 74.8 us -> 90.9 us
  local copies, waits for them, and re-layouts: 8.03 us -> 4.17 us
    all_to_all x2 -> x1, waiting for transfers between devices: 55 us -> 15.1 us  [local(): lax.all_to_all(sent_one, 'narrow', 0, 0, axis_index_groups=rings, tiled=T...]
    all_to_all x0 -> x1, blocking collectives: none -> 15.9 us  [local(): lax.all_to_all(sent_sub, 'narrow', 0, 0, axis_index_groups=rings, tiled=T...]
    all_to_all x2 -> x1, starting transfers between devices: 11.2 us -> 4.19 us  [local(): lax.all_to_all(sent_one, 'narrow', 0, 0, axis_index_groups=rings, tiled=T...]
    ppermute x0 -> x2, waiting for transfers between devices: none -> 4.42 us  [the longest x1 2.47 us: local(): lax.ppermute(given, 'narrow', partner).astype(jnp.float32)]
    ppermute x0 -> x2, starting transfers between devices: none -> 4.21 us  [the longest x1 2.56 us: local(): other_half = lax.ppermute(half_new, 'narrow', partner)]
  transfers between devices with their start and end apart: 4 -> 5, of which waited for: 4 -> 5; matrix products, arithmetic and copies ran while one was open for 1% -> 1% of each run, Pallas kernels for 0% -> 0%
where the time goes in v4:
time: 278 us; the launch traced here: 277 us
  waiting for transfers between devices  142 us (51%)
  blocking collectives  90.9 us (33%)
  starting transfers between devices  18 us (6%)
  other arithmetic  11.3 us (4%)
  matrix products  10.3 us (4%)
  local copies, waits for them, and re-layouts  4.17 us (2%)
    all_to_all x1, waiting for transfers between devices, local(): lax.all_to_all(block_rows, 'wide', split_axis=0, concat_axis=0, tiled=True)  94.7 us
    all_to_all x1, blocking collectives, local(): lax.all_to_all(sent_three, 'wide', split_axis=0, concat_axis=0, tiled=True)  37.7 us
    all_to_all x1, waiting for transfers between devices, local(): lax.all_to_all(sent_two, 'wide', split_axis=0, concat_axis=0, tiled=True)  27.3 us
    all_to_all x1, blocking collectives, local(): lax.all_to_all(sent_ids, 'wide', split_axis=0, concat_axis=0, tiled=True)  20.3 us
    psum x1, blocking collectives, local(): inertia_sum = lax.psum(jnp.sum(inertia_all), 'narrow')  17 us
    all_to_all x1, blocking collectives, local(): lax.all_to_all(sent_sub, 'narrow', 0, 0, axis_index_groups=rings, tiled=T...  15.9 us
    all_to_all x1, waiting for transfers between devices, local(): lax.all_to_all(sent_one, 'narrow', 0, 0, axis_index_groups=rings, tiled=T...  15.1 us
    dot_general x1, matrix products, local(): jnp.dot(owner_table.astype(jnp.bfloat16), got_rows.reshape(-1, feature_di...  7.06 us
  transfers between devices with their start and end apart: 5, of which 5 were waited for; matrix products, arithmetic and copies ran while one was open for 1% of the time, Pallas kernels for 0%

profile of v4, /device:TPU:1, one launch (start us, length us, event | category | flops | bytes accessed | tf_op | source)
XLA Modules:
  0.0 277.1 jit_solution(10248366838765174795)
XLA Ops:
  0.6 0.0 copy-start
  0.6 0.9 reshape.115
  1.6 0.8 compare_select_fusion
  2.3 20.3 %all_to_all.31 = s32[32,1,64]{2,1,0:T(1,128)S(1)} all-to-all(s32[32,1,64]{2,1,0:T(1,128)S(1)} %compare_select_fusion), channel_id=1, replica_groups=mesh['wide'=32,'narrow'=8] {'wide'}, dimensions={0} | all-to-all | bytes 16384 | tf_op jit(solution)/shard_map/all_to_all | solution.py:45
  22.6 4.9 %all-to-all-start.1 = ((bf16[32,64,1024]{2,1,0:T(8,128)(2,1)}), bf16[32,64,1024]{2,1,0:T(8,128)(2,1)}, u32[]{:S(2)}, u32[]{:S(2)}) async-start(bf16[32,64,1024]{2,1,0:T(8,128)(2,1)} %bitcast.24), calls=%async_computation.1 | async-start | bytes 8388608 | tf_op jit(solution)/shard_map/all_to_all | solution.py:44
  27.6 0.1 sub.56
  27.7 1.5 multiply_subtract_fusion
  29.2 0.1 select_convert_fusion
  29.3 94.7 %all-to-all-done.1 = bf16[32,64,1024]{2,1,0:T(8,128)(2,1)} async-done(((bf16[32,64,1024]{2,1,0:T(8,128)(2,1)}), bf16[32,64,1024]{2,1,0:T(8,128)(2,1)}, u32[]{:S(2)}, u32[]{:S(2)}) %all-to-all-start.1) | async-done | bytes 4194336 | tf_op jit(solution)/shard_map/all_to_all | solution.py:44
  124.0 7.1 %fusion.6 = bf16[1024,1024]{0,1:T(8,128)(2,1)S(1)} fusion(bf16[2048,1024]{1,0:T(8,128)(2,1)} %bitcast.1, s32[2048]{0:T(1024)S(1)} %sub.56), kind=kOutput, calls=%fused_computation.16 | convolution fusion | flops 4298113024 | bytes 6299648 | tf_op jit(solution)/shard_map/dot_general | solution.py:49
  131.1 0.4 broadcast_select_fusion
  131.5 1.6 collective-permute-start
  133.1 2.5 collective-permute-done
  135.6 1.5 copy_bitcast_fusion
  137.1 4.2 %all-to-all-start.2 = ((bf16[4,128,1152]{1,2,0:T(8,128)(2,1)}), bf16[4,128,1152]{1,2,0:T(8,128)(2,1)S(1)}, u32[]{:S(2)}, u32[]{:S(2)}) async-start(bf16[4,128,1152]{1,2,0:T(8,128)(2,1)} %copy_bitcast_fusion), calls=%async_computation.2 | async-start | bytes 2359296 | tf_op jit(solution)/shard_map/all_to_all | solution.py:74
  141.3 0.0 copy-done
  141.3 0.8 copy.30
  142.1 15.1 %all-to-all-done.2 = bf16[4,128,1152]{1,2,0:T(8,128)(2,1)S(1)} async-done(((bf16[4,128,1152]{1,2,0:T(8,128)(2,1)}), bf16[4,128,1152]{1,2,0:T(8,128)(2,1)S(1)}, u32[]{:S(2)}, u32[]{:S(2)}) %all-to-all-start.2) | async-done | bytes 1179680 | tf_op jit(solution)/shard_map/all_to_all | solution.py:74
  157.2 0.1 convert_reduce_fusion.1
  157.4 1.0 divide_convert_fusion
  158.4 0.0 copy-start.2
  158.4 0.1 copy.26
  158.6 0.1 broadcast_in_dim.136
  158.7 15.9 %all_to_all.32 = bf16[4,128,1024]{2,1,0:T(8,128)(2,1)S(1)} all-to-all(bf16[4,128,1024]{2,1,0:T(8,128)(2,1)S(1)} %broadcast_in_dim.136), channel_id=1, replica_groups={{0,2,4,6},{1,3,5,7},{8,10,12,14},{9,11,13,15},{16,18,20,22},{17,19,21,2..., dimensions={0} | all-to-all | bytes 2097152 | tf_op jit(solution)/shard_map/all_to_all | solution.py:82
  174.6 2.6 collective-permute-start.1
  177.2 0.0 copy-done.2
  177.2 0.5 multiply_subtract_fusion.1
  177.6 1.9 collective-permute-done.1
  179.6 2.2 multiply_reduce_fusion
  181.8 0.0 copy-start.1
  181.8 0.3 select_reduce_fusion
  182.1 1.3 fusion.7
  183.3 0.0 copy-done.1
  183.4 0.3 select_convert_fusion.1
  183.7 1.1 pad_maximum_fusion.1
  184.8 4.7 %all-to-all-start.4 = ((bf16[32,16,1152]{2,1,0:T(8,128)(2,1)}), bf16[32,16,1152]{2,1,0:T(8,128)(2,1)S(1)}, u32[]{:S(2)}, u32[]{:S(2)}) async-start(bf16[32,16,1152]{2,1,0:T(8,128)(2,1)} %bitcast.21), calls=%async_computation.4 | async-start | bytes 2359296 | tf_op jit(solution)/shard_map/all_to_all | solution.py:108
  189.5 27.3 %all-to-all-done.4 = bf16[32,16,1152]{2,1,0:T(8,128)(2,1)S(1)} async-done(((bf16[32,16,1152]{2,1,0:T(8,128)(2,1)}), bf16[32,16,1152]{2,1,0:T(8,128)(2,1)S(1)}, u32[]{:S(2)}, u32[]{:S(2)}) %all-to-all-start.4) | async-done | bytes 1179680 | tf_op jit(solution)/shard_map/all_to_all | solution.py:108
  216.9 0.2 add_reduce_fusion
  217.1 0.2 convert_reduce_fusion
  217.3 1.0 multiply_reduce_fusion.1
  218.2 0.1 copy.27
  218.3 0.1 copy.28
  218.4 0.2 convert_reduce_fusion.5
  218.6 0.1 select_convert_fusion.2
  218.7 0.1 broadcast_in_dim.155
  218.8 37.7 %all_to_all.33 = bf16[32,16,1152]{2,1,0:T(8,128)(2,1)S(1)} all-to-all(bf16[32,16,1152]{2,1,0:T(8,128)(2,1)S(1)} %broadcast_in_dim.155), channel_id=1, replica_groups=mesh['wide'=32,'narrow'=8] {'wide'}, dimensions={0} | all-to-all | bytes 2359296 | tf_op jit(solution)/shard_map/all_to_all | solution.py:124
  256.5 0.8 fusion.22
  257.3 17.0 %psum.7 = f32[]{:T(128)} all-reduce(f32[]{:T(128)} %fusion.22), channel_id=1, replica_groups=mesh['wide'=32,'narrow'=8] {'narrow'}, use_global_device_ids=true, to_apply=%region_9.10 | all-reduce | flops 1 | bytes 8 | tf_op jit(solution)/shard_map/psum | solution.py:128
  274.4 0.9 fusion.12
  275.3 0.7 div.56
  276.0 1.1 slice.94
  (12 shorter events, 0.2 us)
Async XLA Ops:
  0.6 140.6 %copy-start = (bf16[1024,1024]{1,0:T(8,128)(2,1)S(1)}, bf16[1024,1024]{1,0:T(8,128)(2,1)}, u32[]{:S(2)}) copy-start(bf16[1024,1024]{1,0:T(8,128)(2,1)} %param.9) | copy-start | bytes 6291460
  22.6 101.4 %all-to-all-start.1 = ((bf16[32,64,1024]{2,1,0:T(8,128)(2,1)}), bf16[32,64,1024]{2,1,0:T(8,128)(2,1)}, u32[]{:S(2)}, u32[]{:S(2)}) async-start(bf16[32,64,1024]{2,1,0:T(8,128)(2,1)} %bitcast.24), calls=%async_computation.1 | async-start | bytes 8388608 | tf_op jit(solution)/shard_map/all_to_all | solution.py:44
  131.5 4.1 %collective-permute-start = (bf16[512,1152]{0,1:T(8,128)(2,1)S(1)}, bf16[512,1152]{0,1:T(8,128)(2,1)S(1)}, u32[]{:S(2)}, u32[]{:S(2)}) collective-permute-start(bf16[512,1152]{0,1:T(8,128)(2,1)S(1)} %broadcast_select_fusion), channel_id=1, source_target_pairs={{0,1},{1,0},{2,3},{3,2},{4,5},{5,4},{6,7},{7,6},{8,9},{9,8},{10,11... | collective-permute-start | bytes 3538952 | tf_op jit(solution)/shard_map/ppermute | solution.py:71
  137.1 20.1 %all-to-all-start.2 = ((bf16[4,128,1152]{1,2,0:T(8,128)(2,1)}), bf16[4,128,1152]{1,2,0:T(8,128)(2,1)S(1)}, u32[]{:S(2)}, u32[]{:S(2)}) async-start(bf16[4,128,1152]{1,2,0:T(8,128)(2,1)} %copy_bitcast_fusion), calls=%async_computation.2 | async-start | bytes 2359296 | tf_op jit(solution)/shard_map/all_to_all | solution.py:74
  158.4 18.8 %copy-start.2 = (s32[1024]{0:T(1024)S(1)}, s32[1024]{0:T(1024)}, u32[]{:S(2)}) copy-start(s32[1024]{0:T(1024)} %param.11) | copy-start | bytes 12292
  174.6 5.0 %collective-permute-start.1 = (bf16[512,1024]{1,0:T(8,128)(2,1)S(1)}, bf16[512,1024]{1,0:T(8,128)(2,1)}, u32[]{:S(2)}, u32[]{:S(2)}) collective-permute-start(bf16[512,1024]{1,0:T(8,128)(2,1)S(1)} %bitcast.22), channel_id=1, source_target_pairs={{0,1},{1,0},{2,3},{3,2},{4,5},{5,4},{6,7},{7,6},{8,9},{9,8},{10,11... | collective-permute-start | bytes 3145736 | tf_op jit(solution)/shard_map/ppermute | solution.py:83
  181.8 1.6 copy-start.1
  184.8 32.1 %all-to-all-start.4 = ((bf16[32,16,1152]{2,1,0:T(8,128)(2,1)}), bf16[32,16,1152]{2,1,0:T(8,128)(2,1)S(1)}, u32[]{:S(2)}, u32[]{:S(2)}) async-start(bf16[32,16,1152]{2,1,0:T(8,128)(2,1)} %bitcast.21), calls=%async_computation.4 | async-start | bytes 2359296 | tf_op jit(solution)/shard_map/all_to_all | solution.py:108

commit v5 on v4

--- a/solution.py
+++ b/solution.py
@@ -101,11 +101,24 @@
     group_squares = jnp.sum(jnp.where(group_table, squares[None, :], 0.0), axis=1)
 
     part_size = group_size // wide_count
+    z_count = 8
+    x_count = wide_count // z_count
+    x_rings = [[z + z_count * x for x in range(x_count)] for z in range(z_count)]
+    z_rings = [[z + z_count * x for z in range(z_count)] for x in range(x_count)]
     squares_high, squares_low = split_float(group_squares, 2)
     counts_high, counts_low = split_whole(group_counts, 16.0)
     sent_two = pack_columns(group_sums, [squares_high, squares_low, counts_high, counts_low])
-    sent_two = sent_two.reshape(wide_count, part_size, -1)
-    got_two = lax.all_to_all(sent_two, "wide", split_axis=0, concat_axis=0, tiled=True)
+    sent_two = sent_two.reshape(x_count, z_count * part_size, -1)
+    got_x = lax.all_to_all(sent_two, "wide", 0, 0, axis_index_groups=x_rings, tiled=True)
+    x_sums = jnp.sum(got_x[:, :, :feature_dim].astype(jnp.float32), axis=0)
+    x_tail = jnp.sum(got_x[:, :, feature_dim : feature_dim + 4].astype(jnp.float32), axis=0)
+    x_squares = x_tail[:, 0] + x_tail[:, 1]
+    x_counts = 16.0 * x_tail[:, 2] + x_tail[:, 3]
+    squares_high, squares_low = split_float(x_squares, 2)
+    counts_high, counts_low = split_whole(x_counts, 16.0)
+    sent_z = pack_columns(x_sums, [squares_high, squares_low, counts_high, counts_low])
+    sent_z = sent_z.reshape(z_count, part_size, -1)
+    got_two = lax.all_to_all(sent_z, "wide", 0, 0, axis_index_groups=z_rings, tiled=True)
     sums_two = jnp.sum(got_two[:, :, :feature_dim].astype(jnp.float32), axis=0)
     tail_two = jnp.sum(got_two[:, :, feature_dim : feature_dim + 4].astype(jnp.float32), axis=0)
     squares_two = tail_two[:, 0] + tail_two[:, 1]
@@ -120,8 +133,11 @@
 
     inertia_pieces = split_float(inertia, 3)
     sent_three = pack_columns(means_two, inertia_pieces)
-    sent_three = jnp.broadcast_to(sent_three[None], (wide_count,) + sent_three.shape)
-    got_three = lax.all_to_all(sent_three, "wide", split_axis=0, concat_axis=0, tiled=True)
+    sent_three = jnp.broadcast_to(sent_three[None], (z_count,) + sent_three.shape)
+    got_z = lax.all_to_all(sent_three, "wide", 0, 0, axis_index_groups=z_rings, tiled=True)
+    sent_x = jnp.broadcast_to(got_z[None], (x_count,) + got_z.shape)
+    got_three = lax.all_to_all(sent_x, "wide", 0, 0, axis_index_groups=x_rings, tiled=True)
+    got_three = got_three.reshape(wide_count, part_size, -1)
     level2_new = got_three[:, :, :feature_dim].reshape(group_size, feature_dim)
     tail_three = got_three[:, :, feature_dim : feature_dim + 3].astype(jnp.float32)
     inertia_all = ((tail_three[:, :, 0] + tail_three[:, :, 1]) + tail_three[:, :, 2]).reshape(group_size)

time: 278 us -> 268 us (0.964)
  waiting for transfers between devices: 142 us -> 125 us
  blocking collectives: 90.9 us -> 99.6 us
    all_to_all x1, waiting for transfers between devices: 27.3 us -> 10.5 us  [local(): lax.all_to_all(sent_z, 'wide', 0, 0, axis_index_groups=z_rings, tiled=True)]
    all_to_all x1 -> x3, blocking collectives: 37.7 us -> 46.2 us  [the longest x1 18.7 us: local(): lax.all_to_all(sent_two, 'wide', 0, 0, axis_index_groups=x_rings, tiled=T...]
where the time goes in v5:
time: 268 us
  waiting for transfers between devices  125 us (47%)
  blocking collectives  99.6 us (37%)
  starting transfers between devices  16.7 us (6%)
  other arithmetic  10.6 us (4%)
  matrix products  10.3 us (4%)
  local copies, waits for them, and re-layouts  4.94 us (2%)
    all_to_all x1, waiting for transfers between devices, local(): lax.all_to_all(block_rows, 'wide', split_axis=0, concat_axis=0, tiled=True)  94.7 us
    all_to_all x1, blocking collectives, local(): lax.all_to_all(sent_ids, 'wide', split_axis=0, concat_axis=0, tiled=True)  20.3 us
    all_to_all x1, blocking collectives, local(): lax.all_to_all(sent_two, 'wide', 0, 0, axis_index_groups=x_rings, tiled=T...  18.7 us
    psum x1, blocking collectives, local(): inertia_sum = lax.psum(jnp.sum(inertia_all), 'narrow')  17.1 us
    all_to_all x1, blocking collectives, local(): lax.all_to_all(sent_sub, 'narrow', 0, 0, axis_index_groups=rings, tiled=T...  15.9 us
    all_to_all x1, blocking collectives, local(): lax.all_to_all(sent_x, 'wide', 0, 0, axis_index_groups=x_rings, tiled=True)  15.1 us
    all_to_all x1, waiting for transfers between devices, local(): lax.all_to_all(sent_one, 'narrow', 0, 0, axis_index_groups=rings, tiled=T...  15.1 us
    all_to_all x1, blocking collectives, local(): lax.all_to_all(sent_three, 'wide', 0, 0, axis_index_groups=z_rings, tiled...  12.4 us
  transfers between devices with their start and end apart: 5, of which 5 were waited for; matrix products, arithmetic and copies ran while one was open for 1% of the time, Pallas kernels for 0%

profile of v5, /device:TPU:1, one launch (start us, length us, event | category | flops | bytes accessed | tf_op | source)
XLA Modules:
  0.0 267.8 jit_solution(3138587664863887276)
XLA Ops:
  0.6 0.0 copy-start
  0.6 0.9 reshape.159
  1.6 0.8 compare_select_fusion
  2.3 20.3 %all_to_all.41 = s32[32,1,64]{2,1,0:T(1,128)S(1)} all-to-all(s32[32,1,64]{2,1,0:T(1,128)S(1)} %compare_select_fusion), channel_id=1, replica_groups=mesh['wide'=32,'narrow'=8] {'wide'}, dimensions={0} | all-to-all | bytes 16384 | tf_op jit(solution)/shard_map/all_to_all | solution.py:45
  22.6 4.9 %all-to-all-start.1 = ((bf16[32,64,1024]{2,1,0:T(8,128)(2,1)}), bf16[32,64,1024]{2,1,0:T(8,128)(2,1)}, u32[]{:S(2)}, u32[]{:S(2)}) async-start(bf16[32,64,1024]{2,1,0:T(8,128)(2,1)} %bitcast.46), calls=%async_computation.1 | async-start | bytes 8388608 | tf_op jit(solution)/shard_map/all_to_all | solution.py:44
  27.6 0.1 sub.64
  27.7 1.5 multiply_subtract_fusion
  29.2 0.1 select_convert_fusion
  29.3 94.7 %all-to-all-done.1 = bf16[32,64,1024]{2,1,0:T(8,128)(2,1)} async-done(((bf16[32,64,1024]{2,1,0:T(8,128)(2,1)}), bf16[32,64,1024]{2,1,0:T(8,128)(2,1)}, u32[]{:S(2)}, u32[]{:S(2)}) %all-to-all-start.1) | async-done | bytes 4194336 | tf_op jit(solution)/shard_map/all_to_all | solution.py:44
  124.0 7.1 %fusion.6 = bf16[1024,1024]{0,1:T(8,128)(2,1)S(1)} fusion(bf16[2048,1024]{1,0:T(8,128)(2,1)} %bitcast.1, s32[2048]{0:T(1024)S(1)} %sub.64), kind=kOutput, calls=%fused_computation.15 | convolution fusion | flops 4298113024 | bytes 6299648 | tf_op jit(solution)/shard_map/dot_general | solution.py:49
  131.1 0.4 broadcast_select_fusion
  131.5 1.6 collective-permute-start
  133.1 2.5 collective-permute-done
  135.6 1.5 copy_bitcast_fusion
  137.1 4.2 %all-to-all-start.2 = ((bf16[4,128,1152]{1,2,0:T(8,128)(2,1)}), bf16[4,128,1152]{1,2,0:T(8,128)(2,1)S(1)}, u32[]{:S(2)}, u32[]{:S(2)}) async-start(bf16[4,128,1152]{1,2,0:T(8,128)(2,1)} %copy_bitcast_fusion), calls=%async_computation.2 | async-start | bytes 2359296 | tf_op jit(solution)/shard_map/all_to_all | solution.py:74
  141.3 0.0 copy-done
  141.3 0.8 copy.62
  142.1 15.1 %all-to-all-done.2 = bf16[4,128,1152]{1,2,0:T(8,128)(2,1)S(1)} async-done(((bf16[4,128,1152]{1,2,0:T(8,128)(2,1)}), bf16[4,128,1152]{1,2,0:T(8,128)(2,1)S(1)}, u32[]{:S(2)}, u32[]{:S(2)}) %all-to-all-start.2) | async-done | bytes 1179680 | tf_op jit(solution)/shard_map/all_to_all | solution.py:74
  157.2 0.1 convert_reduce_fusion
  157.4 1.0 divide_convert_fusion
  158.4 0.0 copy-start.2
  158.4 0.1 copy.56
  158.6 0.1 broadcast_in_dim.182
  158.7 15.9 %all_to_all.42 = bf16[4,128,1024]{2,1,0:T(8,128)(2,1)S(1)} all-to-all(bf16[4,128,1024]{2,1,0:T(8,128)(2,1)S(1)} %broadcast_in_dim.182), channel_id=1, replica_groups={{0,2,4,6},{1,3,5,7},{8,10,12,14},{9,11,13,15},{16,18,20,22},{17,19,21,2..., dimensions={0} | all-to-all | bytes 2097152 | tf_op jit(solution)/shard_map/all_to_all | solution.py:82
  174.6 2.6 collective-permute-start.1
  177.2 0.0 copy-done.2
  177.2 0.5 multiply_subtract_fusion.1
  177.7 1.9 collective-permute-done.1
  179.6 2.2 multiply_reduce_fusion
  181.8 0.0 copy-start.1
  181.8 0.3 select_reduce_fusion
  182.1 1.3 fusion.7
  183.4 0.0 copy-done.1
  183.4 0.3 select_convert_fusion.1
  183.7 0.1 pad_maximum_fusion.1
  183.8 18.7 %all_to_all.43 = bf16[4,128,1152]{2,1,0:T(8,128)(2,1)S(1)} all-to-all(bf16[4,128,1152]{2,1,0:T(8,128)(2,1)S(1)} %bitcast.43), channel_id=1, replica_groups={{0,64,128,192},{8,72,136,200},{16,80,144,208},{24,88,152,216},{32,96,16..., dimensions={0} | all-to-all | bytes 2359296 | tf_op jit(solution)/shard_map/all_to_all | solution.py:112
  202.5 0.2 convert_reduce_fusion.4
  202.7 0.1 copy.63
  202.8 0.1 copy.64
  202.9 0.1 broadcast_in_dim.193
  203.0 0.1 reshape.167
  203.1 0.1 broadcast_in_dim.195
  203.2 0.1 broadcast_in_dim.200
  203.3 0.2 select_convert_fusion.2
  203.4 0.1 slice_reduce_fusion
  203.6 0.7 pad_maximum_fusion.2
  204.3 3.4 %all-to-all-start.5 = ((bf16[8,16,1152]{2,1,0:T(8,128)(2,1)}), bf16[8,16,1152]{2,1,0:T(8,128)(2,1)S(1)}, u32[]{:S(2)}, u32[]{:S(2)}) async-start(bf16[8,16,1152]{2,1,0:T(8,128)(2,1)} %pad_maximum_fusion.2), calls=%async_computation.5 | async-start | bytes 589824 | tf_op jit(solution)/shard_map/all_to_all | solution.py:121
  207.7 10.5 %all-to-all-done.5 = bf16[8,16,1152]{2,1,0:T(8,128)(2,1)S(1)} async-done(((bf16[8,16,1152]{2,1,0:T(8,128)(2,1)}), bf16[8,16,1152]{2,1,0:T(8,128)(2,1)S(1)}, u32[]{:S(2)}, u32[]{:S(2)}) %all-to-all-start.5) | async-done | bytes 294944 | tf_op jit(solution)/shard_map/all_to_all | solution.py:121
  218.3 0.1 copy.65
  218.5 1.0 multiply_reduce_fusion.2
  219.5 0.1 select_convert_fusion.3
  219.6 12.4 %all_to_all.44 = bf16[8,16,1152]{2,1,0:T(8,128)(2,1)S(1)} all-to-all(bf16[8,16,1152]{2,1,0:T(8,128)(2,1)S(1)} %broadcast_in_dim.211), channel_id=1, replica_groups={{0,8,16,24,32,40,48,56},{64,72,80,88,96,104,112,120},{128,136,144,152,1..., dimensions={0} | all-to-all | bytes 589824 | tf_op jit(solution)/shard_map/all_to_all | solution.py:137
  232.0 0.1 broadcast_in_dim.212
  232.1 15.1 %all_to_all.45 = bf16[4,8,16,1152]{3,2,1,0:T(8,128)(2,1)S(1)} all-to-all(bf16[4,8,16,1152]{3,2,1,0:T(8,128)(2,1)S(1)} %broadcast_in_dim.212), channel_id=1, replica_groups={{0,64,128,192},{8,72,136,200},{16,80,144,208},{24,88,152,216},{32,96,16..., dimensions={0} | all-to-all | bytes 2359296 | tf_op jit(solution)/shard_map/all_to_all | solution.py:139
  247.3 0.3 copy.66
  247.6 0.6 fusion.20
  248.2 1.1 slice.120
  249.3 17.1 %psum.7 = f32[]{:T(128)} all-reduce(f32[]{:T(128)} %fusion.20), channel_id=1, replica_groups=mesh['wide'=32,'narrow'=8] {'narrow'}, use_global_device_ids=true, to_apply=%region_11.12 | all-reduce | flops 1 | bytes 8 | tf_op jit(solution)/shard_map/psum | solution.py:144
  266.4 0.7 multiply_divide_fusion
  267.1 0.7 div.60
  (20 shorter events, 0.3 us)
Async XLA Ops:
  0.6 140.6 %copy-start = (bf16[1024,1024]{1,0:T(8,128)(2,1)S(1)}, bf16[1024,1024]{1,0:T(8,128)(2,1)}, u32[]{:S(2)}) copy-start(bf16[1024,1024]{1,0:T(8,128)(2,1)} %param.9) | copy-start | bytes 6291460
  22.6 101.4 %all-to-all-start.1 = ((bf16[32,64,1024]{2,1,0:T(8,128)(2,1)}), bf16[32,64,1024]{2,1,0:T(8,128)(2,1)}, u32[]{:S(2)}, u32[]{:S(2)}) async-start(bf16[32,64,1024]{2,1,0:T(8,128)(2,1)} %bitcast.46), calls=%async_computation.1 | async-start | bytes 8388608 | tf_op jit(solution)/shard_map/all_to_all | solution.py:44
  131.5 4.1 %collective-permute-start = (bf16[512,1152]{0,1:T(8,128)(2,1)S(1)}, bf16[512,1152]{0,1:T(8,128)(2,1)S(1)}, u32[]{:S(2)}, u32[]{:S(2)}) collective-permute-start(bf16[512,1152]{0,1:T(8,128)(2,1)S(1)} %broadcast_select_fusion), channel_id=1, source_target_pairs={{0,1},{1,0},{2,3},{3,2},{4,5},{5,4},{6,7},{7,6},{8,9},{9,8},{10,11... | collective-permute-start | bytes 3538952 | tf_op jit(solution)/shard_map/ppermute | solution.py:71
  137.1 20.1 %all-to-all-start.2 = ((bf16[4,128,1152]{1,2,0:T(8,128)(2,1)}), bf16[4,128,1152]{1,2,0:T(8,128)(2,1)S(1)}, u32[]{:S(2)}, u32[]{:S(2)}) async-start(bf16[4,128,1152]{1,2,0:T(8,128)(2,1)} %copy_bitcast_fusion), calls=%async_computation.2 | async-start | bytes 2359296 | tf_op jit(solution)/shard_map/all_to_all | solution.py:74
  158.4 18.8 %copy-start.2 = (s32[1024]{0:T(1024)S(1)}, s32[1024]{0:T(1024)}, u32[]{:S(2)}) copy-start(s32[1024]{0:T(1024)} %param.11) | copy-start | bytes 12292
  174.6 5.0 %collective-permute-start.1 = (bf16[512,1024]{1,0:T(8,128)(2,1)S(1)}, bf16[512,1024]{1,0:T(8,128)(2,1)}, u32[]{:S(2)}, u32[]{:S(2)}) collective-permute-start(bf16[512,1024]{1,0:T(8,128)(2,1)S(1)} %bitcast.44), channel_id=1, source_target_pairs={{0,1},{1,0},{2,3},{3,2},{4,5},{5,4},{6,7},{7,6},{8,9},{9,8},{10,11... | collective-permute-start | bytes 3145736 | tf_op jit(solution)/shard_map/ppermute | solution.py:83
  181.8 1.6 copy-start.1
  204.3 14.0 %all-to-all-start.5 = ((bf16[8,16,1152]{2,1,0:T(8,128)(2,1)}), bf16[8,16,1152]{2,1,0:T(8,128)(2,1)S(1)}, u32[]{:S(2)}, u32[]{:S(2)}) async-start(bf16[8,16,1152]{2,1,0:T(8,128)(2,1)} %pad_maximum_fusion.2), calls=%async_computation.5 | async-start | bytes 589824 | tf_op jit(solution)/shard_map/all_to_all | solution.py:121

commit v6 on v5

--- a/solution.py
+++ b/solution.py
@@ -108,17 +108,17 @@
     squares_high, squares_low = split_float(group_squares, 2)
     counts_high, counts_low = split_whole(group_counts, 16.0)
     sent_two = pack_columns(group_sums, [squares_high, squares_low, counts_high, counts_low])
-    sent_two = sent_two.reshape(x_count, z_count * part_size, -1)
-    got_x = lax.all_to_all(sent_two, "wide", 0, 0, axis_index_groups=x_rings, tiled=True)
-    x_sums = jnp.sum(got_x[:, :, :feature_dim].astype(jnp.float32), axis=0)
-    x_tail = jnp.sum(got_x[:, :, feature_dim : feature_dim + 4].astype(jnp.float32), axis=0)
-    x_squares = x_tail[:, 0] + x_tail[:, 1]
-    x_counts = 16.0 * x_tail[:, 2] + x_tail[:, 3]
-    squares_high, squares_low = split_float(x_squares, 2)
-    counts_high, counts_low = split_whole(x_counts, 16.0)
-    sent_z = pack_columns(x_sums, [squares_high, squares_low, counts_high, counts_low])
-    sent_z = sent_z.reshape(z_count, part_size, -1)
-    got_two = lax.all_to_all(sent_z, "wide", 0, 0, axis_index_groups=z_rings, tiled=True)
+    sent_two = sent_two.reshape(x_count, z_count, part_size, -1).transpose(1, 0, 2, 3)
+    got_z = lax.all_to_all(sent_two, "wide", 0, 0, axis_index_groups=z_rings, tiled=True)
+    z_sums = jnp.sum(got_z[:, :, :, :feature_dim].astype(jnp.float32), axis=0)
+    z_tail = jnp.sum(got_z[:, :, :, feature_dim : feature_dim + 4].astype(jnp.float32), axis=0)
+    z_squares = z_tail[:, :, 0] + z_tail[:, :, 1]
+    z_counts = 16.0 * z_tail[:, :, 2] + z_tail[:, :, 3]
+    squares_high, squares_low = split_float(z_squares.reshape(-1), 2)
+    counts_high, counts_low = split_whole(z_counts.reshape(-1), 16.0)
+    sent_x = pack_columns(z_sums.reshape(x_count * part_size, -1), [squares_high, squares_low, counts_high, counts_low])
+    sent_x = sent_x.reshape(x_count, part_size, -1)
+    got_two = lax.all_to_all(sent_x, "wide", 0, 0, axis_index_groups=x_rings, tiled=True)
     sums_two = jnp.sum(got_two[:, :, :feature_dim].astype(jnp.float32), axis=0)
     tail_two = jnp.sum(got_two[:, :, feature_dim : feature_dim + 4].astype(jnp.float32), axis=0)
     squares_two = tail_two[:, 0] + tail_two[:, 1]

time: 268 us -> 278 us (1.037)
  blocking collectives: 99.6 us -> 114 us
  waiting for transfers between devices: 125 us -> 119 us
    all_to_all x1, blocking collectives: 18.7 us -> 33.9 us  [local(): lax.all_to_all(sent_two, 'wide', 0, 0, axis_index_groups=z_rings, tiled=T...]
    all_to_all x1, waiting for transfers between devices: 10.5 us -> 4.87 us  [local(): lax.all_to_all(sent_x, 'wide', 0, 0, axis_index_groups=x_rings, tiled=True)]
where the time goes in v6:
time: 278 us; the launch traced here: 277 us
  waiting for transfers between devices  119 us (43%)
  blocking collectives  114 us (41%)
  starting transfers between devices  16.6 us (6%)
  other arithmetic  10.4 us (4%)
  matrix products  10.3 us (4%)
  local copies, waits for them, and re-layouts  5.24 us (2%)
    all_to_all x1, waiting for transfers between devices, local(): lax.all_to_all(block_rows, 'wide', split_axis=0, concat_axis=0, tiled=True)  94.7 us
    all_to_all x1, blocking collectives, local(): lax.all_to_all(sent_two, 'wide', 0, 0, axis_index_groups=z_rings, tiled=T...  33.9 us
    all_to_all x1, blocking collectives, local(): lax.all_to_all(sent_ids, 'wide', split_axis=0, concat_axis=0, tiled=True)  20.3 us
    psum x1, blocking collectives, local(): inertia_sum = lax.psum(jnp.sum(inertia_all), 'narrow')  17.7 us
    all_to_all x1, blocking collectives, local(): lax.all_to_all(sent_sub, 'narrow', 0, 0, axis_index_groups=rings, tiled=T...  15.9 us
    all_to_all x1, waiting for transfers between devices, local(): lax.all_to_all(sent_one, 'narrow', 0, 0, axis_index_groups=rings, tiled=T...  15.1 us
    all_to_all x1, blocking collectives, local(): lax.all_to_all(sent_x, 'wide', 0, 0, axis_index_groups=x_rings, tiled=True)  14.6 us
    all_to_all x1, blocking collectives, local(): lax.all_to_all(sent_three, 'wide', 0, 0, axis_index_groups=z_rings, tiled...  12.1 us
  transfers between devices with their start and end apart: 5, of which 5 were waited for; matrix products, arithmetic and copies ran while one was open for 1% of the time, Pallas kernels for 0%

profile of v6, /device:TPU:1, one launch (start us, length us, event | category | flops | bytes accessed | tf_op | source)
XLA Modules:
  0.0 277.0 jit_solution(2654421768362115929)
XLA Ops:
  0.6 0.0 copy-start
  0.6 0.9 reshape.209
  1.6 0.8 compare_select_fusion
  2.3 20.3 %all_to_all.41 = s32[32,1,64]{2,1,0:T(1,128)S(1)} all-to-all(s32[32,1,64]{2,1,0:T(1,128)S(1)} %compare_select_fusion), channel_id=1, replica_groups=mesh['wide'=32,'narrow'=8] {'wide'}, dimensions={0} | all-to-all | bytes 16384 | tf_op jit(solution)/shard_map/all_to_all | solution.py:45
  22.6 4.9 %all-to-all-start.1 = ((bf16[32,64,1024]{2,1,0:T(8,128)(2,1)}), bf16[32,64,1024]{2,1,0:T(8,128)(2,1)}, u32[]{:S(2)}, u32[]{:S(2)}) async-start(bf16[32,64,1024]{2,1,0:T(8,128)(2,1)} %bitcast.49), calls=%async_computation.1 | async-start | bytes 8388608 | tf_op jit(solution)/shard_map/all_to_all | solution.py:44
  27.6 0.1 sub.70
  27.7 1.5 multiply_subtract_fusion
  29.2 0.1 select_convert_fusion
  29.3 94.7 %all-to-all-done.1 = bf16[32,64,1024]{2,1,0:T(8,128)(2,1)} async-done(((bf16[32,64,1024]{2,1,0:T(8,128)(2,1)}), bf16[32,64,1024]{2,1,0:T(8,128)(2,1)}, u32[]{:S(2)}, u32[]{:S(2)}) %all-to-all-start.1) | async-done | bytes 4194336 | tf_op jit(solution)/shard_map/all_to_all | solution.py:44
  124.0 7.1 %fusion.6 = bf16[1024,1024]{0,1:T(8,128)(2,1)S(1)} fusion(bf16[2048,1024]{1,0:T(8,128)(2,1)} %bitcast.1, s32[2048]{0:T(1024)S(1)} %sub.70), kind=kOutput, calls=%fused_computation.15 | convolution fusion | flops 4298113024 | bytes 6299648 | tf_op jit(solution)/shard_map/dot_general | solution.py:49
  131.1 0.4 broadcast_select_fusion
  131.5 1.6 collective-permute-start
  133.1 2.5 collective-permute-done
  135.6 1.5 copy_bitcast_fusion
  137.1 4.2 %all-to-all-start.2 = ((bf16[4,128,1152]{1,2,0:T(8,128)(2,1)}), bf16[4,128,1152]{1,2,0:T(8,128)(2,1)S(1)}, u32[]{:S(2)}, u32[]{:S(2)}) async-start(bf16[4,128,1152]{1,2,0:T(8,128)(2,1)} %copy_bitcast_fusion), calls=%async_computation.2 | async-start | bytes 2359296 | tf_op jit(solution)/shard_map/all_to_all | solution.py:74
  141.3 0.0 copy-done
  141.3 0.8 copy.52
  142.1 15.1 %all-to-all-done.2 = bf16[4,128,1152]{1,2,0:T(8,128)(2,1)S(1)} async-done(((bf16[4,128,1152]{1,2,0:T(8,128)(2,1)}), bf16[4,128,1152]{1,2,0:T(8,128)(2,1)S(1)}, u32[]{:S(2)}, u32[]{:S(2)}) %all-to-all-start.2) | async-done | bytes 1179680 | tf_op jit(solution)/shard_map/all_to_all | solution.py:74
  157.2 0.1 convert_reduce_fusion
  157.4 1.0 divide_convert_fusion
  158.4 0.0 copy-start.2
  158.4 0.1 copy.44
  158.6 0.1 broadcast_in_dim.172
  158.7 15.9 %all_to_all.42 = bf16[4,128,1024]{2,1,0:T(8,128)(2,1)S(1)} all-to-all(bf16[4,128,1024]{2,1,0:T(8,128)(2,1)S(1)} %broadcast_in_dim.172), channel_id=1, replica_groups={{0,2,4,6},{1,3,5,7},{8,10,12,14},{9,11,13,15},{16,18,20,22},{17,19,21,2..., dimensions={0} | all-to-all | bytes 2097152 | tf_op jit(solution)/shard_map/all_to_all | solution.py:82
  174.6 2.6 collective-permute-start.1
  177.2 0.0 copy-done.2
  177.2 0.5 multiply_subtract_fusion.2
  177.7 1.9 collective-permute-done.1
  179.6 2.2 multiply_reduce_fusion
  181.8 0.0 copy-start.1
  181.8 0.3 select_reduce_fusion
  182.1 1.3 fusion.7
  183.4 0.0 copy-done.1
  183.4 0.3 select_convert_fusion.1
  183.7 0.1 pad_maximum_fusion.1
  183.8 0.1 copy.63
  183.9 33.9 %all_to_all.43 = bf16[8,4,16,1152]{3,2,1,0:T(8,128)(2,1)S(1)} all-to-all(bf16[8,4,16,1152]{3,2,1,0:T(8,128)(2,1)S(1)} %bitcast.46), channel_id=1, replica_groups={{0,8,16,24,32,40,48,56},{64,72,80,88,96,104,112,120},{128,136,144,152,1..., dimensions={0} | all-to-all | bytes 2359296 | tf_op jit(solution)/shard_map/all_to_all | solution.py:112
  217.9 0.3 copy.53
  218.2 0.1 copy.54
  218.3 0.1 copy.56
  218.4 0.1 copy.55
  218.5 0.1 add_reduce_fusion.1
  218.6 0.1 copy.57
  218.7 0.1 add_reduce_fusion
  218.8 0.1 select_convert_fusion.2
  218.9 0.1 slice_reduce_fusion
  219.1 0.7 pad_maximum_fusion.2
  219.7 3.3 %all-to-all-start.5 = ((bf16[4,16,1152]{2,1,0:T(8,128)(2,1)}), bf16[4,16,1152]{2,1,0:T(8,128)(2,1)S(1)}, u32[]{:S(2)}, u32[]{:S(2)}) async-start(bf16[4,16,1152]{2,1,0:T(8,128)(2,1)} %pad_maximum_fusion.2), calls=%async_computation.5 | async-start | bytes 294912 | tf_op jit(solution)/shard_map/all_to_all | solution.py:121
  223.1 4.9 %all-to-all-done.5 = bf16[4,16,1152]{2,1,0:T(8,128)(2,1)S(1)} async-done(((bf16[4,16,1152]{2,1,0:T(8,128)(2,1)}), bf16[4,16,1152]{2,1,0:T(8,128)(2,1)S(1)}, u32[]{:S(2)}, u32[]{:S(2)}) %all-to-all-start.5) | async-done | bytes 147488 | tf_op jit(solution)/shard_map/all_to_all | solution.py:121
  228.0 0.1 copy.58
  228.1 1.0 multiply_reduce_fusion.2
  229.1 0.1 select_convert_fusion.3
  229.2 12.1 %all_to_all.44 = bf16[8,16,1152]{2,1,0:T(8,128)(2,1)S(1)} all-to-all(bf16[8,16,1152]{2,1,0:T(8,128)(2,1)S(1)} %broadcast_in_dim.196), channel_id=1, replica_groups={{0,8,16,24,32,40,48,56},{64,72,80,88,96,104,112,120},{128,136,144,152,1..., dimensions={0} | all-to-all | bytes 589824 | tf_op jit(solution)/shard_map/all_to_all | solution.py:137
  241.3 0.1 broadcast_in_dim.197
  241.4 14.6 %all_to_all.45 = bf16[4,8,16,1152]{3,2,1,0:T(8,128)(2,1)S(1)} all-to-all(bf16[4,8,16,1152]{3,2,1,0:T(8,128)(2,1)S(1)} %broadcast_in_dim.197), channel_id=1, replica_groups={{0,64,128,192},{8,72,136,200},{16,80,144,208},{24,88,152,216},{32,96,16..., dimensions={0} | all-to-all | bytes 2359296 | tf_op jit(solution)/shard_map/all_to_all | solution.py:139
  256.0 0.3 copy.59
  256.3 0.6 fusion.19
  256.9 1.1 slice.120
  258.0 17.7 %psum.7 = f32[]{:T(128)} all-reduce(f32[]{:T(128)} %fusion.19), channel_id=1, replica_groups=mesh['wide'=32,'narrow'=8] {'narrow'}, use_global_device_ids=true, to_apply=%region_11.12 | all-reduce | flops 1 | bytes 8 | tf_op jit(solution)/shard_map/psum | solution.py:144
  275.7 0.7 multiply_divide_fusion
  276.4 0.7 div.60
  (23 shorter events, 0.3 us)
Async XLA Ops:
  0.6 140.6 %copy-start = (bf16[1024,1024]{1,0:T(8,128)(2,1)S(1)}, bf16[1024,1024]{1,0:T(8,128)(2,1)}, u32[]{:S(2)}) copy-start(bf16[1024,1024]{1,0:T(8,128)(2,1)} %param.9) | copy-start | bytes 6291460
  22.6 101.4 %all-to-all-start.1 = ((bf16[32,64,1024]{2,1,0:T(8,128)(2,1)}), bf16[32,64,1024]{2,1,0:T(8,128)(2,1)}, u32[]{:S(2)}, u32[]{:S(2)}) async-start(bf16[32,64,1024]{2,1,0:T(8,128)(2,1)} %bitcast.49), calls=%async_computation.1 | async-start | bytes 8388608 | tf_op jit(solution)/shard_map/all_to_all | solution.py:44
  131.5 4.1 %collective-permute-start = (bf16[512,1152]{0,1:T(8,128)(2,1)S(1)}, bf16[512,1152]{0,1:T(8,128)(2,1)S(1)}, u32[]{:S(2)}, u32[]{:S(2)}) collective-permute-start(bf16[512,1152]{0,1:T(8,128)(2,1)S(1)} %broadcast_select_fusion), channel_id=1, source_target_pairs={{0,1},{1,0},{2,3},{3,2},{4,5},{5,4},{6,7},{7,6},{8,9},{9,8},{10,11... | collective-permute-start | bytes 3538952 | tf_op jit(solution)/shard_map/ppermute | solution.py:71
  137.1 20.1 %all-to-all-start.2 = ((bf16[4,128,1152]{1,2,0:T(8,128)(2,1)}), bf16[4,128,1152]{1,2,0:T(8,128)(2,1)S(1)}, u32[]{:S(2)}, u32[]{:S(2)}) async-start(bf16[4,128,1152]{1,2,0:T(8,128)(2,1)} %copy_bitcast_fusion), calls=%async_computation.2 | async-start | bytes 2359296 | tf_op jit(solution)/shard_map/all_to_all | solution.py:74
  158.4 18.8 %copy-start.2 = (s32[1024]{0:T(1024)S(1)}, s32[1024]{0:T(1024)}, u32[]{:S(2)}) copy-start(s32[1024]{0:T(1024)} %param.11) | copy-start | bytes 12292
  174.6 5.0 %collective-permute-start.1 = (bf16[512,1024]{1,0:T(8,128)(2,1)S(1)}, bf16[512,1024]{1,0:T(8,128)(2,1)}, u32[]{:S(2)}, u32[]{:S(2)}) collective-permute-start(bf16[512,1024]{1,0:T(8,128)(2,1)S(1)} %bitcast.47), channel_id=1, source_target_pairs={{0,1},{1,0},{2,3},{3,2},{4,5},{5,4},{6,7},{7,6},{8,9},{9,8},{10,11... | collective-permute-start | bytes 3145736 | tf_op jit(solution)/shard_map/ppermute | solution.py:83
  181.8 1.6 copy-start.1
  219.7 8.2 %all-to-all-start.5 = ((bf16[4,16,1152]{2,1,0:T(8,128)(2,1)}), bf16[4,16,1152]{2,1,0:T(8,128)(2,1)S(1)}, u32[]{:S(2)}, u32[]{:S(2)}) async-start(bf16[4,16,1152]{2,1,0:T(8,128)(2,1)} %pad_maximum_fusion.2), calls=%async_computation.5 | async-start | bytes 294912 | tf_op jit(solution)/shard_map/all_to_all | solution.py:121

commit v7 on v5

--- a/solution.py
+++ b/solution.py
@@ -141,7 +141,9 @@
     level2_new = got_three[:, :, :feature_dim].reshape(group_size, feature_dim)
     tail_three = got_three[:, :, feature_dim : feature_dim + 3].astype(jnp.float32)
     inertia_all = ((tail_three[:, :, 0] + tail_three[:, :, 1]) + tail_three[:, :, 2]).reshape(group_size)
-    inertia_sum = lax.psum(jnp.sum(inertia_all), "narrow")
+    inertia_part = jnp.sum(inertia_all)
+    inertia_chip = inertia_part + lax.ppermute(inertia_part, "narrow", partner)
+    inertia_sum = lax.psum(inertia_chip, "narrow", axis_index_groups=rings)
     centroid_total = float(group_size * narrow_count)
     split_weights = centroid_total * inertia_all / inertia_sum
     return (level1_new, level2_new, split_weights)

time: 268 us -> 266 us (level)
  blocking collectives: 99.6 us -> 89.8 us
  starting transfers between devices: 16.7 us -> 21.4 us
    psum x1, blocking collectives: 17.1 us -> 7.36 us  [local(): inertia_sum = lax.psum(inertia_chip, 'narrow', axis_index_groups=rings)]
    ppermute x0 -> x1, starting transfers between devices: none -> 4.75 us  [local(): inertia_chip = inertia_part + lax.ppermute(inertia_part, 'narrow', partner)]
  transfers between devices with their start and end apart: 5 -> 6, of which waited for: 5 -> 6; matrix products, arithmetic and copies ran while one was open for 1% -> 1% of each run, Pallas kernels for 0% -> 0%
where the time goes in v7:
time: 266 us; the launch traced here: 265 us
  waiting for transfers between devices  126 us (47%)
  blocking collectives  89.8 us (34%)
  starting transfers between devices  21.4 us (8%)
  other arithmetic  10.6 us (4%)
  matrix products  10.3 us (4%)
  local copies, waits for them, and re-layouts  4.94 us (2%)
    all_to_all x1, waiting for transfers between devices, local(): lax.all_to_all(block_rows, 'wide', split_axis=0, concat_axis=0, tiled=True)  94.7 us
    all_to_all x1, blocking collectives, local(): lax.all_to_all(sent_ids, 'wide', split_axis=0, concat_axis=0, tiled=True)  20.3 us
    all_to_all x1, blocking collectives, local(): lax.all_to_all(sent_two, 'wide', 0, 0, axis_index_groups=x_rings, tiled=T...  18.7 us
    all_to_all x1, blocking collectives, local(): lax.all_to_all(sent_sub, 'narrow', 0, 0, axis_index_groups=rings, tiled=T...  15.9 us
    all_to_all x1, blocking collectives, local(): lax.all_to_all(sent_x, 'wide', 0, 0, axis_index_groups=x_rings, tiled=True)  15.1 us
    all_to_all x1, waiting for transfers between devices, local(): lax.all_to_all(sent_one, 'narrow', 0, 0, axis_index_groups=rings, tiled=T...  15.1 us
    all_to_all x1, blocking collectives, local(): lax.all_to_all(sent_three, 'wide', 0, 0, axis_index_groups=z_rings, tiled...  12.4 us
    all_to_all x1, waiting for transfers between devices, local(): lax.all_to_all(sent_z, 'wide', 0, 0, axis_index_groups=z_rings, tiled=True)  10.5 us
  transfers between devices with their start and end apart: 6, of which 6 were waited for; matrix products, arithmetic and copies ran while one was open for 1% of the time, Pallas kernels for 0%

profile of v7, /device:TPU:1, one launch (start us, length us, event | category | flops | bytes accessed | tf_op | source)
XLA Modules:
  0.0 265.0 jit_solution(5989779130863208358)
XLA Ops:
  0.6 0.0 copy-start
  0.6 0.9 reshape.159
  1.6 0.8 compare_select_fusion
  2.3 20.3 %all_to_all.41 = s32[32,1,64]{2,1,0:T(1,128)S(1)} all-to-all(s32[32,1,64]{2,1,0:T(1,128)S(1)} %compare_select_fusion), channel_id=1, replica_groups=mesh['wide'=32,'narrow'=8] {'wide'}, dimensions={0} | all-to-all | bytes 16384 | tf_op jit(solution)/shard_map/all_to_all | solution.py:45
  22.6 4.9 %all-to-all-start.1 = ((bf16[32,64,1024]{2,1,0:T(8,128)(2,1)}), bf16[32,64,1024]{2,1,0:T(8,128)(2,1)}, u32[]{:S(2)}, u32[]{:S(2)}) async-start(bf16[32,64,1024]{2,1,0:T(8,128)(2,1)} %bitcast.46), calls=%async_computation.1 | async-start | bytes 8388608 | tf_op jit(solution)/shard_map/all_to_all | solution.py:44
  27.6 0.1 sub.64
  27.7 1.5 multiply_subtract_fusion
  29.2 0.1 select_convert_fusion
  29.3 94.7 %all-to-all-done.1 = bf16[32,64,1024]{2,1,0:T(8,128)(2,1)} async-done(((bf16[32,64,1024]{2,1,0:T(8,128)(2,1)}), bf16[32,64,1024]{2,1,0:T(8,128)(2,1)}, u32[]{:S(2)}, u32[]{:S(2)}) %all-to-all-start.1) | async-done | bytes 4194336 | tf_op jit(solution)/shard_map/all_to_all | solution.py:44
  124.0 7.1 %fusion.6 = bf16[1024,1024]{0,1:T(8,128)(2,1)S(1)} fusion(bf16[2048,1024]{1,0:T(8,128)(2,1)} %bitcast.1, s32[2048]{0:T(1024)S(1)} %sub.64), kind=kOutput, calls=%fused_computation.15 | convolution fusion | flops 4298113024 | bytes 6299648 | tf_op jit(solution)/shard_map/dot_general | solution.py:49
  131.1 0.4 broadcast_select_fusion
  131.5 1.6 collective-permute-start
  133.1 2.5 collective-permute-done
  135.6 1.5 copy_bitcast_fusion
  137.1 4.2 %all-to-all-start.2 = ((bf16[4,128,1152]{1,2,0:T(8,128)(2,1)}), bf16[4,128,1152]{1,2,0:T(8,128)(2,1)S(1)}, u32[]{:S(2)}, u32[]{:S(2)}) async-start(bf16[4,128,1152]{1,2,0:T(8,128)(2,1)} %copy_bitcast_fusion), calls=%async_computation.2 | async-start | bytes 2359296 | tf_op jit(solution)/shard_map/all_to_all | solution.py:74
  141.3 0.0 copy-done
  141.3 0.8 copy.62
  142.1 15.1 %all-to-all-done.2 = bf16[4,128,1152]{1,2,0:T(8,128)(2,1)S(1)} async-done(((bf16[4,128,1152]{1,2,0:T(8,128)(2,1)}), bf16[4,128,1152]{1,2,0:T(8,128)(2,1)S(1)}, u32[]{:S(2)}, u32[]{:S(2)}) %all-to-all-start.2) | async-done | bytes 1179680 | tf_op jit(solution)/shard_map/all_to_all | solution.py:74
  157.2 0.1 convert_reduce_fusion
  157.4 1.0 divide_convert_fusion
  158.4 0.0 copy-start.2
  158.4 0.1 copy.56
  158.6 0.1 broadcast_in_dim.182
  158.7 15.9 %all_to_all.42 = bf16[4,128,1024]{2,1,0:T(8,128)(2,1)S(1)} all-to-all(bf16[4,128,1024]{2,1,0:T(8,128)(2,1)S(1)} %broadcast_in_dim.182), channel_id=1, replica_groups={{0,2,4,6},{1,3,5,7},{8,10,12,14},{9,11,13,15},{16,18,20,22},{17,19,21,2..., dimensions={0} | all-to-all | bytes 2097152 | tf_op jit(solution)/shard_map/all_to_all | solution.py:82
  174.6 2.6 collective-permute-start.1
  177.2 0.0 copy-done.2
  177.2 0.5 multiply_subtract_fusion.1
  177.7 1.9 collective-permute-done.1
  179.6 2.2 multiply_reduce_fusion
  181.8 0.0 copy-start.1
  181.8 0.3 select_reduce_fusion
  182.1 1.3 fusion.7
  183.4 0.0 copy-done.1
  183.4 0.3 select_convert_fusion.1
  183.7 0.1 pad_maximum_fusion.1
  183.8 18.7 %all_to_all.43 = bf16[4,128,1152]{2,1,0:T(8,128)(2,1)S(1)} all-to-all(bf16[4,128,1152]{2,1,0:T(8,128)(2,1)S(1)} %bitcast.43), channel_id=1, replica_groups={{0,64,128,192},{8,72,136,200},{16,80,144,208},{24,88,152,216},{32,96,16..., dimensions={0} | all-to-all | bytes 2359296 | tf_op jit(solution)/shard_map/all_to_all | solution.py:112
  202.5 0.2 convert_reduce_fusion.4
  202.7 0.1 copy.63
  202.8 0.1 copy.64
  202.9 0.1 broadcast_in_dim.193
  203.0 0.1 reshape.167
  203.1 0.1 broadcast_in_dim.195
  203.2 0.1 broadcast_in_dim.200
  203.3 0.2 select_convert_fusion.2
  203.4 0.1 slice_reduce_fusion
  203.6 0.7 pad_maximum_fusion.2
  204.3 3.4 %all-to-all-start.5 = ((bf16[8,16,1152]{2,1,0:T(8,128)(2,1)}), bf16[8,16,1152]{2,1,0:T(8,128)(2,1)S(1)}, u32[]{:S(2)}, u32[]{:S(2)}) async-start(bf16[8,16,1152]{2,1,0:T(8,128)(2,1)} %pad_maximum_fusion.2), calls=%async_computation.5 | async-start | bytes 589824 | tf_op jit(solution)/shard_map/all_to_all | solution.py:121
  207.7 10.5 %all-to-all-done.5 = bf16[8,16,1152]{2,1,0:T(8,128)(2,1)S(1)} async-done(((bf16[8,16,1152]{2,1,0:T(8,128)(2,1)}), bf16[8,16,1152]{2,1,0:T(8,128)(2,1)S(1)}, u32[]{:S(2)}, u32[]{:S(2)}) %all-to-all-start.5) | async-done | bytes 294944 | tf_op jit(solution)/shard_map/all_to_all | solution.py:121
  218.3 0.1 copy.65
  218.5 1.0 multiply_reduce_fusion.2
  219.5 0.1 select_convert_fusion.3
  219.6 12.4 %all_to_all.44 = bf16[8,16,1152]{2,1,0:T(8,128)(2,1)S(1)} all-to-all(bf16[8,16,1152]{2,1,0:T(8,128)(2,1)S(1)} %broadcast_in_dim.211), channel_id=1, replica_groups={{0,8,16,24,32,40,48,56},{64,72,80,88,96,104,112,120},{128,136,144,152,1..., dimensions={0} | all-to-all | bytes 589824 | tf_op jit(solution)/shard_map/all_to_all | solution.py:137
  232.0 0.1 broadcast_in_dim.212
  232.1 15.1 %all_to_all.45 = bf16[4,8,16,1152]{3,2,1,0:T(8,128)(2,1)S(1)} all-to-all(bf16[4,8,16,1152]{3,2,1,0:T(8,128)(2,1)S(1)} %broadcast_in_dim.212), channel_id=1, replica_groups={{0,64,128,192},{8,72,136,200},{16,80,144,208},{24,88,152,216},{32,96,16..., dimensions={0} | all-to-all | bytes 2359296 | tf_op jit(solution)/shard_map/all_to_all | solution.py:139
  247.3 0.3 copy.66
  247.6 0.6 fusion.20
  248.2 4.8 %collective-permute-start.2 = (f32[]{:T(128)}, f32[]{:T(128)}, u32[]{:S(2)}, u32[]{:S(2)}) collective-permute-start(f32[]{:T(128)} %fusion.20), channel_id=1, source_target_pairs={{0,1},{1,0},{2,3},{3,2},{4,5},{5,4},{6,7},{7,6},{8,9},{9,8},{10,11... | collective-permute-start | bytes 20 | tf_op jit(solution)/shard_map/ppermute | solution.py:145
  252.9 1.0 collective-permute-done.2
  255.2 1.1 slice.120
  256.3 7.4 %psum.7 = f32[]{:T(128)} all-reduce(f32[]{:T(128)S(6)} %add.102), channel_id=1, replica_groups={{0,2,4,6},{1,3,5,7},{8,10,12,14},{9,11,13,15},{16,18,20,22},{17,19,21,2..., use_global_device_ids=true, to_apply=%region_11.12 | all-reduce | flops 1 | bytes 8 | tf_op jit(solution)/shard_map/psum | solution.py:146
  263.7 0.7 multiply_divide_fusion
  264.4 0.7 div.60
  (20 shorter events, 0.3 us)
Async XLA Ops:
  0.6 140.6 %copy-start = (bf16[1024,1024]{1,0:T(8,128)(2,1)S(1)}, bf16[1024,1024]{1,0:T(8,128)(2,1)}, u32[]{:S(2)}) copy-start(bf16[1024,1024]{1,0:T(8,128)(2,1)} %param.9) | copy-start | bytes 6291460
  22.6 101.4 %all-to-all-start.1 = ((bf16[32,64,1024]{2,1,0:T(8,128)(2,1)}), bf16[32,64,1024]{2,1,0:T(8,128)(2,1)}, u32[]{:S(2)}, u32[]{:S(2)}) async-start(bf16[32,64,1024]{2,1,0:T(8,128)(2,1)} %bitcast.46), calls=%async_computation.1 | async-start | bytes 8388608 | tf_op jit(solution)/shard_map/all_to_all | solution.py:44
  131.5 4.1 %collective-permute-start = (bf16[512,1152]{0,1:T(8,128)(2,1)S(1)}, bf16[512,1152]{0,1:T(8,128)(2,1)S(1)}, u32[]{:S(2)}, u32[]{:S(2)}) collective-permute-start(bf16[512,1152]{0,1:T(8,128)(2,1)S(1)} %broadcast_select_fusion), channel_id=1, source_target_pairs={{0,1},{1,0},{2,3},{3,2},{4,5},{5,4},{6,7},{7,6},{8,9},{9,8},{10,11... | collective-permute-start | bytes 3538952 | tf_op jit(solution)/shard_map/ppermute | solution.py:71
  137.1 20.1 %all-to-all-start.2 = ((bf16[4,128,1152]{1,2,0:T(8,128)(2,1)}), bf16[4,128,1152]{1,2,0:T(8,128)(2,1)S(1)}, u32[]{:S(2)}, u32[]{:S(2)}) async-start(bf16[4,128,1152]{1,2,0:T(8,128)(2,1)} %copy_bitcast_fusion), calls=%async_computation.2 | async-start | bytes 2359296 | tf_op jit(solution)/shard_map/all_to_all | solution.py:74
  158.4 18.8 %copy-start.2 = (s32[1024]{0:T(1024)S(1)}, s32[1024]{0:T(1024)}, u32[]{:S(2)}) copy-start(s32[1024]{0:T(1024)} %param.11) | copy-start | bytes 12292
  174.6 5.0 %collective-permute-start.1 = (bf16[512,1024]{1,0:T(8,128)(2,1)S(1)}, bf16[512,1024]{1,0:T(8,128)(2,1)}, u32[]{:S(2)}, u32[]{:S(2)}) collective-permute-start(bf16[512,1024]{1,0:T(8,128)(2,1)S(1)} %bitcast.44), channel_id=1, source_target_pairs={{0,1},{1,0},{2,3},{3,2},{4,5},{5,4},{6,7},{7,6},{8,9},{9,8},{10,11... | collective-permute-start | bytes 3145736 | tf_op jit(solution)/shard_map/ppermute | solution.py:83
  181.8 1.6 copy-start.1
  204.3 14.0 %all-to-all-start.5 = ((bf16[8,16,1152]{2,1,0:T(8,128)(2,1)}), bf16[8,16,1152]{2,1,0:T(8,128)(2,1)S(1)}, u32[]{:S(2)}, u32[]{:S(2)}) async-start(bf16[8,16,1152]{2,1,0:T(8,128)(2,1)} %pad_maximum_fusion.2), calls=%async_computation.5 | async-start | bytes 589824 | tf_op jit(solution)/shard_map/all_to_all | solution.py:121
  248.2 5.7 %collective-permute-start.2 = (f32[]{:T(128)}, f32[]{:T(128)}, u32[]{:S(2)}, u32[]{:S(2)}) collective-permute-start(f32[]{:T(128)} %fusion.20), channel_id=1, source_target_pairs={{0,1},{1,0},{2,3},{3,2},{4,5},{5,4},{6,7},{7,6},{8,9},{9,8},{10,11... | collective-permute-start | bytes 20 | tf_op jit(solution)/shard_map/ppermute | solution.py:145

commit v8 on v7

--- a/solution.py
+++ b/solution.py
@@ -42,7 +42,13 @@
     live_slots = position < block_counts[:, None]
     sent_ids = jnp.where(live_slots, level1_ids.reshape(wide_count, slot_count), -1)
     got_rows = lax.all_to_all(block_rows, "wide", split_axis=0, concat_axis=0, tiled=True)
-    got_ids = lax.all_to_all(sent_ids, "wide", split_axis=0, concat_axis=0, tiled=True)
+    shifted = [jnp.take(sent_ids, wide_index, axis=0)]
+    for shift in range(1, wide_count):
+        chunk = jnp.take(sent_ids, (wide_index + shift) % wide_count, axis=0)
+        pairs = [(i, (i + shift) % wide_count) for i in range(wide_count)]
+        shifted.append(lax.ppermute(chunk, "wide", pairs))
+    by_shift = jnp.stack(shifted)
+    got_ids = jnp.take(by_shift, (wide_index - jnp.arange(wide_count)) % wide_count, axis=0)
 
     owner_index = got_ids.reshape(-1) - owner_base
     owner_table = lax.broadcasted_iota(jnp.int32, (owner_size, 1), 0) == owner_index[None, :]

time: 266 us -> 347 us (1.30); the launches traced: 265 us -> 342 us
  starting transfers between devices: 21.4 us -> 129 us
  blocking collectives: 89.8 us -> 69.3 us
  waiting for transfers between devices: 126 us -> 116 us
    all_to_all x1, waiting for transfers between devices: 94.7 us -> 0.01 us  [local(): lax.all_to_all(block_rows, 'wide', split_axis=0, concat_axis=0, tiled=True)]
    ppermute x0 -> x31, starting transfers between devices: none -> 93.2 us  [local(): shifted.append(lax.ppermute(chunk, 'wide', pairs))]
    ppermute x0 -> x31, waiting for transfers between devices: none -> 85.3 us  [local(): shifted.append(lax.ppermute(chunk, 'wide', pairs))]
    all_to_all x1 -> x0, blocking collectives: 20.3 us -> none  [local(): lax.all_to_all(sent_ids, 'wide', split_axis=0, concat_axis=0, tiled=True)]
    all_to_all x1, starting transfers between devices: 4.85 us -> 12.1 us  [local(): lax.all_to_all(block_rows, 'wide', split_axis=0, concat_axis=0, tiled=True)]
    ppermute x1, starting transfers between devices: 1.64 us -> 7.2 us  [local(): lax.ppermute(given, 'narrow', partner).astype(jnp.float32)]
  transfers between devices with their start and end apart: 6 -> 37, of which waited for: 6 -> 7; matrix products, arithmetic and copies ran while one was open for 1% -> 1% of each run, Pallas kernels for 0% -> 0%
where the time goes in v8:
time: 347 us; the launch traced here: 342 us
  starting transfers between devices  129 us (37%)
  waiting for transfers between devices  116 us (33%)
  blocking collectives  69.3 us (20%)
  matrix products  10.3 us (3%)
  other arithmetic  10.1 us (3%)
  local copies, waits for them, and re-layouts  4.78 us (1%)
    ppermute x31, starting transfers between devices, local(): shifted.append(lax.ppermute(chunk, 'wide', pairs))  93.2 us
    ppermute x31, waiting for transfers between devices, local(): shifted.append(lax.ppermute(chunk, 'wide', pairs))  85.3 us
    all_to_all x1, blocking collectives, local(): lax.all_to_all(sent_two, 'wide', 0, 0, axis_index_groups=x_rings, tiled=T...  18.7 us
    all_to_all x1, blocking collectives, local(): lax.all_to_all(sent_sub, 'narrow', 0, 0, axis_index_groups=rings, tiled=T...  15.9 us
    all_to_all x1, waiting for transfers between devices, local(): lax.all_to_all(sent_one, 'narrow', 0, 0, axis_index_groups=rings, tiled=T...  15.1 us
    all_to_all x1, blocking collectives, local(): lax.all_to_all(sent_x, 'wide', 0, 0, axis_index_groups=x_rings, tiled=True)  14.4 us
    all_to_all x1, blocking collectives, local(): lax.all_to_all(sent_three, 'wide', 0, 0, axis_index_groups=z_rings, tiled...  12.9 us
    all_to_all x1, starting transfers between devices, local(): lax.all_to_all(block_rows, 'wide', split_axis=0, concat_axis=0, tiled=True)  12.1 us
  transfers between devices with their start and end apart: 37, of which 7 were waited for; matrix products, arithmetic and copies ran while one was open for 1% of the time, Pallas kernels for 0%

profile of v8, /device:TPU:1, one launch (start us, length us, event | category | flops | bytes accessed | tf_op | source)
XLA Modules:
  0.0 341.8 jit_solution(7083727175629676415)
XLA Ops:
  0.7 12.1 %all-to-all-start = ((bf16[32,64,1024]{2,1,0:T(8,128)(2,1)}), bf16[32,64,1024]{2,1,0:T(8,128)(2,1)}, u32[]{:S(2)}, u32[]{:S(2)}) async-start(bf16[32,64,1024]{2,1,0:T(8,128)(2,1)} %bitcast.142), calls=%async_computation | async-start | bytes 8388608 | tf_op jit(solution)/shard_map/all_to_all | solution.py:44
  13.2 4.9 %collective-permute-start.22 = (s32[64]{0:T(128)S(1)}, s32[64]{0:T(128)S(1)}, u32[]{:S(2)}, u32[]{:S(2)}) collective-permute-start(s32[64]{0:T(128)S(1)} %get-tuple-element.36), channel_id=1, source_target_pairs={{0,184},{8,192},{16,200},{24,208},{32,216},{40,224},{48,232},{56,2... | collective-permute-start | bytes 776 | tf_op jit(solution)/shard_map/ppermute | solution.py:49
  18.0 0.9 collective-permute-start.23
  18.9 0.5 collective-permute-start.25
  19.5 5.5 %collective-permute-start.26 = (s32[64]{0:T(128)S(1)}, s32[64]{0:T(128)S(1)}, u32[]{:S(2)}, u32[]{:S(2)}) collective-permute-start(s32[64]{0:T(128)S(1)} %get-tuple-element.32), channel_id=1, source_target_pairs={{0,216},{8,224},{16,232},{24,240},{32,248},{40,0},{48,8},{56,16},{... | collective-permute-start | bytes 776 | tf_op jit(solution)/shard_map/ppermute | solution.py:49
  25.1 78.8 %collective-permute-done.22 = s32[64]{0:T(128)S(1)} collective-permute-done((s32[64]{0:T(128)S(1)}, s32[64]{0:T(128)S(1)}, u32[]{:S(2)}, u32[]{:S(2)}) %collective-permute-start.22) | collective-permute-done | bytes 288 | tf_op jit(solution)/shard_map/ppermute | solution.py:49
  103.9 4.4 %collective-permute-start.27 = (s32[64]{0:T(128)S(1)}, s32[64]{0:T(128)S(1)}, u32[]{:S(2)}, u32[]{:S(2)}) collective-permute-start(s32[64]{0:T(128)S(1)} %get-tuple-element.31), channel_id=1, source_target_pairs={{0,224},{8,232},{16,240},{24,248},{32,0},{40,8},{48,16},{56,24},{6... | collective-permute-start | bytes 776 | tf_op jit(solution)/shard_map/ppermute | solution.py:49
  108.3 2.8 collective-permute-start.28
  111.1 1.8 collective-permute-start.29
  112.9 10.9 %collective-permute-start.30 = (s32[64]{0:T(128)S(1)}, s32[64]{0:T(128)S(1)}, u32[]{:S(2)}, u32[]{:S(2)}) collective-permute-start(s32[64]{0:T(128)S(1)} %get-tuple-element.28), channel_id=1, source_target_pairs={{0,248},{8,0},{16,8},{24,16},{32,24},{40,32},{48,40},{56,48},{64,5... | collective-permute-start | bytes 776 | tf_op jit(solution)/shard_map/ppermute | solution.py:49
  123.8 5.9 %collective-permute-start.13 = (s32[64]{0:T(128)S(1)}, s32[64]{0:T(128)S(1)}, u32[]{:S(2)}, u32[]{:S(2)}) collective-permute-start(s32[64]{0:T(128)S(1)} %get-tuple-element.45), channel_id=1, source_target_pairs={{0,112},{8,120},{16,128},{24,136},{32,144},{40,152},{48,160},{56,1... | collective-permute-start | bytes 776 | tf_op jit(solution)/shard_map/ppermute | solution.py:49
  129.7 2.5 collective-permute-start.14
  132.2 1.8 collective-permute-start.15
  133.9 2.1 collective-permute-start.16
  136.0 0.4 collective-permute-start.17
  136.4 4.2 %collective-permute-start.18 = (s32[64]{0:T(128)S(1)}, s32[64]{0:T(128)S(1)}, u32[]{:S(2)}, u32[]{:S(2)}) collective-permute-start(s32[64]{0:T(128)S(1)} %get-tuple-element.40), channel_id=1, source_target_pairs={{0,152},{8,160},{16,168},{24,176},{32,184},{40,192},{48,200},{56,2... | collective-permute-start | bytes 776 | tf_op jit(solution)/shard_map/ppermute | solution.py:49
  140.6 4.9 %collective-permute-start.19 = (s32[64]{0:T(128)S(1)}, s32[64]{0:T(128)S(1)}, u32[]{:S(2)}, u32[]{:S(2)}) collective-permute-start(s32[64]{0:T(128)S(1)} %get-tuple-element.39), channel_id=1, source_target_pairs={{0,160},{8,168},{16,176},{24,184},{32,192},{40,200},{48,208},{56,2... | collective-permute-start | bytes 776 | tf_op jit(solution)/shard_map/ppermute | solution.py:49
  145.5 3.1 collective-permute-start.20
  148.5 0.7 collective-permute-start.21
  149.2 1.9 collective-permute-start.4
  151.1 3.7 %collective-permute-start.5 = (s32[64]{0:T(128)S(1)}, s32[64]{0:T(128)S(1)}, u32[]{:S(2)}, u32[]{:S(2)}) collective-permute-start(s32[64]{0:T(128)S(1)} %get-tuple-element.53), channel_id=1, source_target_pairs={{0,48},{8,56},{16,64},{24,72},{32,80},{40,88},{48,96},{56,104},{64... | collective-permute-start | bytes 776 | tf_op jit(solution)/shard_map/ppermute | solution.py:49
  154.8 0.9 collective-permute-start.6
  155.7 1.5 collective-permute-start.7
  157.2 1.9 collective-permute-start.8
  159.1 3.9 %collective-permute-start.10 = (s32[64]{0:T(128)S(1)}, s32[64]{0:T(128)S(1)}, u32[]{:S(2)}, u32[]{:S(2)}) collective-permute-start(s32[64]{0:T(128)S(1)} %get-tuple-element.48), channel_id=1, source_target_pairs={{0,88},{8,96},{16,104},{24,112},{32,120},{40,128},{48,136},{56,144... | collective-permute-start | bytes 776 | tf_op jit(solution)/shard_map/ppermute | solution.py:49
  162.9 3.4 %collective-permute-start.11 = (s32[64]{0:T(128)S(1)}, s32[64]{0:T(128)S(1)}, u32[]{:S(2)}, u32[]{:S(2)}) collective-permute-start(s32[64]{0:T(128)S(1)} %get-tuple-element.47), channel_id=1, source_target_pairs={{0,96},{8,104},{16,112},{24,120},{32,128},{40,136},{48,144},{56,15... | collective-permute-start | bytes 776 | tf_op jit(solution)/shard_map/ppermute | solution.py:49
  166.4 2.8 collective-permute-start.12
  169.2 2.1 collective-permute-start
  171.2 1.3 collective-permute-start.1
  172.5 2.5 collective-permute-start.2
  175.0 10.5 %collective-permute-start.3 = (s32[64]{0:T(128)S(1)}, s32[64]{0:T(128)S(1)}, u32[]{:S(2)}, u32[]{:S(2)}) collective-permute-start(s32[64]{0:T(128)S(1)} %get-tuple-element.55), channel_id=1, source_target_pairs={{0,32},{8,40},{16,48},{24,56},{32,64},{40,72},{48,80},{56,88},{64,... | collective-permute-start | bytes 776 | tf_op jit(solution)/shard_map/ppermute | solution.py:49
  185.5 6.5 %collective-permute-done.3 = s32[64]{0:T(128)S(1)} collective-permute-done((s32[64]{0:T(128)S(1)}, s32[64]{0:T(128)S(1)}, u32[]{:S(2)}, u32[]{:S(2)}) %collective-permute-start.3) | collective-permute-done | bytes 288 | tf_op jit(solution)/shard_map/ppermute | solution.py:49
  192.1 0.6 gather_fusion
  192.8 1.5 multiply_subtract_fusion
  194.4 7.1 %fusion.6 = bf16[1024,1024]{0,1:T(8,128)(2,1)S(1)} fusion(bf16[2048,1024]{1,0:T(8,128)(2,1)} %bitcast.65, s32[2048]{0:T(1024)S(1)} %sub.87), kind=kOutput, calls=%fused_computation.16 | convolution fusion | flops 4298113024 | bytes 6299648 | tf_op jit(solution)/shard_map/dot_general | solution.py:55
  201.5 0.4 broadcast_select_fusion
  201.9 7.2 %collective-permute-start.31 = (bf16[512,1152]{0,1:T(8,128)(2,1)S(1)}, bf16[512,1152]{0,1:T(8,128)(2,1)S(1)}, u32[]{:S(2)}, u32[]{:S(2)}) collective-permute-start(bf16[512,1152]{0,1:T(8,128)(2,1)S(1)} %broadcast_select_fusion), channel_id=1, source_target_pairs={{0,1},{1,0},{2,3},{3,2},{4,5},{5,4},{6,7},{7,6},{8,9},{9,8},{10,11... | collective-permute-start | bytes 3538952 | tf_op jit(solution)/shard_map/ppermute | solution.py:77
  209.1 2.5 collective-permute-done.31
  211.6 1.5 copy_bitcast_fusion
  213.1 4.1 %all-to-all-start.1 = ((bf16[4,128,1152]{1,2,0:T(8,128)(2,1)}), bf16[4,128,1152]{1,2,0:T(8,128)(2,1)S(1)}, u32[]{:S(2)}, u32[]{:S(2)}) async-start(bf16[4,128,1152]{1,2,0:T(8,128)(2,1)} %copy_bitcast_fusion), calls=%async_computation.1 | async-start | bytes 2359296 | tf_op jit(solution)/shard_map/all_to_all | solution.py:80
  217.2 0.8 copy.62
  218.0 15.1 %all-to-all-done.1 = bf16[4,128,1152]{1,2,0:T(8,128)(2,1)S(1)} async-done(((bf16[4,128,1152]{1,2,0:T(8,128)(2,1)}), bf16[4,128,1152]{1,2,0:T(8,128)(2,1)S(1)}, u32[]{:S(2)}, u32[]{:S(2)}) %all-to-all-start.1) | async-done | bytes 1179680 | tf_op jit(solution)/shard_map/all_to_all | solution.py:80
  233.2 1.0 divide_convert_fusion
  234.6 15.9 %all_to_all.35 = bf16[4,128,1024]{2,1,0:T(8,128)(2,1)S(1)} all-to-all(bf16[4,128,1024]{2,1,0:T(8,128)(2,1)S(1)} %broadcast_in_dim.203), channel_id=1, replica_groups={{0,2,4,6},{1,3,5,7},{8,10,12,14},{9,11,13,15},{16,18,20,22},{17,19,21,2..., dimensions={0} | all-to-all | bytes 2097152 | tf_op jit(solution)/shard_map/all_to_all | solution.py:88
  250.5 2.6 collective-permute-start.32
  253.1 0.5 multiply_subtract_fusion.1
  253.5 1.9 collective-permute-done.32
  255.5 2.2 multiply_reduce_fusion
  257.7 1.3 fusion.7
  259.3 0.3 select_convert_fusion.1
  259.7 18.7 %all_to_all.36 = bf16[4,128,1152]{2,1,0:T(8,128)(2,1)S(1)} all-to-all(bf16[4,128,1152]{2,1,0:T(8,128)(2,1)S(1)} %bitcast.139), channel_id=1, replica_groups={{0,64,128,192},{8,72,136,200},{16,80,144,208},{24,88,152,216},{32,96,16..., dimensions={0} | all-to-all | bytes 2359296 | tf_op jit(solution)/shard_map/all_to_all | solution.py:118
  279.5 0.7 pad_maximum_fusion.2
  280.2 4.5 %all-to-all-start.4 = ((bf16[8,16,1152]{2,1,0:T(8,128)(2,1)}), bf16[8,16,1152]{2,1,0:T(8,128)(2,1)S(1)}, u32[]{:S(2)}, u32[]{:S(2)}) async-start(bf16[8,16,1152]{2,1,0:T(8,128)(2,1)} %pad_maximum_fusion.2), calls=%async_computation.4 | async-start | bytes 589824 | tf_op jit(solution)/shard_map/all_to_all | solution.py:127
  284.7 9.6 %all-to-all-done.4 = bf16[8,16,1152]{2,1,0:T(8,128)(2,1)S(1)} async-done(((bf16[8,16,1152]{2,1,0:T(8,128)(2,1)}), bf16[8,16,1152]{2,1,0:T(8,128)(2,1)S(1)}, u32[]{:S(2)}, u32[]{:S(2)}) %all-to-all-start.4) | async-done | bytes 294944 | tf_op jit(solution)/shard_map/all_to_all | solution.py:127
  294.6 1.0 multiply_reduce_fusion.2
  295.7 12.9 %all_to_all.37 = bf16[8,16,1152]{2,1,0:T(8,128)(2,1)S(1)} all-to-all(bf16[8,16,1152]{2,1,0:T(8,128)(2,1)S(1)} %broadcast_in_dim.232), channel_id=1, replica_groups={{0,8,16,24,32,40,48,56},{64,72,80,88,96,104,112,120},{128,136,144,152,1..., dimensions={0} | all-to-all | bytes 589824 | tf_op jit(solution)/shard_map/all_to_all | solution.py:143
  308.7 14.4 %all_to_all.38 = bf16[4,8,16,1152]{3,2,1,0:T(8,128)(2,1)S(1)} all-to-all(bf16[4,8,16,1152]{3,2,1,0:T(8,128)(2,1)S(1)} %broadcast_in_dim.233), channel_id=1, replica_groups={{0,64,128,192},{8,72,136,200},{16,80,144,208},{24,88,152,216},{32,96,16..., dimensions={0} | all-to-all | bytes 2359296 | tf_op jit(solution)/shard_map/all_to_all | solution.py:145
  323.4 0.6 fusion.55
  324.0 5.4 %collective-permute-start.33 = (f32[]{:T(128)}, f32[]{:T(128)}, u32[]{:S(2)}, u32[]{:S(2)}) collective-permute-start(f32[]{:T(128)} %fusion.55), channel_id=1, source_target_pairs={{0,1},{1,0},{2,3},{3,2},{4,5},{5,4},{6,7},{7,6},{8,9},{9,8},{10,11... | collective-permute-start | bytes 20 | tf_op jit(solution)/shard_map/ppermute | solution.py:151
  329.5 1.1 collective-permute-done.33
  331.9 1.1 slice.129
  333.0 7.4 %psum.7 = f32[]{:T(128)} all-reduce(f32[]{:T(128)S(6)} %add.391), channel_id=1, replica_groups={{0,2,4,6},{1,3,5,7},{8,10,12,14},{9,11,13,15},{16,18,20,22},{17,19,21,2..., use_global_device_ids=true, to_apply=%region_11.13 | all-reduce | flops 1 | bytes 8 | tf_op jit(solution)/shard_map/psum | solution.py:152
  340.3 0.7 multiply_divide_fusion
  341.0 0.7 div.60
  (92 shorter events, 3.4 us)
Async XLA Ops:
  0.6 216.5 %copy-start = (bf16[1024,1024]{1,0:T(8,128)(2,1)S(1)}, bf16[1024,1024]{1,0:T(8,128)(2,1)}, u32[]{:S(2)}) copy-start(bf16[1024,1024]{1,0:T(8,128)(2,1)} %param.11) | copy-start | bytes 6291460
  0.6 12.3 %copy-start.2 = (s32[2048]{0:T(1024)S(1)}, s32[2048]{0:T(1024)}, u32[]{:S(2)}) copy-start(s32[2048]{0:T(1024)} %param.9) | copy-start | bytes 24580
  0.7 12.4 %copy-start.4 = (s32[32]{0:T(128)S(1)}, s32[32]{0:T(128)}, u32[]{:S(2)}) copy-start(s32[32]{0:T(128)} %param.10) | copy-start | bytes 388
  0.7 193.8 %all-to-all-start = ((bf16[32,64,1024]{2,1,0:T(8,128)(2,1)}), bf16[32,64,1024]{2,1,0:T(8,128)(2,1)}, u32[]{:S(2)}, u32[]{:S(2)}) async-start(bf16[32,64,1024]{2,1,0:T(8,128)(2,1)} %bitcast.142), calls=%async_computation | async-start | bytes 8388608 | tf_op jit(solution)/shard_map/all_to_all | solution.py:44
  13.2 90.7 %collective-permute-start.22 = (s32[64]{0:T(128)S(1)}, s32[64]{0:T(128)S(1)}, u32[]{:S(2)}, u32[]{:S(2)}) collective-permute-start(s32[64]{0:T(128)S(1)} %get-tuple-element.36), channel_id=1, source_target_pairs={{0,184},{8,192},{16,200},{24,208},{32,216},{40,224},{48,232},{56,2... | collective-permute-start | bytes 776 | tf_op jit(solution)/shard_map/ppermute | solution.py:49
  18.0 90.3 %collective-permute-start.23 = (s32[64]{0:T(128)S(1)}, s32[64]{0:T(128)S(1)}, u32[]{:S(2)}, u32[]{:S(2)}) collective-permute-start(s32[64]{0:T(128)S(1)} %get-tuple-element.35), channel_id=1, source_target_pairs={{0,192},{8,200},{16,208},{24,216},{32,224},{40,232},{48,240},{56,2... | collective-permute-start | bytes 776 | tf_op jit(solution)/shard_map/ppermute | solution.py:49
  18.9 92.2 %collective-permute-start.24 = (s32[64]{0:T(128)S(1)}, s32[64]{0:T(128)S(1)}, u32[]{:S(2)}, u32[]{:S(2)}) collective-permute-start(s32[64]{0:T(128)S(1)} %get-tuple-element.34), channel_id=1, source_target_pairs={{0,200},{8,208},{16,216},{24,224},{32,232},{40,240},{48,248},{56,0... | collective-permute-start | bytes 776 | tf_op jit(solution)/shard_map/ppermute | solution.py:49
  18.9 94.0 %collective-permute-start.25 = (s32[64]{0:T(128)S(1)}, s32[64]{0:T(128)S(1)}, u32[]{:S(2)}, u32[]{:S(2)}) collective-permute-start(s32[64]{0:T(128)S(1)} %get-tuple-element.33), channel_id=1, source_target_pairs={{0,208},{8,216},{16,224},{24,232},{32,240},{40,248},{48,0},{56,8},... | collective-permute-start | bytes 776 | tf_op jit(solution)/shard_map/ppermute | solution.py:49
  19.5 104.4 %collective-permute-start.26 = (s32[64]{0:T(128)S(1)}, s32[64]{0:T(128)S(1)}, u32[]{:S(2)}, u32[]{:S(2)}) collective-permute-start(s32[64]{0:T(128)S(1)} %get-tuple-element.32), channel_id=1, source_target_pairs={{0,216},{8,224},{16,232},{24,240},{32,248},{40,0},{48,8},{56,16},{... | collective-permute-start | bytes 776 | tf_op jit(solution)/shard_map/ppermute | solution.py:49
  103.9 25.8 %collective-permute-start.27 = (s32[64]{0:T(128)S(1)}, s32[64]{0:T(128)S(1)}, u32[]{:S(2)}, u32[]{:S(2)}) collective-permute-start(s32[64]{0:T(128)S(1)} %get-tuple-element.31), channel_id=1, source_target_pairs={{0,224},{8,232},{16,240},{24,248},{32,0},{40,8},{48,16},{56,24},{6... | collective-permute-start | bytes 776 | tf_op jit(solution)/shard_map/ppermute | solution.py:49
  108.3 23.8 %collective-permute-start.28 = (s32[64]{0:T(128)S(1)}, s32[64]{0:T(128)S(1)}, u32[]{:S(2)}, u32[]{:S(2)}) collective-permute-start(s32[64]{0:T(128)S(1)} %get-tuple-element.30), channel_id=1, source_target_pairs={{0,232},{8,240},{16,248},{24,0},{32,8},{40,16},{48,24},{56,32},{64... | collective-permute-start | bytes 776 | tf_op jit(solution)/shard_map/ppermute | solution.py:49
  111.1 22.8 %collective-permute-start.29 = (s32[64]{0:T(128)S(1)}, s32[64]{0:T(128)S(1)}, u32[]{:S(2)}, u32[]{:S(2)}) collective-permute-start(s32[64]{0:T(128)S(1)} %get-tuple-element.29), channel_id=1, source_target_pairs={{0,240},{8,248},{16,0},{24,8},{32,16},{40,24},{48,32},{56,40},{64,... | collective-permute-start | bytes 776 | tf_op jit(solution)/shard_map/ppermute | solution.py:49
  112.9 23.1 %collective-permute-start.30 = (s32[64]{0:T(128)S(1)}, s32[64]{0:T(128)S(1)}, u32[]{:S(2)}, u32[]{:S(2)}) collective-permute-start(s32[64]{0:T(128)S(1)} %get-tuple-element.28), channel_id=1, source_target_pairs={{0,248},{8,0},{16,8},{24,16},{32,24},{40,32},{48,40},{56,48},{64,5... | collective-permute-start | bytes 776 | tf_op jit(solution)/shard_map/ppermute | solution.py:49
  123.8 12.5 %collective-permute-start.13 = (s32[64]{0:T(128)S(1)}, s32[64]{0:T(128)S(1)}, u32[]{:S(2)}, u32[]{:S(2)}) collective-permute-start(s32[64]{0:T(128)S(1)} %get-tuple-element.45), channel_id=1, source_target_pairs={{0,112},{8,120},{16,128},{24,136},{32,144},{40,152},{48,160},{56,1... | collective-permute-start | bytes 776 | tf_op jit(solution)/shard_map/ppermute | solution.py:49
  129.7 10.9 %collective-permute-start.14 = (s32[64]{0:T(128)S(1)}, s32[64]{0:T(128)S(1)}, u32[]{:S(2)}, u32[]{:S(2)}) collective-permute-start(s32[64]{0:T(128)S(1)} %get-tuple-element.44), channel_id=1, source_target_pairs={{0,120},{8,128},{16,136},{24,144},{32,152},{40,160},{48,168},{56,1... | collective-permute-start | bytes 776 | tf_op jit(solution)/shard_map/ppermute | solution.py:49
  132.2 13.3 %collective-permute-start.15 = (s32[64]{0:T(128)S(1)}, s32[64]{0:T(128)S(1)}, u32[]{:S(2)}, u32[]{:S(2)}) collective-permute-start(s32[64]{0:T(128)S(1)} %get-tuple-element.43), channel_id=1, source_target_pairs={{0,128},{8,136},{16,144},{24,152},{32,160},{40,168},{48,176},{56,1... | collective-permute-start | bytes 776 | tf_op jit(solution)/shard_map/ppermute | solution.py:49
  133.9 14.6 %collective-permute-start.16 = (s32[64]{0:T(128)S(1)}, s32[64]{0:T(128)S(1)}, u32[]{:S(2)}, u32[]{:S(2)}) collective-permute-start(s32[64]{0:T(128)S(1)} %get-tuple-element.42), channel_id=1, source_target_pairs={{0,136},{8,144},{16,152},{24,160},{32,168},{40,176},{48,184},{56,1... | collective-permute-start | bytes 776 | tf_op jit(solution)/shard_map/ppermute | solution.py:49
  136.0 13.2 %collective-permute-start.17 = (s32[64]{0:T(128)S(1)}, s32[64]{0:T(128)S(1)}, u32[]{:S(2)}, u32[]{:S(2)}) collective-permute-start(s32[64]{0:T(128)S(1)} %get-tuple-element.41), channel_id=1, source_target_pairs={{0,144},{8,152},{16,160},{24,168},{32,176},{40,184},{48,192},{56,2... | collective-permute-start | bytes 776 | tf_op jit(solution)/shard_map/ppermute | solution.py:49
  136.4 14.7 %collective-permute-start.18 = (s32[64]{0:T(128)S(1)}, s32[64]{0:T(128)S(1)}, u32[]{:S(2)}, u32[]{:S(2)}) collective-permute-start(s32[64]{0:T(128)S(1)} %get-tuple-element.40), channel_id=1, source_target_pairs={{0,152},{8,160},{16,168},{24,176},{32,184},{40,192},{48,200},{56,2... | collective-permute-start | bytes 776 | tf_op jit(solution)/shard_map/ppermute | solution.py:49
  140.6 14.2 %collective-permute-start.19 = (s32[64]{0:T(128)S(1)}, s32[64]{0:T(128)S(1)}, u32[]{:S(2)}, u32[]{:S(2)}) collective-permute-start(s32[64]{0:T(128)S(1)} %get-tuple-element.39), channel_id=1, source_target_pairs={{0,160},{8,168},{16,176},{24,184},{32,192},{40,200},{48,208},{56,2... | collective-permute-start | bytes 776 | tf_op jit(solution)/shard_map/ppermute | solution.py:49
  145.5 10.2 %collective-permute-start.20 = (s32[64]{0:T(128)S(1)}, s32[64]{0:T(128)S(1)}, u32[]{:S(2)}, u32[]{:S(2)}) collective-permute-start(s32[64]{0:T(128)S(1)} %get-tuple-element.38), channel_id=1, source_target_pairs={{0,168},{8,176},{16,184},{24,192},{32,200},{40,208},{48,216},{56,2... | collective-permute-start | bytes 776 | tf_op jit(solution)/shard_map/ppermute | solution.py:49
  148.5 8.7 %collective-permute-start.21 = (s32[64]{0:T(128)S(1)}, s32[64]{0:T(128)S(1)}, u32[]{:S(2)}, u32[]{:S(2)}) collective-permute-start(s32[64]{0:T(128)S(1)} %get-tuple-element.37), channel_id=1, source_target_pairs={{0,176},{8,184},{16,192},{24,200},{32,208},{40,216},{48,224},{56,2... | collective-permute-start | bytes 776 | tf_op jit(solution)/shard_map/ppermute | solution.py:49
  149.2 9.8 %collective-permute-start.4 = (s32[64]{0:T(128)S(1)}, s32[64]{0:T(128)S(1)}, u32[]{:S(2)}, u32[]{:S(2)}) collective-permute-start(s32[64]{0:T(128)S(1)} %get-tuple-element.54), channel_id=1, source_target_pairs={{0,40},{8,48},{16,56},{24,64},{32,72},{40,80},{48,88},{56,96},{64,... | collective-permute-start | bytes 776 | tf_op jit(solution)/shard_map/ppermute | solution.py:49
  151.1 8.0 %collective-permute-start.5 = (s32[64]{0:T(128)S(1)}, s32[64]{0:T(128)S(1)}, u32[]{:S(2)}, u32[]{:S(2)}) collective-permute-start(s32[64]{0:T(128)S(1)} %get-tuple-element.53), channel_id=1, source_target_pairs={{0,48},{8,56},{16,64},{24,72},{32,80},{40,88},{48,96},{56,104},{64... | collective-permute-start | bytes 776 | tf_op jit(solution)/shard_map/ppermute | solution.py:49
  154.8 8.2 %collective-permute-start.6 = (s32[64]{0:T(128)S(1)}, s32[64]{0:T(128)S(1)}, u32[]{:S(2)}, u32[]{:S(2)}) collective-permute-start(s32[64]{0:T(128)S(1)} %get-tuple-element.52), channel_id=1, source_target_pairs={{0,56},{8,64},{16,72},{24,80},{32,88},{40,96},{48,104},{56,112},{6... | collective-permute-start | bytes 776 | tf_op jit(solution)/shard_map/ppermute | solution.py:49
  155.7 10.7 %collective-permute-start.7 = (s32[64]{0:T(128)S(1)}, s32[64]{0:T(128)S(1)}, u32[]{:S(2)}, u32[]{:S(2)}) collective-permute-start(s32[64]{0:T(128)S(1)} %get-tuple-element.51), channel_id=1, source_target_pairs={{0,64},{8,72},{16,80},{24,88},{32,96},{40,104},{48,112},{56,120},{... | collective-permute-start | bytes 776 | tf_op jit(solution)/shard_map/ppermute | solution.py:49
  157.2 12.0 %collective-permute-start.8 = (s32[64]{0:T(128)S(1)}, s32[64]{0:T(128)S(1)}, u32[]{:S(2)}, u32[]{:S(2)}) collective-permute-start(s32[64]{0:T(128)S(1)} %get-tuple-element.50), channel_id=1, source_target_pairs={{0,72},{8,80},{16,88},{24,96},{32,104},{40,112},{48,120},{56,128},... | collective-permute-start | bytes 776 | tf_op jit(solution)/shard_map/ppermute | solution.py:49
  159.1 12.2 %collective-permute-start.9 = (s32[64]{0:T(128)S(1)}, s32[64]{0:T(128)S(1)}, u32[]{:S(2)}, u32[]{:S(2)}) collective-permute-start(s32[64]{0:T(128)S(1)} %get-tuple-element.49), channel_id=1, source_target_pairs={{0,80},{8,88},{16,96},{24,104},{32,112},{40,120},{48,128},{56,136}... | collective-permute-start | bytes 776 | tf_op jit(solution)/shard_map/ppermute | solution.py:49
  159.1 13.4 %collective-permute-start.10 = (s32[64]{0:T(128)S(1)}, s32[64]{0:T(128)S(1)}, u32[]{:S(2)}, u32[]{:S(2)}) collective-permute-start(s32[64]{0:T(128)S(1)} %get-tuple-element.48), channel_id=1, source_target_pairs={{0,88},{8,96},{16,104},{24,112},{32,120},{40,128},{48,136},{56,144... | collective-permute-start | bytes 776 | tf_op jit(solution)/shard_map/ppermute | solution.py:49
  162.9 12.0 %collective-permute-start.11 = (s32[64]{0:T(128)S(1)}, s32[64]{0:T(128)S(1)}, u32[]{:S(2)}, u32[]{:S(2)}) collective-permute-start(s32[64]{0:T(128)S(1)} %get-tuple-element.47), channel_id=1, source_target_pairs={{0,96},{8,104},{16,112},{24,120},{32,128},{40,136},{48,144},{56,15... | collective-permute-start | bytes 776 | tf_op jit(solution)/shard_map/ppermute | solution.py:49
  166.4 19.1 %collective-permute-start.12 = (s32[64]{0:T(128)S(1)}, s32[64]{0:T(128)S(1)}, u32[]{:S(2)}, u32[]{:S(2)}) collective-permute-start(s32[64]{0:T(128)S(1)} %get-tuple-element.46), channel_id=1, source_target_pairs={{0,104},{8,112},{16,120},{24,128},{32,136},{40,144},{48,152},{56,1... | collective-permute-start | bytes 776 | tf_op jit(solution)/shard_map/ppermute | solution.py:49
  169.2 16.3 %collective-permute-start = (s32[64]{0:T(128)S(1)}, s32[64]{0:T(128)S(1)}, u32[]{:S(2)}, u32[]{:S(2)}) collective-permute-start(s32[64]{0:T(128)S(1)} %get-tuple-element.58), channel_id=1, source_target_pairs={{0,8},{8,16},{16,24},{24,32},{32,40},{40,48},{48,56},{56,64},{64,7... | collective-permute-start | bytes 776 | tf_op jit(solution)/shard_map/ppermute | solution.py:49
  171.2 14.2 %collective-permute-start.1 = (s32[64]{0:T(128)S(1)}, s32[64]{0:T(128)S(1)}, u32[]{:S(2)}, u32[]{:S(2)}) collective-permute-start(s32[64]{0:T(128)S(1)} %get-tuple-element.57), channel_id=1, source_target_pairs={{0,16},{8,24},{16,32},{24,40},{32,48},{40,56},{48,64},{56,72},{64,... | collective-permute-start | bytes 776 | tf_op jit(solution)/shard_map/ppermute | solution.py:49
  172.5 13.0 %collective-permute-start.2 = (s32[64]{0:T(128)S(1)}, s32[64]{0:T(128)S(1)}, u32[]{:S(2)}, u32[]{:S(2)}) collective-permute-start(s32[64]{0:T(128)S(1)} %get-tuple-element.56), channel_id=1, source_target_pairs={{0,24},{8,32},{16,40},{24,48},{32,56},{40,64},{48,72},{56,80},{64,... | collective-permute-start | bytes 776 | tf_op jit(solution)/shard_map/ppermute | solution.py:49
  175.0 17.0 %collective-permute-start.3 = (s32[64]{0:T(128)S(1)}, s32[64]{0:T(128)S(1)}, u32[]{:S(2)}, u32[]{:S(2)}) collective-permute-start(s32[64]{0:T(128)S(1)} %get-tuple-element.55), channel_id=1, source_target_pairs={{0,32},{8,40},{16,48},{24,56},{32,64},{40,72},{48,80},{56,88},{64,... | collective-permute-start | bytes 776 | tf_op jit(solution)/shard_map/ppermute | solution.py:49
  201.9 9.7 %collective-permute-start.31 = (bf16[512,1152]{0,1:T(8,128)(2,1)S(1)}, bf16[512,1152]{0,1:T(8,128)(2,1)S(1)}, u32[]{:S(2)}, u32[]{:S(2)}) collective-permute-start(bf16[512,1152]{0,1:T(8,128)(2,1)S(1)} %broadcast_select_fusion), channel_id=1, source_target_pairs={{0,1},{1,0},{2,3},{3,2},{4,5},{5,4},{6,7},{7,6},{8,9},{9,8},{10,11... | collective-permute-start | bytes 3538952 | tf_op jit(solution)/shard_map/ppermute | solution.py:77
  213.1 20.0 %all-to-all-start.1 = ((bf16[4,128,1152]{1,2,0:T(8,128)(2,1)}), bf16[4,128,1152]{1,2,0:T(8,128)(2,1)S(1)}, u32[]{:S(2)}, u32[]{:S(2)}) async-start(bf16[4,128,1152]{1,2,0:T(8,128)(2,1)} %copy_bitcast_fusion), calls=%async_computation.1 | async-start | bytes 2359296 | tf_op jit(solution)/shard_map/all_to_all | solution.py:80
  234.3 18.8 %copy-start.3 = (s32[1024]{0:T(1024)S(1)}, s32[1024]{0:T(1024)}, u32[]{:S(2)}) copy-start(s32[1024]{0:T(1024)} %param.13) | copy-start | bytes 12292
  250.5 5.0 %collective-permute-start.32 = (bf16[512,1024]{1,0:T(8,128)(2,1)S(1)}, bf16[512,1024]{1,0:T(8,128)(2,1)}, u32[]{:S(2)}, u32[]{:S(2)}) collective-permute-start(bf16[512,1024]{1,0:T(8,128)(2,1)S(1)} %bitcast.140), channel_id=1, source_target_pairs={{0,1},{1,0},{2,3},{3,2},{4,5},{5,4},{6,7},{7,6},{8,9},{9,8},{10,11... | collective-permute-start | bytes 3145736 | tf_op jit(solution)/shard_map/ppermute | solution.py:89
  257.7 1.3 copy-start.1
  280.2 14.1 %all-to-all-start.4 = ((bf16[8,16,1152]{2,1,0:T(8,128)(2,1)}), bf16[8,16,1152]{2,1,0:T(8,128)(2,1)S(1)}, u32[]{:S(2)}, u32[]{:S(2)}) async-start(bf16[8,16,1152]{2,1,0:T(8,128)(2,1)} %pad_maximum_fusion.2), calls=%async_computation.4 | async-start | bytes 589824 | tf_op jit(solution)/shard_map/all_to_all | solution.py:127
  324.0 6.5 %collective-permute-start.33 = (f32[]{:T(128)}, f32[]{:T(128)}, u32[]{:S(2)}, u32[]{:S(2)}) collective-permute-start(f32[]{:T(128)} %fusion.55), channel_id=1, source_target_pairs={{0,1},{1,0},{2,3},{3,2},{4,5},{5,4},{6,7},{7,6},{8,9},{9,8},{10,11... | collective-permute-start | bytes 20 | tf_op jit(solution)/shard_map/ppermute | solution.py:151

commit v9 on v7

--- a/solution.py
+++ b/solution.py
@@ -45,30 +45,26 @@
     got_ids = lax.all_to_all(sent_ids, "wide", split_axis=0, concat_axis=0, tiled=True)
 
     owner_index = got_ids.reshape(-1) - owner_base
-    owner_table = lax.broadcasted_iota(jnp.int32, (owner_size, 1), 0) == owner_index[None, :]
-    row_sums = jnp.dot(
-        owner_table.astype(jnp.bfloat16),
-        got_rows.reshape(-1, feature_dim),
-        preferred_element_type=jnp.float32,
-    )
-    row_counts = jnp.dot(
-        owner_table.astype(jnp.bfloat16),
-        jnp.ones((owner_index.shape[0], 128), jnp.bfloat16),
-        preferred_element_type=jnp.float32,
-    )[:, 0]
-
     core_count = 2
     chip_count = narrow_count // core_count
     core = narrow_index % core_count
     chip = narrow_index // core_count
     half_size = owner_size // core_count
     sub_size = half_size // chip_count
-    count_high, count_low = split_whole(row_counts, 16.0)
-    packed = pack_columns(row_sums, [count_high, count_low]).reshape(core_count, half_size, -1)
-    kept = jnp.where(core == 0, packed[0], packed[1])
-    given = jnp.where(core == 0, packed[1], packed[0])
+    rows_here = got_rows.reshape(-1, feature_dim)
+    ones_here = jnp.ones((owner_index.shape[0], 128), jnp.bfloat16)
+
+    def half_packed(half):
+        half_ids = lax.broadcasted_iota(jnp.int32, (half_size, 1), 0) + half * half_size
+        table = (half_ids == owner_index[None, :]).astype(jnp.bfloat16)
+        sums = jnp.dot(table, rows_here, preferred_element_type=jnp.float32)
+        counts = jnp.dot(table, ones_here, preferred_element_type=jnp.float32)[:, 0]
+        count_high, count_low = split_whole(counts, 16.0)
+        return pack_columns(sums, [count_high, count_low])
+
     partner = [(i, i ^ 1) for i in range(narrow_count)]
-    chip_part = kept.astype(jnp.float32) + lax.ppermute(given, "narrow", partner).astype(jnp.float32)
+    given_back = lax.ppermute(half_packed(1 - core), "narrow", partner)
+    chip_part = half_packed(core).astype(jnp.float32) + given_back.astype(jnp.float32)
     rings = [[c + core_count * y for y in range(chip_count)] for c in range(core_count)]
     sent_one = chip_part.astype(jnp.bfloat16).reshape(chip_count, sub_size, -1)
     got_one = lax.all_to_all(sent_one, "narrow", 0, 0, axis_index_groups=rings, tiled=True)

time: 266 us -> 265 us (level)
    dot_general x2 -> x4, matrix products: 8.58 us -> 10.7 us  [the longest x2 9.11 us: half_packed(): sums = jnp.dot(table, rows_here, preferred_element_type=jnp.float32)]
  transfers between devices with their start and end apart: 6 -> 6, of which waited for: 6 -> 5; matrix products, arithmetic and copies ran while one was open for 1% -> 3% of each run, Pallas kernels for 0% -> 0%
where the time goes in v9:
time: 265 us; the launch traced here: 264 us
  waiting for transfers between devices  124 us (47%)
  blocking collectives  90.3 us (34%)
  starting transfers between devices  20.9 us (8%)
  matrix products  12.4 us (5%)
  other arithmetic  10.6 us (4%)
  local copies, waits for them, and re-layouts  3.63 us (1%)
    all_to_all x1, waiting for transfers between devices, local(): lax.all_to_all(block_rows, 'wide', split_axis=0, concat_axis=0, tiled=True)  94.4 us
    all_to_all x1, blocking collectives, local(): lax.all_to_all(sent_ids, 'wide', split_axis=0, concat_axis=0, tiled=True)  20.3 us
    all_to_all x1, blocking collectives, local(): lax.all_to_all(sent_two, 'wide', 0, 0, axis_index_groups=x_rings, tiled=T...  18.7 us
    all_to_all x1, blocking collectives, local(): lax.all_to_all(sent_sub, 'narrow', 0, 0, axis_index_groups=rings, tiled=T...  16.4 us
    all_to_all x1, waiting for transfers between devices, local(): lax.all_to_all(sent_one, 'narrow', 0, 0, axis_index_groups=rings, tiled=T...  16.3 us
    all_to_all x1, blocking collectives, local(): lax.all_to_all(sent_x, 'wide', 0, 0, axis_index_groups=x_rings, tiled=True)  15.1 us
    all_to_all x1, blocking collectives, local(): lax.all_to_all(sent_three, 'wide', 0, 0, axis_index_groups=z_rings, tiled...  12.4 us
    all_to_all x1, waiting for transfers between devices, local(): lax.all_to_all(sent_z, 'wide', 0, 0, axis_index_groups=z_rings, tiled=True)  10.5 us
  transfers between devices with their start and end apart: 6, of which 5 were waited for; matrix products, arithmetic and copies ran while one was open for 3% of the time, Pallas kernels for 0%

profile of v9, /device:TPU:1, one launch (start us, length us, event | category | flops | bytes accessed | tf_op | source)
XLA Modules:
  0.0 264.4 jit_solution(5518016752760206461)
XLA Ops:
  0.6 0.8 reshape.164
  1.4 0.8 compare_select_fusion
  2.2 20.3 %all_to_all.41 = s32[32,1,64]{2,1,0:T(1,128)S(1)} all-to-all(s32[32,1,64]{2,1,0:T(1,128)S(1)} %compare_select_fusion), channel_id=1, replica_groups=mesh['wide'=32,'narrow'=8] {'wide'}, dimensions={0} | all-to-all | bytes 16384 | tf_op jit(solution)/shard_map/all_to_all | solution.py:45
  22.5 4.9 %all-to-all-start.1 = ((bf16[32,64,1024]{2,1,0:T(8,128)(2,1)}), bf16[32,64,1024]{2,1,0:T(8,128)(2,1)}, u32[]{:S(2)}, u32[]{:S(2)}) async-start(bf16[32,64,1024]{2,1,0:T(8,128)(2,1)} %bitcast.43), calls=%async_computation.1 | async-start | bytes 8388608 | tf_op jit(solution)/shard_map/all_to_all | solution.py:44
  27.4 0.1 sub.71
  27.5 0.8 multiply_subtract_fusion.1
  28.3 0.8 multiply_subtract_fusion.2
  29.1 0.3 select_convert_fusion.2
  29.5 94.4 %all-to-all-done.1 = bf16[32,64,1024]{2,1,0:T(8,128)(2,1)} async-done(((bf16[32,64,1024]{2,1,0:T(8,128)(2,1)}), bf16[32,64,1024]{2,1,0:T(8,128)(2,1)}, u32[]{:S(2)}, u32[]{:S(2)}) %all-to-all-start.1) | async-done | bytes 4194336 | tf_op jit(solution)/shard_map/all_to_all | solution.py:44
  123.9 4.6 %fusion.22 = bf16[512,1024]{1,0:T(8,128)(2,1)S(1)} fusion(bf16[2048,1024]{1,0:T(8,128)(2,1)} %bitcast.1, s32[2048]{0:T(1024)S(1)} %sub.71, s32[512]{0:T(512)S(1)} %iota_add_fusion), kind=kOutput, calls=%fused_computation.26 | convolution fusion | flops 2149056512 | bytes 5253120 | tf_op jit(solution)/shard_map/dot_general | solution.py:60
  128.4 0.1 pad_maximum_fusion
  128.5 1.6 collective-permute-start
  130.2 4.6 %fusion.19 = bf16[512,1024]{1,0:T(8,128)(2,1)S(1)} fusion(bf16[2048,1024]{1,0:T(8,128)(2,1)} %bitcast.1, s32[2048]{0:T(1024)S(1)} %sub.71, s32[512]{0:T(512)S(1)} %iota_add_fusion.1), kind=kOutput, calls=%fused_computation.25 | convolution fusion | flops 2149056512 | bytes 5253120 | tf_op jit(solution)/shard_map/dot_general | solution.py:60
  134.7 0.0 collective-permute-done
  134.8 1.3 add_convert_fusion
  136.1 4.2 %all-to-all-start.2 = ((bf16[4,128,1152]{2,1,0:T(8,128)(2,1)}), bf16[4,128,1152]{2,1,0:T(8,128)(2,1)S(1)}, u32[]{:S(2)}, u32[]{:S(2)}) async-start(bf16[4,128,1152]{2,1,0:T(8,128)(2,1)} %bitcast.6), calls=%async_computation.2 | async-start | bytes 2359296 | tf_op jit(solution)/shard_map/all_to_all | solution.py:70
  140.3 16.3 %all-to-all-done.2 = bf16[4,128,1152]{2,1,0:T(8,128)(2,1)S(1)} async-done(((bf16[4,128,1152]{2,1,0:T(8,128)(2,1)}), bf16[4,128,1152]{2,1,0:T(8,128)(2,1)S(1)}, u32[]{:S(2)}, u32[]{:S(2)}) %all-to-all-start.2) | async-done | bytes 1179680 | tf_op jit(solution)/shard_map/all_to_all | solution.py:70
  156.7 0.2 fusion.32
  156.8 0.1 convert_reduce_fusion
  157.0 0.0 copy-start.1
  157.0 1.1 divide_convert_fusion
  158.1 0.1 broadcast_in_dim.193
  158.2 16.4 %all_to_all.42 = bf16[4,128,1024]{2,1,0:T(8,128)(2,1)S(1)} all-to-all(bf16[4,128,1024]{2,1,0:T(8,128)(2,1)S(1)} %broadcast_in_dim.193), channel_id=1, replica_groups={{0,2,4,6},{1,3,5,7},{8,10,12,14},{9,11,13,15},{16,18,20,22},{17,19,21,2..., dimensions={0} | all-to-all | bytes 2097152 | tf_op jit(solution)/shard_map/all_to_all | solution.py:78
  174.6 2.0 collective-permute-start.1
  176.7 0.0 copy-done.1
  176.7 0.5 multiply_subtract_fusion
  177.1 1.9 collective-permute-done.1
  179.1 2.2 multiply_reduce_fusion
  181.3 0.0 copy-start
  181.3 0.3 select_reduce_fusion
  181.6 1.2 fusion.18
  182.8 0.0 copy-done
  182.8 0.3 select_convert_fusion
  183.2 0.1 pad_maximum_fusion.1
  183.3 18.7 %all_to_all.43 = bf16[4,128,1152]{2,1,0:T(8,128)(2,1)S(1)} all-to-all(bf16[4,128,1152]{2,1,0:T(8,128)(2,1)S(1)} %bitcast.40), channel_id=1, replica_groups={{0,64,128,192},{8,72,136,200},{16,80,144,208},{24,88,152,216},{32,96,16..., dimensions={0} | all-to-all | bytes 2359296 | tf_op jit(solution)/shard_map/all_to_all | solution.py:108
  202.0 0.2 subtract_reduce_fusion
  202.2 0.1 broadcast_in_dim.203
  202.3 0.1 reshape.172
  202.4 0.1 broadcast_in_dim.205
  202.5 0.1 broadcast_in_dim.210
  202.6 0.2 select_convert_fusion.3
  202.7 0.1 slice_reduce_fusion
  202.9 0.7 pad_maximum_fusion.2
  203.6 3.4 %all-to-all-start.5 = ((bf16[8,16,1152]{2,1,0:T(8,128)(2,1)}), bf16[8,16,1152]{2,1,0:T(8,128)(2,1)S(1)}, u32[]{:S(2)}, u32[]{:S(2)}) async-start(bf16[8,16,1152]{2,1,0:T(8,128)(2,1)} %pad_maximum_fusion.2), calls=%async_computation.5 | async-start | bytes 589824 | tf_op jit(solution)/shard_map/all_to_all | solution.py:117
  207.0 10.5 %all-to-all-done.5 = bf16[8,16,1152]{2,1,0:T(8,128)(2,1)S(1)} async-done(((bf16[8,16,1152]{2,1,0:T(8,128)(2,1)}), bf16[8,16,1152]{2,1,0:T(8,128)(2,1)S(1)}, u32[]{:S(2)}, u32[]{:S(2)}) %all-to-all-start.5) | async-done | bytes 294944 | tf_op jit(solution)/shard_map/all_to_all | solution.py:117
  217.6 0.1 copy.22
  217.8 1.0 multiply_reduce_fusion.2
  218.8 0.1 select_convert_fusion.4
  218.9 12.4 %all_to_all.44 = bf16[8,16,1152]{2,1,0:T(8,128)(2,1)S(1)} all-to-all(bf16[8,16,1152]{2,1,0:T(8,128)(2,1)S(1)} %broadcast_in_dim.221), channel_id=1, replica_groups={{0,8,16,24,32,40,48,56},{64,72,80,88,96,104,112,120},{128,136,144,152,1..., dimensions={0} | all-to-all | bytes 589824 | tf_op jit(solution)/shard_map/all_to_all | solution.py:133
  231.3 0.1 broadcast_in_dim.222
  231.4 15.1 %all_to_all.45 = bf16[4,8,16,1152]{3,2,1,0:T(8,128)(2,1)S(1)} all-to-all(bf16[4,8,16,1152]{3,2,1,0:T(8,128)(2,1)S(1)} %broadcast_in_dim.222), channel_id=1, replica_groups={{0,64,128,192},{8,72,136,200},{16,80,144,208},{24,88,152,216},{32,96,16..., dimensions={0} | all-to-all | bytes 2359296 | tf_op jit(solution)/shard_map/all_to_all | solution.py:135
  246.6 0.3 copy.23
  246.9 0.6 fusion.39
  247.5 4.8 %collective-permute-start.2 = (f32[]{:T(128)}, f32[]{:T(128)}, u32[]{:S(2)}, u32[]{:S(2)}) collective-permute-start(f32[]{:T(128)} %fusion.39), channel_id=1, source_target_pairs={{0,1},{1,0},{2,3},{3,2},{4,5},{5,4},{6,7},{7,6},{8,9},{9,8},{10,11... | collective-permute-start | bytes 20 | tf_op jit(solution)/shard_map/ppermute | solution.py:141
  252.2 1.0 collective-permute-done.2
  254.5 1.1 slice.114
  255.6 7.4 %psum.7 = f32[]{:T(128)} all-reduce(f32[]{:T(128)S(6)} %add.128), channel_id=1, replica_groups={{0,2,4,6},{1,3,5,7},{8,10,12,14},{9,11,13,15},{16,18,20,22},{17,19,21,2..., use_global_device_ids=true, to_apply=%region_11.12 | all-reduce | flops 1 | bytes 8 | tf_op jit(solution)/shard_map/psum | solution.py:142
  263.0 0.7 multiply_divide_fusion
  263.7 0.7 div.64
  (19 shorter events, 0.3 us)
Async XLA Ops:
  22.5 101.4 %all-to-all-start.1 = ((bf16[32,64,1024]{2,1,0:T(8,128)(2,1)}), bf16[32,64,1024]{2,1,0:T(8,128)(2,1)}, u32[]{:S(2)}, u32[]{:S(2)}) async-start(bf16[32,64,1024]{2,1,0:T(8,128)(2,1)} %bitcast.43), calls=%async_computation.1 | async-start | bytes 8388608 | tf_op jit(solution)/shard_map/all_to_all | solution.py:44
  128.5 6.2 %collective-permute-start = (bf16[512,1152]{1,0:T(8,128)(2,1)S(1)}, bf16[512,1152]{1,0:T(8,128)(2,1)S(1)}, u32[]{:S(2)}, u32[]{:S(2)}) collective-permute-start(bf16[512,1152]{1,0:T(8,128)(2,1)S(1)} %pad_maximum_fusion), channel_id=1, source_target_pairs={{0,1},{1,0},{2,3},{3,2},{4,5},{5,4},{6,7},{7,6},{8,9},{9,8},{10,11... | collective-permute-start | bytes 3538952 | tf_op jit(solution)/shard_map/ppermute | solution.py:66
  136.1 20.5 %all-to-all-start.2 = ((bf16[4,128,1152]{2,1,0:T(8,128)(2,1)}), bf16[4,128,1152]{2,1,0:T(8,128)(2,1)S(1)}, u32[]{:S(2)}, u32[]{:S(2)}) async-start(bf16[4,128,1152]{2,1,0:T(8,128)(2,1)} %bitcast.6), calls=%async_computation.2 | async-start | bytes 2359296 | tf_op jit(solution)/shard_map/all_to_all | solution.py:70
  157.0 19.7 %copy-start.1 = (s32[1024]{0:T(1024)S(1)}, s32[1024]{0:T(1024)}, u32[]{:S(2)}) copy-start(s32[1024]{0:T(1024)} %param.11) | copy-start | bytes 12292
  174.6 4.5 %collective-permute-start.1 = (bf16[512,1024]{1,0:T(8,128)(2,1)S(1)}, bf16[512,1024]{1,0:T(8,128)(2,1)}, u32[]{:S(2)}, u32[]{:S(2)}) collective-permute-start(bf16[512,1024]{1,0:T(8,128)(2,1)S(1)} %bitcast.41), channel_id=1, source_target_pairs={{0,1},{1,0},{2,3},{3,2},{4,5},{5,4},{6,7},{7,6},{8,9},{9,8},{10,11... | collective-permute-start | bytes 3145736 | tf_op jit(solution)/shard_map/ppermute | solution.py:79
  181.3 1.6 copy-start
  203.6 14.0 %all-to-all-start.5 = ((bf16[8,16,1152]{2,1,0:T(8,128)(2,1)}), bf16[8,16,1152]{2,1,0:T(8,128)(2,1)S(1)}, u32[]{:S(2)}, u32[]{:S(2)}) async-start(bf16[8,16,1152]{2,1,0:T(8,128)(2,1)} %pad_maximum_fusion.2), calls=%async_computation.5 | async-start | bytes 589824 | tf_op jit(solution)/shard_map/all_to_all | solution.py:117
  247.5 5.7 %collective-permute-start.2 = (f32[]{:T(128)}, f32[]{:T(128)}, u32[]{:S(2)}, u32[]{:S(2)}) collective-permute-start(f32[]{:T(128)} %fusion.39), channel_id=1, source_target_pairs={{0,1},{1,0},{2,3},{3,2},{4,5},{5,4},{6,7},{7,6},{8,9},{9,8},{10,11... | collective-permute-start | bytes 20 | tf_op jit(solution)/shard_map/ppermute | solution.py:141

commit v10 on v9

--- a/solution.py
+++ b/solution.py
@@ -85,16 +85,20 @@
 
     group_size = level2_old.shape[0]
     group_index = level2_ids - narrow_index * group_size
-    group_table = lax.broadcasted_iota(jnp.int32, (group_size, 1), 0) == group_index[None, :]
-    group_sums = jnp.dot(group_table.astype(jnp.bfloat16), level1_new, preferred_element_type=jnp.float32)
-    group_counts = jnp.dot(
-        group_table.astype(jnp.bfloat16),
-        jnp.ones((group_index.shape[0], 128), jnp.bfloat16),
-        preferred_element_type=jnp.float32,
-    )[:, 0]
-    level1_float = level1_new.astype(jnp.float32)
-    squares = jnp.sum(level1_float * level1_float, axis=1)
-    group_squares = jnp.sum(jnp.where(group_table, squares[None, :], 0.0), axis=1)
+    ones_half = jnp.ones((half_size, 128), jnp.bfloat16)
+
+    def half_stats(half, rows):
+        half_index = lax.dynamic_slice_in_dim(group_index, half * half_size, half_size)
+        table = lax.broadcasted_iota(jnp.int32, (group_size, 1), 0) == half_index[None, :]
+        sums = jnp.dot(table.astype(jnp.bfloat16), rows, preferred_element_type=jnp.float32)
+        counts = jnp.dot(table.astype(jnp.bfloat16), ones_half, preferred_element_type=jnp.float32)[:, 0]
+        rows_float = rows.astype(jnp.float32)
+        squares = jnp.sum(rows_float * rows_float, axis=1)
+        return sums, counts, jnp.sum(jnp.where(table, squares[None, :], 0.0), axis=1)
+
+    own_stats = half_stats(core, half_new)
+    other_stats = half_stats(1 - core, other_half)
+    group_sums, group_counts, group_squares = (a + b for a, b in zip(own_stats, other_stats))
 
     part_size = group_size // wide_count
     z_count = 8

time: 265 us -> 267 us (level)
  blocking collectives: 90.3 us -> 58.8 us
  waiting for transfers between devices: 124 us -> 147 us
  starting transfers between devices: 20.9 us -> 28.2 us
    all_to_all x2 -> x0, blocking collectives: 31.6 us -> none  [the longest x1 16.4 us: local(): lax.all_to_all(sent_sub, 'narrow', 0, 0, axis_index_groups=rings, tiled=T...]
    all_to_all x0 -> x2, waiting for transfers between devices: none -> 23.9 us  [the longest x1 13.8 us: local(): lax.all_to_all(sent_sub, 'narrow', 0, 0, axis_index_groups=rings, tiled=T...]
    all_to_all x0 -> x2, starting transfers between devices: none -> 7.04 us  [the longest x1 3.53 us: local(): lax.all_to_all(sent_x, 'wide', 0, 0, axis_index_groups=x_rings, tiled=True)]
  transfers between devices with their start and end apart: 6 -> 8, of which waited for: 5 -> 7; matrix products, arithmetic and copies ran while one was open for 3% -> 4% of each run, Pallas kernels for 0% -> 0%
where the time goes in v10:
time: 267 us; the launch traced here: 266 us
  waiting for transfers between devices  147 us (55%)
  blocking collectives  58.8 us (22%)
  starting transfers between devices  28.2 us (11%)
  matrix products  12.7 us (5%)
  other arithmetic  11.4 us (4%)
  local copies, waits for them, and re-layouts  5.7 us (2%)
    all_to_all x1, waiting for transfers between devices, local(): lax.all_to_all(block_rows, 'wide', split_axis=0, concat_axis=0, tiled=True)  94.4 us
    all_to_all x1, blocking collectives, local(): lax.all_to_all(sent_ids, 'wide', split_axis=0, concat_axis=0, tiled=True)  20.3 us
    all_to_all x1, blocking collectives, local(): lax.all_to_all(sent_two, 'wide', 0, 0, axis_index_groups=x_rings, tiled=T...  18.7 us
    all_to_all x1, waiting for transfers between devices, local(): lax.all_to_all(sent_one, 'narrow', 0, 0, axis_index_groups=rings, tiled=T...  16.3 us
    all_to_all x1, waiting for transfers between devices, local(): lax.all_to_all(sent_sub, 'narrow', 0, 0, axis_index_groups=rings, tiled=T...  13.8 us
    all_to_all x1, blocking collectives, local(): lax.all_to_all(sent_three, 'wide', 0, 0, axis_index_groups=z_rings, tiled...  12.4 us
    all_to_all x1, waiting for transfers between devices, local(): lax.all_to_all(sent_z, 'wide', 0, 0, axis_index_groups=z_rings, tiled=True)  10.5 us
    all_to_all x1, waiting for transfers between devices, local(): lax.all_to_all(sent_x, 'wide', 0, 0, axis_index_groups=x_rings, tiled=True)  10 us
  transfers between devices with their start and end apart: 8, of which 7 were waited for; matrix products, arithmetic and copies ran while one was open for 4% of the time, Pallas kernels for 0%

profile of v10, /device:TPU:1, one launch (start us, length us, event | category | flops | bytes accessed | tf_op | source)
XLA Modules:
  0.0 265.8 jit_solution(5087402894906645878)
XLA Ops:
  0.6 0.8 reshape.173
  1.4 0.8 compare_select_fusion
  2.2 20.3 %all_to_all.41 = s32[32,1,64]{2,1,0:T(1,128)S(1)} all-to-all(s32[32,1,64]{2,1,0:T(1,128)S(1)} %compare_select_fusion), channel_id=1, replica_groups=mesh['wide'=32,'narrow'=8] {'wide'}, dimensions={0} | all-to-all | bytes 16384 | tf_op jit(solution)/shard_map/all_to_all | solution.py:45
  22.5 4.9 %all-to-all-start.1 = ((bf16[32,64,1024]{2,1,0:T(8,128)(2,1)}), bf16[32,64,1024]{2,1,0:T(8,128)(2,1)}, u32[]{:S(2)}, u32[]{:S(2)}) async-start(bf16[32,64,1024]{2,1,0:T(8,128)(2,1)} %bitcast.46), calls=%async_computation.1 | async-start | bytes 8388608 | tf_op jit(solution)/shard_map/all_to_all | solution.py:44
  27.4 0.1 sub.72
  27.5 0.8 multiply_subtract_fusion.1
  28.3 0.8 multiply_subtract_fusion.2
  29.1 0.3 select_convert_fusion.2
  29.5 94.4 %all-to-all-done.1 = bf16[32,64,1024]{2,1,0:T(8,128)(2,1)} async-done(((bf16[32,64,1024]{2,1,0:T(8,128)(2,1)}), bf16[32,64,1024]{2,1,0:T(8,128)(2,1)}, u32[]{:S(2)}, u32[]{:S(2)}) %all-to-all-start.1) | async-done | bytes 4194336 | tf_op jit(solution)/shard_map/all_to_all | solution.py:44
  123.9 4.6 %fusion.19 = bf16[512,1024]{1,0:T(8,128)(2,1)S(1)} fusion(bf16[2048,1024]{1,0:T(8,128)(2,1)} %bitcast.1, s32[2048]{0:T(1024)S(1)} %sub.72, s32[512]{0:T(512)S(1)} %iota_add_fusion), kind=kOutput, calls=%fused_computation.23 | convolution fusion | flops 2149056512 | bytes 5253120 | tf_op jit(solution)/shard_map/dot_general | solution.py:60
  128.4 0.1 pad_maximum_fusion
  128.5 1.6 collective-permute-start
  130.2 4.5 %fusion.16 = bf16[512,1024]{1,0:T(8,128)(2,1)S(1)} fusion(bf16[2048,1024]{1,0:T(8,128)(2,1)} %bitcast.1, s32[2048]{0:T(1024)S(1)} %sub.72, s32[512]{0:T(512)S(1)} %iota_add_fusion.1), kind=kOutput, calls=%fused_computation.22 | convolution fusion | flops 2149056512 | bytes 5253120 | tf_op jit(solution)/shard_map/dot_general | solution.py:60
  134.7 0.0 collective-permute-done
  134.7 1.3 add_convert_fusion
  136.1 4.2 %all-to-all-start.2 = ((bf16[4,128,1152]{2,1,0:T(8,128)(2,1)}), bf16[4,128,1152]{2,1,0:T(8,128)(2,1)S(1)}, u32[]{:S(2)}, u32[]{:S(2)}) async-start(bf16[4,128,1152]{2,1,0:T(8,128)(2,1)} %bitcast.6), calls=%async_computation.2 | async-start | bytes 2359296 | tf_op jit(solution)/shard_map/all_to_all | solution.py:70
  140.3 16.3 %all-to-all-done.2 = bf16[4,128,1152]{2,1,0:T(8,128)(2,1)S(1)} async-done(((bf16[4,128,1152]{2,1,0:T(8,128)(2,1)}), bf16[4,128,1152]{2,1,0:T(8,128)(2,1)S(1)}, u32[]{:S(2)}, u32[]{:S(2)}) %all-to-all-start.2) | async-done | bytes 1179680 | tf_op jit(solution)/shard_map/all_to_all | solution.py:70
  156.6 0.2 fusion.32
  156.8 0.1 convert_reduce_fusion
  157.0 0.0 copy-start
  157.0 1.1 divide_convert_fusion
  158.1 1.1 broadcast_in_dim.203
  159.2 3.5 %all-to-all-start.3 = ((bf16[4,128,1024]{2,1,0:T(8,128)(2,1)}), bf16[4,128,1024]{2,1,0:T(8,128)(2,1)S(1)}, u32[]{:S(2)}, u32[]{:S(2)}) async-start(bf16[4,128,1024]{2,1,0:T(8,128)(2,1)} %broadcast_in_dim.203), calls=%async_computation.3 | async-start | bytes 2097152 | tf_op jit(solution)/shard_map/all_to_all | solution.py:78
  162.7 0.1 fusion.45
  162.8 13.8 %all-to-all-done.3 = bf16[4,128,1024]{2,1,0:T(8,128)(2,1)S(1)} async-done(((bf16[4,128,1024]{2,1,0:T(8,128)(2,1)}), bf16[4,128,1024]{2,1,0:T(8,128)(2,1)S(1)}, u32[]{:S(2)}, u32[]{:S(2)}) %all-to-all-start.3) | async-done | bytes 1048608 | tf_op jit(solution)/shard_map/all_to_all | solution.py:78
  176.7 2.0 collective-permute-start.1
  178.7 0.3 fusion.22
  179.0 0.3 multiply_subtract_fusion
  179.3 0.3 multiply_reduce_fusion.1
  179.6 0.2 select_reduce_fusion.1
  179.7 0.7 fusion.23
  180.5 0.5 collective-permute-done.1
  181.0 0.3 multiply_reduce_fusion
  181.3 0.2 select_reduce_fusion
  181.5 0.3 select_convert_fusion
  181.8 0.7 add_convert_fusion.1
  182.6 0.1 pad_maximum_fusion.1
  182.7 18.7 %all_to_all.42 = bf16[4,128,1152]{2,1,0:T(8,128)(2,1)S(1)} all-to-all(bf16[4,128,1152]{2,1,0:T(8,128)(2,1)S(1)} %bitcast.45), channel_id=1, replica_groups={{0,64,128,192},{8,72,136,200},{16,80,144,208},{24,88,152,216},{32,96,16..., dimensions={0} | all-to-all | bytes 2359296 | tf_op jit(solution)/shard_map/all_to_all | solution.py:112
  201.4 0.2 subtract_reduce_fusion
  201.6 0.1 broadcast_in_dim.215
  201.7 0.1 reshape.181
  201.8 0.1 broadcast_in_dim.217
  201.9 0.1 broadcast_in_dim.222
  202.0 0.2 select_convert_fusion.3
  202.1 0.1 slice_reduce_fusion
  202.3 0.7 pad_maximum_fusion.2
  203.0 3.4 %all-to-all-start.5 = ((bf16[8,16,1152]{2,1,0:T(8,128)(2,1)}), bf16[8,16,1152]{2,1,0:T(8,128)(2,1)S(1)}, u32[]{:S(2)}, u32[]{:S(2)}) async-start(bf16[8,16,1152]{2,1,0:T(8,128)(2,1)} %pad_maximum_fusion.2), calls=%async_computation.5 | async-start | bytes 589824 | tf_op jit(solution)/shard_map/all_to_all | solution.py:121
  206.5 10.5 %all-to-all-done.5 = bf16[8,16,1152]{2,1,0:T(8,128)(2,1)S(1)} async-done(((bf16[8,16,1152]{2,1,0:T(8,128)(2,1)}), bf16[8,16,1152]{2,1,0:T(8,128)(2,1)S(1)}, u32[]{:S(2)}, u32[]{:S(2)}) %all-to-all-start.5) | async-done | bytes 294944 | tf_op jit(solution)/shard_map/all_to_all | solution.py:121
  217.0 0.1 copy.22
  217.2 1.0 multiply_reduce_fusion.3
  218.2 0.1 select_convert_fusion.4
  218.3 12.4 %all_to_all.43 = bf16[8,16,1152]{2,1,0:T(8,128)(2,1)S(1)} all-to-all(bf16[8,16,1152]{2,1,0:T(8,128)(2,1)S(1)} %broadcast_in_dim.233), channel_id=1, replica_groups={{0,8,16,24,32,40,48,56},{64,72,80,88,96,104,112,120},{128,136,144,152,1..., dimensions={0} | all-to-all | bytes 589824 | tf_op jit(solution)/shard_map/all_to_all | solution.py:137
  230.7 1.1 broadcast_in_dim.234
  231.8 3.5 %all-to-all-start.7 = ((bf16[4,8,16,1152]{3,2,1,0:T(8,128)(2,1)}), bf16[4,8,16,1152]{3,2,1,0:T(8,128)(2,1)S(1)}, u32[]{:S(2)}, u32[]{:S(2)}) async-start(bf16[4,8,16,1152]{3,2,1,0:T(8,128)(2,1)} %broadcast_in_dim.234), calls=%async_computation.7 | async-start | bytes 2359296 | tf_op jit(solution)/shard_map/all_to_all | solution.py:139
  235.4 2.3 maximum_select_fusion
  237.7 10.0 %all-to-all-done.7 = bf16[4,8,16,1152]{3,2,1,0:T(8,128)(2,1)S(1)} async-done(((bf16[4,8,16,1152]{3,2,1,0:T(8,128)(2,1)}), bf16[4,8,16,1152]{3,2,1,0:T(8,128)(2,1)S(1)}, u32[]{:S(2)}, u32[]{:S(2)}) %all-to-all-start.7) | async-done | bytes 1179680 | tf_op jit(solution)/shard_map/all_to_all | solution.py:139
  247.8 0.3 copy.23
  248.1 0.6 fusion.42
  248.7 5.0 %collective-permute-start.2 = (f32[]{:T(128)}, f32[]{:T(128)}, u32[]{:S(2)}, u32[]{:S(2)}) collective-permute-start(f32[]{:T(128)} %fusion.42), channel_id=1, source_target_pairs={{0,1},{1,0},{2,3},{3,2},{4,5},{5,4},{6,7},{7,6},{8,9},{9,8},{10,11... | collective-permute-start | bytes 20 | tf_op jit(solution)/shard_map/ppermute | solution.py:145
  253.7 1.0 collective-permute-done.2
  256.0 1.1 slice.120
  257.1 7.4 %psum.7 = f32[]{:T(128)} all-reduce(f32[]{:T(128)S(6)} %add.157), channel_id=1, replica_groups={{0,2,4,6},{1,3,5,7},{8,10,12,14},{9,11,13,15},{16,18,20,22},{17,19,21,2..., use_global_device_ids=true, to_apply=%region_13.14 | all-reduce | flops 1 | bytes 8 | tf_op jit(solution)/shard_map/psum | solution.py:146
  264.5 0.7 multiply_divide_fusion
  265.1 0.7 div.64
  (20 shorter events, 0.3 us)
Async XLA Ops:
  22.5 101.4 %all-to-all-start.1 = ((bf16[32,64,1024]{2,1,0:T(8,128)(2,1)}), bf16[32,64,1024]{2,1,0:T(8,128)(2,1)}, u32[]{:S(2)}, u32[]{:S(2)}) async-start(bf16[32,64,1024]{2,1,0:T(8,128)(2,1)} %bitcast.46), calls=%async_computation.1 | async-start | bytes 8388608 | tf_op jit(solution)/shard_map/all_to_all | solution.py:44
  128.5 6.2 %collective-permute-start = (bf16[512,1152]{1,0:T(8,128)(2,1)S(1)}, bf16[512,1152]{1,0:T(8,128)(2,1)S(1)}, u32[]{:S(2)}, u32[]{:S(2)}) collective-permute-start(bf16[512,1152]{1,0:T(8,128)(2,1)S(1)} %pad_maximum_fusion), channel_id=1, source_target_pairs={{0,1},{1,0},{2,3},{3,2},{4,5},{5,4},{6,7},{7,6},{8,9},{9,8},{10,11... | collective-permute-start | bytes 3538952 | tf_op jit(solution)/shard_map/ppermute | solution.py:66
  136.1 20.5 %all-to-all-start.2 = ((bf16[4,128,1152]{2,1,0:T(8,128)(2,1)}), bf16[4,128,1152]{2,1,0:T(8,128)(2,1)S(1)}, u32[]{:S(2)}, u32[]{:S(2)}) async-start(bf16[4,128,1152]{2,1,0:T(8,128)(2,1)} %bitcast.6), calls=%async_computation.2 | async-start | bytes 2359296 | tf_op jit(solution)/shard_map/all_to_all | solution.py:70
  157.0 5.7 %copy-start = (s32[1024]{0:T(1024)S(1)}, s32[1024]{0:T(1024)}, u32[]{:S(2)}) copy-start(s32[1024]{0:T(1024)} %param.11) | copy-start | bytes 12292
  159.2 17.5 %all-to-all-start.3 = ((bf16[4,128,1024]{2,1,0:T(8,128)(2,1)}), bf16[4,128,1024]{2,1,0:T(8,128)(2,1)S(1)}, u32[]{:S(2)}, u32[]{:S(2)}) async-start(bf16[4,128,1024]{2,1,0:T(8,128)(2,1)} %broadcast_in_dim.203), calls=%async_computation.3 | async-start | bytes 2097152 | tf_op jit(solution)/shard_map/all_to_all | solution.py:78
  176.7 4.3 %collective-permute-start.1 = (bf16[512,1024]{1,0:T(8,128)(2,1)S(1)}, bf16[512,1024]{1,0:T(8,128)(2,1)S(1)}, u32[]{:S(2)}, u32[]{:S(2)}) collective-permute-start(bf16[512,1024]{1,0:T(8,128)(2,1)S(1)} %bitcast.40), channel_id=1, source_target_pairs={{0,1},{1,0},{2,3},{3,2},{4,5},{5,4},{6,7},{7,6},{8,9},{9,8},{10,11... | collective-permute-start | bytes 3145736 | tf_op jit(solution)/shard_map/ppermute | solution.py:79
  203.0 14.0 %all-to-all-start.5 = ((bf16[8,16,1152]{2,1,0:T(8,128)(2,1)}), bf16[8,16,1152]{2,1,0:T(8,128)(2,1)S(1)}, u32[]{:S(2)}, u32[]{:S(2)}) async-start(bf16[8,16,1152]{2,1,0:T(8,128)(2,1)} %pad_maximum_fusion.2), calls=%async_computation.5 | async-start | bytes 589824 | tf_op jit(solution)/shard_map/all_to_all | solution.py:121
  231.8 15.9 %all-to-all-start.7 = ((bf16[4,8,16,1152]{3,2,1,0:T(8,128)(2,1)}), bf16[4,8,16,1152]{3,2,1,0:T(8,128)(2,1)S(1)}, u32[]{:S(2)}, u32[]{:S(2)}) async-start(bf16[4,8,16,1152]{3,2,1,0:T(8,128)(2,1)} %broadcast_in_dim.234), calls=%async_computation.7 | async-start | bytes 2359296 | tf_op jit(solution)/shard_map/all_to_all | solution.py:139
  248.7 6.0 %collective-permute-start.2 = (f32[]{:T(128)}, f32[]{:T(128)}, u32[]{:S(2)}, u32[]{:S(2)}) collective-permute-start(f32[]{:T(128)} %fusion.42), channel_id=1, source_target_pairs={{0,1},{1,0},{2,3},{3,2},{4,5},{5,4},{6,7},{7,6},{8,9},{9,8},{10,11... | collective-permute-start | bytes 20 | tf_op jit(solution)/shard_map/ppermute | solution.py:145

commit v11 on v9

--- a/solution.py
+++ b/solution.py
@@ -42,7 +42,13 @@
     live_slots = position < block_counts[:, None]
     sent_ids = jnp.where(live_slots, level1_ids.reshape(wide_count, slot_count), -1)
     got_rows = lax.all_to_all(block_rows, "wide", split_axis=0, concat_axis=0, tiled=True)
-    got_ids = lax.all_to_all(sent_ids, "wide", split_axis=0, concat_axis=0, tiled=True)
+    id_z = 8
+    id_x = wide_count // id_z
+    ids_x_rings = [[z + id_z * x for x in range(id_x)] for z in range(id_z)]
+    ids_z_rings = [[z + id_z * x for z in range(id_z)] for x in range(id_x)]
+    ids_by_x = lax.all_to_all(sent_ids.reshape(id_x, id_z, slot_count), "wide", 0, 0, axis_index_groups=ids_x_rings, tiled=True)
+    ids_by_z = lax.all_to_all(ids_by_x.transpose(1, 0, 2), "wide", 0, 0, axis_index_groups=ids_z_rings, tiled=True)
+    got_ids = ids_by_z.transpose(1, 0, 2).reshape(wide_count, slot_count)
 
     owner_index = got_ids.reshape(-1) - owner_base
     core_count = 2

time: 265 us -> 270 us (1.019)
  waiting for transfers between devices: 124 us -> 119 us
  starting transfers between devices: 20.9 us -> 25.8 us
  blocking collectives: 90.3 us -> 93.7 us
    all_to_all x1, waiting for transfers between devices: 94.4 us -> 88.7 us  [local(): lax.all_to_all(block_rows, 'wide', split_axis=0, concat_axis=0, tiled=True)]
    ppermute x1, starting transfers between devices: 1.64 us -> 6.62 us  [local(): given_back = lax.ppermute(half_packed(1 - core), 'narrow', partner)]
    all_to_all x1 -> x2, blocking collectives: 20.3 us -> 23.3 us  [the longest x1 14.5 us: local(): lax.all_to_all(ids_by_x.transpose(1, 0, 2), 'wide', 0, 0, axis_index_grou...]
where the time goes in v11:
time: 270 us; the launch traced here: 269 us
  waiting for transfers between devices  119 us (44%)
  blocking collectives  93.7 us (35%)
  starting transfers between devices  25.8 us (10%)
  matrix products  12.4 us (5%)
  other arithmetic  11.2 us (4%)
  local copies, waits for them, and re-layouts  5.21 us (2%)
    all_to_all x1, waiting for transfers between devices, local(): lax.all_to_all(block_rows, 'wide', split_axis=0, concat_axis=0, tiled=True)  88.7 us
    all_to_all x1, blocking collectives, local(): lax.all_to_all(sent_two, 'wide', 0, 0, axis_index_groups=x_rings, tiled=T...  18.7 us
    all_to_all x1, blocking collectives, local(): lax.all_to_all(sent_sub, 'narrow', 0, 0, axis_index_groups=rings, tiled=T...  16.4 us
    all_to_all x1, waiting for transfers between devices, local(): lax.all_to_all(sent_one, 'narrow', 0, 0, axis_index_groups=rings, tiled=T...  16.3 us
    all_to_all x1, blocking collectives, local(): lax.all_to_all(sent_x, 'wide', 0, 0, axis_index_groups=x_rings, tiled=True)  15.2 us
    all_to_all x1, blocking collectives, local(): lax.all_to_all(ids_by_x.transpose(1, 0, 2), 'wide', 0, 0, axis_index_grou...  14.5 us
    all_to_all x1, blocking collectives, local(): lax.all_to_all(sent_three, 'wide', 0, 0, axis_index_groups=z_rings, tiled...  12.6 us
    all_to_all x1, waiting for transfers between devices, local(): lax.all_to_all(sent_z, 'wide', 0, 0, axis_index_groups=z_rings, tiled=True)  10.6 us
  transfers between devices with their start and end apart: 6, of which 5 were waited for; matrix products, arithmetic and copies ran while one was open for 3% of the time, Pallas kernels for 0%

profile of v11, /device:TPU:1, one launch (start us, length us, event | category | flops | bytes accessed | tf_op | source)
XLA Modules:
  0.0 269.1 jit_solution(2751727573039647111)
XLA Ops:
  0.6 0.7 lt.25
  1.4 0.8 reshape.134
  2.1 0.1 fusion.34
  2.2 0.1 reshape.149
  2.3 8.8 %all_to_all.45 = s32[4,1,512]{2,1,0:T(1,128)S(1)} all-to-all(s32[4,1,512]{2,1,0:T(1,128)S(1)} %reshape.149), channel_id=1, replica_groups={{0,64,128,192},{8,72,136,200},{16,80,144,208},{24,88,152,216},{32,96,16..., dimensions={0} | all-to-all | bytes 16384 | tf_op jit(solution)/shard_map/all_to_all | solution.py:49
  11.1 0.5 broadcast.213
  11.6 0.7 reduce.12
  12.3 0.1 reshape.150
  12.4 0.1 reshape.151
  12.5 14.5 %all_to_all.46 = s32[8,1,256]{2,1,0:T(1,128)S(1)} all-to-all(s32[8,1,256]{2,1,0:T(1,128)S(1)} %reshape.151), channel_id=1, replica_groups={{0,8,16,24,32,40,48,56},{64,72,80,88,96,104,112,120},{128,136,144,152,1..., dimensions={0} | all-to-all | bytes 16384 | tf_op jit(solution)/shard_map/all_to_all | solution.py:50
  27.0 4.9 %all-to-all-start.2 = ((bf16[32,64,1024]{2,1,0:T(8,128)(2,1)}), bf16[32,64,1024]{2,1,0:T(8,128)(2,1)}, u32[]{:S(2)}, u32[]{:S(2)}) async-start(bf16[32,64,1024]{2,1,0:T(8,128)(2,1)} %bitcast.46), calls=%async_computation.2 | async-start | bytes 8388608 | tf_op jit(solution)/shard_map/all_to_all | solution.py:44
  31.9 0.7 reduce.13
  32.6 0.1 reshape.152
  32.7 0.1 sub.75
  32.8 0.8 multiply_subtract_fusion.1
  33.6 0.8 multiply_subtract_fusion.2
  34.4 0.3 select_convert_fusion.2
  34.7 88.7 %all-to-all-done.2 = bf16[32,64,1024]{2,1,0:T(8,128)(2,1)} async-done(((bf16[32,64,1024]{2,1,0:T(8,128)(2,1)}), bf16[32,64,1024]{2,1,0:T(8,128)(2,1)}, u32[]{:S(2)}, u32[]{:S(2)}) %all-to-all-start.2) | async-done | bytes 4194336 | tf_op jit(solution)/shard_map/all_to_all | solution.py:44
  123.4 4.6 %fusion.22 = bf16[512,1024]{1,0:T(8,128)(2,1)S(1)} fusion(bf16[2048,1024]{1,0:T(8,128)(2,1)} %bitcast.3, s32[2048]{0:T(1024)S(1)} %sub.75, s32[512]{0:T(512)S(1)} %iota_add_fusion), kind=kOutput, calls=%fused_computation.26 | convolution fusion | flops 2149056512 | bytes 5253120 | tf_op jit(solution)/shard_map/dot_general | solution.py:66
  127.9 0.1 pad_maximum_fusion
  128.0 6.6 %collective-permute-start = (bf16[512,1152]{1,0:T(8,128)(2,1)S(1)}, bf16[512,1152]{1,0:T(8,128)(2,1)S(1)}, u32[]{:S(2)}, u32[]{:S(2)}) collective-permute-start(bf16[512,1152]{1,0:T(8,128)(2,1)S(1)} %pad_maximum_fusion), channel_id=1, source_target_pairs={{0,1},{1,0},{2,3},{3,2},{4,5},{5,4},{6,7},{7,6},{8,9},{9,8},{10,11... | collective-permute-start | bytes 3538952 | tf_op jit(solution)/shard_map/ppermute | solution.py:72
  134.7 4.6 %fusion.19 = bf16[512,1024]{1,0:T(8,128)(2,1)S(1)} fusion(bf16[2048,1024]{1,0:T(8,128)(2,1)} %bitcast.3, s32[2048]{0:T(1024)S(1)} %sub.75, s32[512]{0:T(512)S(1)} %iota_add_fusion.1), kind=kOutput, calls=%fused_computation.25 | convolution fusion | flops 2149056512 | bytes 5253120 | tf_op jit(solution)/shard_map/dot_general | solution.py:66
  139.2 1.3 add_convert_fusion
  140.6 4.2 %all-to-all-start.3 = ((bf16[4,128,1152]{2,1,0:T(8,128)(2,1)}), bf16[4,128,1152]{2,1,0:T(8,128)(2,1)S(1)}, u32[]{:S(2)}, u32[]{:S(2)}) async-start(bf16[4,128,1152]{2,1,0:T(8,128)(2,1)} %bitcast.8), calls=%async_computation.3 | async-start | bytes 2359296 | tf_op jit(solution)/shard_map/all_to_all | solution.py:76
  144.8 16.3 %all-to-all-done.3 = bf16[4,128,1152]{2,1,0:T(8,128)(2,1)S(1)} async-done(((bf16[4,128,1152]{2,1,0:T(8,128)(2,1)}), bf16[4,128,1152]{2,1,0:T(8,128)(2,1)S(1)}, u32[]{:S(2)}, u32[]{:S(2)}) %all-to-all-start.3) | async-done | bytes 1179680 | tf_op jit(solution)/shard_map/all_to_all | solution.py:76
  161.1 0.2 fusion.32
  161.3 0.1 convert_reduce_fusion
  161.5 0.0 copy-start.1
  161.5 1.1 divide_convert_fusion
  162.5 0.1 broadcast_in_dim.193
  162.7 16.4 %all_to_all.47 = bf16[4,128,1024]{2,1,0:T(8,128)(2,1)S(1)} all-to-all(bf16[4,128,1024]{2,1,0:T(8,128)(2,1)S(1)} %broadcast_in_dim.193), channel_id=1, replica_groups={{0,2,4,6},{1,3,5,7},{8,10,12,14},{9,11,13,15},{16,18,20,22},{17,19,21,2..., dimensions={0} | all-to-all | bytes 2097152 | tf_op jit(solution)/shard_map/all_to_all | solution.py:84
  179.1 2.0 collective-permute-start.1
  181.2 0.5 multiply_subtract_fusion
  181.6 1.9 collective-permute-done.1
  183.6 2.2 multiply_reduce_fusion
  185.7 0.3 select_reduce_fusion
  186.1 1.2 fusion.18
  187.3 0.3 select_convert_fusion
  187.7 0.1 pad_maximum_fusion.1
  187.8 18.7 %all_to_all.48 = bf16[4,128,1152]{2,1,0:T(8,128)(2,1)S(1)} all-to-all(bf16[4,128,1152]{2,1,0:T(8,128)(2,1)S(1)} %bitcast.43), channel_id=1, replica_groups={{0,64,128,192},{8,72,136,200},{16,80,144,208},{24,88,152,216},{32,96,16..., dimensions={0} | all-to-all | bytes 2359296 | tf_op jit(solution)/shard_map/all_to_all | solution.py:114
  206.5 0.2 subtract_reduce_fusion
  206.7 0.1 broadcast_in_dim.203
  206.8 0.1 reshape.142
  206.9 0.1 broadcast_in_dim.205
  207.0 0.1 broadcast_in_dim.210
  207.0 0.2 select_convert_fusion.3
  207.2 0.1 slice_reduce_fusion
  207.4 0.7 pad_maximum_fusion.2
  208.1 3.4 %all-to-all-start.6 = ((bf16[8,16,1152]{2,1,0:T(8,128)(2,1)}), bf16[8,16,1152]{2,1,0:T(8,128)(2,1)S(1)}, u32[]{:S(2)}, u32[]{:S(2)}) async-start(bf16[8,16,1152]{2,1,0:T(8,128)(2,1)} %pad_maximum_fusion.2), calls=%async_computation.6 | async-start | bytes 589824 | tf_op jit(solution)/shard_map/all_to_all | solution.py:123
  211.5 10.6 %all-to-all-done.6 = bf16[8,16,1152]{2,1,0:T(8,128)(2,1)S(1)} async-done(((bf16[8,16,1152]{2,1,0:T(8,128)(2,1)}), bf16[8,16,1152]{2,1,0:T(8,128)(2,1)S(1)}, u32[]{:S(2)}, u32[]{:S(2)}) %all-to-all-start.6) | async-done | bytes 294944 | tf_op jit(solution)/shard_map/all_to_all | solution.py:123
  222.1 0.1 copy.33
  222.4 1.0 multiply_reduce_fusion.2
  223.3 0.1 select_convert_fusion.4
  223.5 12.6 %all_to_all.49 = bf16[8,16,1152]{2,1,0:T(8,128)(2,1)S(1)} all-to-all(bf16[8,16,1152]{2,1,0:T(8,128)(2,1)S(1)} %broadcast_in_dim.221), channel_id=1, replica_groups={{0,8,16,24,32,40,48,56},{64,72,80,88,96,104,112,120},{128,136,144,152,1..., dimensions={0} | all-to-all | bytes 589824 | tf_op jit(solution)/shard_map/all_to_all | solution.py:139
  236.1 0.1 broadcast_in_dim.222
  236.2 15.2 %all_to_all.50 = bf16[4,8,16,1152]{3,2,1,0:T(8,128)(2,1)S(1)} all-to-all(bf16[4,8,16,1152]{3,2,1,0:T(8,128)(2,1)S(1)} %broadcast_in_dim.222), channel_id=1, replica_groups={{0,64,128,192},{8,72,136,200},{16,80,144,208},{24,88,152,216},{32,96,16..., dimensions={0} | all-to-all | bytes 2359296 | tf_op jit(solution)/shard_map/all_to_all | solution.py:141
  251.4 0.3 copy.34
  251.7 0.6 fusion.40
  252.3 4.7 %collective-permute-start.2 = (f32[]{:T(128)}, f32[]{:T(128)}, u32[]{:S(2)}, u32[]{:S(2)}) collective-permute-start(f32[]{:T(128)} %fusion.40), channel_id=1, source_target_pairs={{0,1},{1,0},{2,3},{3,2},{4,5},{5,4},{6,7},{7,6},{8,9},{9,8},{10,11... | collective-permute-start | bytes 20 | tf_op jit(solution)/shard_map/ppermute | solution.py:147
  257.0 1.0 collective-permute-done.2
  259.3 1.1 slice.114
  260.4 7.4 %psum.7 = f32[]{:T(128)} all-reduce(f32[]{:T(128)S(6)} %add.128), channel_id=1, replica_groups={{0,2,4,6},{1,3,5,7},{8,10,12,14},{9,11,13,15},{16,18,20,22},{17,19,21,2..., use_global_device_ids=true, to_apply=%region_11.12 | all-reduce | flops 1 | bytes 8 | tf_op jit(solution)/shard_map/psum | solution.py:148
  267.8 0.7 multiply_divide_fusion
  268.4 0.7 div.64
  (25 shorter events, 0.3 us)
Async XLA Ops:
  27.0 96.4 %all-to-all-start.2 = ((bf16[32,64,1024]{2,1,0:T(8,128)(2,1)}), bf16[32,64,1024]{2,1,0:T(8,128)(2,1)}, u32[]{:S(2)}, u32[]{:S(2)}) async-start(bf16[32,64,1024]{2,1,0:T(8,128)(2,1)} %bitcast.46), calls=%async_computation.2 | async-start | bytes 8388608 | tf_op jit(solution)/shard_map/all_to_all | solution.py:44
  128.0 11.2 %collective-permute-start = (bf16[512,1152]{1,0:T(8,128)(2,1)S(1)}, bf16[512,1152]{1,0:T(8,128)(2,1)S(1)}, u32[]{:S(2)}, u32[]{:S(2)}) collective-permute-start(bf16[512,1152]{1,0:T(8,128)(2,1)S(1)} %pad_maximum_fusion), channel_id=1, source_target_pairs={{0,1},{1,0},{2,3},{3,2},{4,5},{5,4},{6,7},{7,6},{8,9},{9,8},{10,11... | collective-permute-start | bytes 3538952 | tf_op jit(solution)/shard_map/ppermute | solution.py:72
  140.6 20.5 %all-to-all-start.3 = ((bf16[4,128,1152]{2,1,0:T(8,128)(2,1)}), bf16[4,128,1152]{2,1,0:T(8,128)(2,1)S(1)}, u32[]{:S(2)}, u32[]{:S(2)}) async-start(bf16[4,128,1152]{2,1,0:T(8,128)(2,1)} %bitcast.8), calls=%async_computation.3 | async-start | bytes 2359296 | tf_op jit(solution)/shard_map/all_to_all | solution.py:76
  161.5 19.7 %copy-start.1 = (s32[1024]{0:T(1024)S(1)}, s32[1024]{0:T(1024)}, u32[]{:S(2)}) copy-start(s32[1024]{0:T(1024)} %param.11) | copy-start | bytes 12292
  179.1 4.5 %collective-permute-start.1 = (bf16[512,1024]{1,0:T(8,128)(2,1)S(1)}, bf16[512,1024]{1,0:T(8,128)(2,1)}, u32[]{:S(2)}, u32[]{:S(2)}) collective-permute-start(bf16[512,1024]{1,0:T(8,128)(2,1)S(1)} %bitcast.44), channel_id=1, source_target_pairs={{0,1},{1,0},{2,3},{3,2},{4,5},{5,4},{6,7},{7,6},{8,9},{9,8},{10,11... | collective-permute-start | bytes 3145736 | tf_op jit(solution)/shard_map/ppermute | solution.py:85
  185.7 1.6 copy-start
  208.1 14.0 %all-to-all-start.6 = ((bf16[8,16,1152]{2,1,0:T(8,128)(2,1)}), bf16[8,16,1152]{2,1,0:T(8,128)(2,1)S(1)}, u32[]{:S(2)}, u32[]{:S(2)}) async-start(bf16[8,16,1152]{2,1,0:T(8,128)(2,1)} %pad_maximum_fusion.2), calls=%async_computation.6 | async-start | bytes 589824 | tf_op jit(solution)/shard_map/all_to_all | solution.py:123
  252.3 5.6 %collective-permute-start.2 = (f32[]{:T(128)}, f32[]{:T(128)}, u32[]{:S(2)}, u32[]{:S(2)}) collective-permute-start(f32[]{:T(128)} %fusion.40), channel_id=1, source_target_pairs={{0,1},{1,0},{2,3},{3,2},{4,5},{5,4},{6,7},{7,6},{8,9},{9,8},{10,11... | collective-permute-start | bytes 20 | tf_op jit(solution)/shard_map/ppermute | solution.py:147

commit v12 on v9

--- a/solution.py
+++ b/solution.py
@@ -139,7 +139,10 @@
     inertia_all = ((tail_three[:, :, 0] + tail_three[:, :, 1]) + tail_three[:, :, 2]).reshape(group_size)
     inertia_part = jnp.sum(inertia_all)
     inertia_chip = inertia_part + lax.ppermute(inertia_part, "narrow", partner)
-    inertia_sum = lax.psum(inertia_chip, "narrow", axis_index_groups=rings)
+    inertia_sum = inertia_chip
+    for step in range(1, chip_count.bit_length() - 1 + 1):
+        mask = core_count << (step - 1)
+        inertia_sum = inertia_sum + lax.ppermute(inertia_sum, "narrow", [(i, i ^ mask) for i in range(narrow_count)])
     centroid_total = float(group_size * narrow_count)
     split_weights = centroid_total * inertia_all / inertia_sum
     return (level1_new, level2_new, split_weights)

time: 265 us -> 265 us (level)
  blocking collectives: 90.3 us -> 83 us
  waiting for transfers between devices: 124 us -> 128 us
    psum x1 -> x0, blocking collectives: 7.39 us -> none  [local(): inertia_sum = lax.psum(inertia_chip, 'narrow', axis_index_groups=rings)]
    ppermute x0 -> x2, waiting for transfers between devices: none -> 4.19 us  [local(): lax.ppermute(inertia_sum, 'narrow', [(i, i ^ mask) for i in range(narrow_...]
  transfers between devices with their start and end apart: 6 -> 8, of which waited for: 5 -> 7; matrix products, arithmetic and copies ran while one was open for 3% -> 3% of each run, Pallas kernels for 0% -> 0%
where the time goes in v12:
time: 265 us; the launch traced here: 264 us
  waiting for transfers between devices  128 us (48%)
  blocking collectives  83 us (31%)
  starting transfers between devices  23.4 us (9%)
  matrix products  12.4 us (5%)
  other arithmetic  9.98 us (4%)
  between operations  3.66 us (1%)
  local copies, waits for them, and re-layouts  3.63 us (1%)
    all_to_all x1, waiting for transfers between devices, local(): lax.all_to_all(block_rows, 'wide', split_axis=0, concat_axis=0, tiled=True)  94.4 us
    all_to_all x1, blocking collectives, local(): lax.all_to_all(sent_ids, 'wide', split_axis=0, concat_axis=0, tiled=True)  20.3 us
    all_to_all x1, blocking collectives, local(): lax.all_to_all(sent_two, 'wide', 0, 0, axis_index_groups=x_rings, tiled=T...  18.7 us
    all_to_all x1, blocking collectives, local(): lax.all_to_all(sent_sub, 'narrow', 0, 0, axis_index_groups=rings, tiled=T...  16.4 us
    all_to_all x1, waiting for transfers between devices, local(): lax.all_to_all(sent_one, 'narrow', 0, 0, axis_index_groups=rings, tiled=T...  16.3 us
    all_to_all x1, blocking collectives, local(): lax.all_to_all(sent_x, 'wide', 0, 0, axis_index_groups=x_rings, tiled=True)  15.1 us
    all_to_all x1, blocking collectives, local(): lax.all_to_all(sent_three, 'wide', 0, 0, axis_index_groups=z_rings, tiled...  12.4 us
    all_to_all x1, waiting for transfers between devices, local(): lax.all_to_all(sent_z, 'wide', 0, 0, axis_index_groups=z_rings, tiled=True)  10.5 us
  transfers between devices with their start and end apart: 8, of which 7 were waited for; matrix products, arithmetic and copies ran while one was open for 3% of the time, Pallas kernels for 0%

profile of v12, /device:TPU:1, one launch (start us, length us, event | category | flops | bytes accessed | tf_op | source)
XLA Modules:
  0.0 264.4 jit_solution(11715332283583750623)
XLA Ops:
  0.6 0.8 reshape.164
  1.4 0.8 compare_select_fusion
  2.2 20.3 %all_to_all.41 = s32[32,1,64]{2,1,0:T(1,128)S(1)} all-to-all(s32[32,1,64]{2,1,0:T(1,128)S(1)} %compare_select_fusion), channel_id=1, replica_groups=mesh['wide'=32,'narrow'=8] {'wide'}, dimensions={0} | all-to-all | bytes 16384 | tf_op jit(solution)/shard_map/all_to_all | solution.py:45
  22.5 4.9 %all-to-all-start.1 = ((bf16[32,64,1024]{2,1,0:T(8,128)(2,1)}), bf16[32,64,1024]{2,1,0:T(8,128)(2,1)}, u32[]{:S(2)}, u32[]{:S(2)}) async-start(bf16[32,64,1024]{2,1,0:T(8,128)(2,1)} %bitcast.43), calls=%async_computation.1 | async-start | bytes 8388608 | tf_op jit(solution)/shard_map/all_to_all | solution.py:44
  27.4 0.1 sub.71
  27.5 0.8 multiply_subtract_fusion.1
  28.3 0.8 multiply_subtract_fusion.2
  29.1 0.3 select_convert_fusion.2
  29.5 94.4 %all-to-all-done.1 = bf16[32,64,1024]{2,1,0:T(8,128)(2,1)} async-done(((bf16[32,64,1024]{2,1,0:T(8,128)(2,1)}), bf16[32,64,1024]{2,1,0:T(8,128)(2,1)}, u32[]{:S(2)}, u32[]{:S(2)}) %all-to-all-start.1) | async-done | bytes 4194336 | tf_op jit(solution)/shard_map/all_to_all | solution.py:44
  123.9 4.6 %fusion.22 = bf16[512,1024]{1,0:T(8,128)(2,1)S(1)} fusion(bf16[2048,1024]{1,0:T(8,128)(2,1)} %bitcast.1, s32[2048]{0:T(1024)S(1)} %sub.71, s32[512]{0:T(512)S(1)} %iota_add_fusion), kind=kOutput, calls=%fused_computation.26 | convolution fusion | flops 2149056512 | bytes 5253120 | tf_op jit(solution)/shard_map/dot_general | solution.py:60
  128.4 0.1 pad_maximum_fusion
  128.5 1.6 collective-permute-start
  130.2 4.6 %fusion.19 = bf16[512,1024]{1,0:T(8,128)(2,1)S(1)} fusion(bf16[2048,1024]{1,0:T(8,128)(2,1)} %bitcast.1, s32[2048]{0:T(1024)S(1)} %sub.71, s32[512]{0:T(512)S(1)} %iota_add_fusion.1), kind=kOutput, calls=%fused_computation.25 | convolution fusion | flops 2149056512 | bytes 5253120 | tf_op jit(solution)/shard_map/dot_general | solution.py:60
  134.7 0.0 collective-permute-done
  134.8 1.3 add_convert_fusion
  136.1 4.2 %all-to-all-start.2 = ((bf16[4,128,1152]{2,1,0:T(8,128)(2,1)}), bf16[4,128,1152]{2,1,0:T(8,128)(2,1)S(1)}, u32[]{:S(2)}, u32[]{:S(2)}) async-start(bf16[4,128,1152]{2,1,0:T(8,128)(2,1)} %bitcast.6), calls=%async_computation.2 | async-start | bytes 2359296 | tf_op jit(solution)/shard_map/all_to_all | solution.py:70
  140.3 16.3 %all-to-all-done.2 = bf16[4,128,1152]{2,1,0:T(8,128)(2,1)S(1)} async-done(((bf16[4,128,1152]{2,1,0:T(8,128)(2,1)}), bf16[4,128,1152]{2,1,0:T(8,128)(2,1)S(1)}, u32[]{:S(2)}, u32[]{:S(2)}) %all-to-all-start.2) | async-done | bytes 1179680 | tf_op jit(solution)/shard_map/all_to_all | solution.py:70
  156.7 0.2 fusion.32
  156.8 0.1 convert_reduce_fusion
  157.0 0.0 copy-start.1
  157.0 1.1 divide_convert_fusion
  158.1 0.1 broadcast_in_dim.193
  158.2 16.4 %all_to_all.42 = bf16[4,128,1024]{2,1,0:T(8,128)(2,1)S(1)} all-to-all(bf16[4,128,1024]{2,1,0:T(8,128)(2,1)S(1)} %broadcast_in_dim.193), channel_id=1, replica_groups={{0,2,4,6},{1,3,5,7},{8,10,12,14},{9,11,13,15},{16,18,20,22},{17,19,21,2..., dimensions={0} | all-to-all | bytes 2097152 | tf_op jit(solution)/shard_map/all_to_all | solution.py:78
  174.6 2.0 collective-permute-start.1
  176.7 0.0 copy-done.1
  176.7 0.5 multiply_subtract_fusion
  177.1 1.9 collective-permute-done.1
  179.1 2.2 multiply_reduce_fusion
  181.3 0.0 copy-start
  181.3 0.3 select_reduce_fusion
  181.6 1.3 fusion.18
  182.8 0.0 copy-done
  182.8 0.3 select_convert_fusion
  183.2 0.1 pad_maximum_fusion.1
  183.3 18.7 %all_to_all.43 = bf16[4,128,1152]{2,1,0:T(8,128)(2,1)S(1)} all-to-all(bf16[4,128,1152]{2,1,0:T(8,128)(2,1)S(1)} %bitcast.38), channel_id=1, replica_groups={{0,64,128,192},{8,72,136,200},{16,80,144,208},{24,88,152,216},{32,96,16..., dimensions={0} | all-to-all | bytes 2359296 | tf_op jit(solution)/shard_map/all_to_all | solution.py:108
  202.0 0.2 subtract_reduce_fusion
  202.3 0.1 broadcast_in_dim.203
  202.3 0.1 reshape.172
  202.4 0.1 broadcast_in_dim.205
  202.5 0.1 broadcast_in_dim.210
  202.6 0.2 select_convert_fusion.3
  202.8 0.1 slice_reduce_fusion
  202.9 0.7 pad_maximum_fusion.2
  203.6 3.4 %all-to-all-start.5 = ((bf16[8,16,1152]{2,1,0:T(8,128)(2,1)}), bf16[8,16,1152]{2,1,0:T(8,128)(2,1)S(1)}, u32[]{:S(2)}, u32[]{:S(2)}) async-start(bf16[8,16,1152]{2,1,0:T(8,128)(2,1)} %pad_maximum_fusion.2), calls=%async_computation.5 | async-start | bytes 589824 | tf_op jit(solution)/shard_map/all_to_all | solution.py:117
  207.1 10.5 %all-to-all-done.5 = bf16[8,16,1152]{2,1,0:T(8,128)(2,1)S(1)} async-done(((bf16[8,16,1152]{2,1,0:T(8,128)(2,1)}), bf16[8,16,1152]{2,1,0:T(8,128)(2,1)S(1)}, u32[]{:S(2)}, u32[]{:S(2)}) %all-to-all-start.5) | async-done | bytes 294944 | tf_op jit(solution)/shard_map/all_to_all | solution.py:117
  217.6 0.1 copy.22
  217.8 1.0 multiply_reduce_fusion.2
  218.8 0.1 select_convert_fusion.4
  218.9 12.4 %all_to_all.44 = bf16[8,16,1152]{2,1,0:T(8,128)(2,1)S(1)} all-to-all(bf16[8,16,1152]{2,1,0:T(8,128)(2,1)S(1)} %broadcast_in_dim.221), channel_id=1, replica_groups={{0,8,16,24,32,40,48,56},{64,72,80,88,96,104,112,120},{128,136,144,152,1..., dimensions={0} | all-to-all | bytes 589824 | tf_op jit(solution)/shard_map/all_to_all | solution.py:133
  231.4 0.1 broadcast_in_dim.222
  231.5 15.1 %all_to_all.45 = bf16[4,8,16,1152]{3,2,1,0:T(8,128)(2,1)S(1)} all-to-all(bf16[4,8,16,1152]{3,2,1,0:T(8,128)(2,1)S(1)} %broadcast_in_dim.222), channel_id=1, replica_groups={{0,64,128,192},{8,72,136,200},{16,80,144,208},{24,88,152,216},{32,96,16..., dimensions={0} | all-to-all | bytes 2359296 | tf_op jit(solution)/shard_map/all_to_all | solution.py:135
  246.6 1.1 slice.114
  247.7 0.3 copy.23
  248.0 0.6 fusion.39
  248.6 4.8 %collective-permute-start.2 = (f32[]{:T(128)}, f32[]{:T(128)}, u32[]{:S(2)}, u32[]{:S(2)}) collective-permute-start(f32[]{:T(128)} %fusion.39), channel_id=1, source_target_pairs={{0,1},{1,0},{2,3},{3,2},{4,5},{5,4},{6,7},{7,6},{8,9},{9,8},{10,11... | collective-permute-start | bytes 20 | tf_op jit(solution)/shard_map/ppermute | solution.py:141
  253.4 1.0 collective-permute-done.2
  255.7 1.1 collective-permute-start.3
  256.8 1.5 collective-permute-done.3
  259.0 1.4 collective-permute-start.4
  260.3 2.7 %collective-permute-done.4 = f32[]{:T(128)} collective-permute-done((f32[]{:T(128)}, f32[]{:T(128)}, u32[]{:S(2)}, u32[]{:S(2)}) %collective-permute-start.4) | collective-permute-done | bytes 36 | tf_op jit(solution)/shard_map/ppermute | solution.py:145
  263.8 0.7 div.64
  (20 shorter events, 0.3 us)
Async XLA Ops:
  22.5 101.4 %all-to-all-start.1 = ((bf16[32,64,1024]{2,1,0:T(8,128)(2,1)}), bf16[32,64,1024]{2,1,0:T(8,128)(2,1)}, u32[]{:S(2)}, u32[]{:S(2)}) async-start(bf16[32,64,1024]{2,1,0:T(8,128)(2,1)} %bitcast.43), calls=%async_computation.1 | async-start | bytes 8388608 | tf_op jit(solution)/shard_map/all_to_all | solution.py:44
  128.5 6.2 %collective-permute-start = (bf16[512,1152]{1,0:T(8,128)(2,1)S(1)}, bf16[512,1152]{1,0:T(8,128)(2,1)S(1)}, u32[]{:S(2)}, u32[]{:S(2)}) collective-permute-start(bf16[512,1152]{1,0:T(8,128)(2,1)S(1)} %pad_maximum_fusion), channel_id=1, source_target_pairs={{0,1},{1,0},{2,3},{3,2},{4,5},{5,4},{6,7},{7,6},{8,9},{9,8},{10,11... | collective-permute-start | bytes 3538952 | tf_op jit(solution)/shard_map/ppermute | solution.py:66
  136.1 20.5 %all-to-all-start.2 = ((bf16[4,128,1152]{2,1,0:T(8,128)(2,1)}), bf16[4,128,1152]{2,1,0:T(8,128)(2,1)S(1)}, u32[]{:S(2)}, u32[]{:S(2)}) async-start(bf16[4,128,1152]{2,1,0:T(8,128)(2,1)} %bitcast.6), calls=%async_computation.2 | async-start | bytes 2359296 | tf_op jit(solution)/shard_map/all_to_all | solution.py:70
  157.0 19.7 %copy-start.1 = (s32[1024]{0:T(1024)S(1)}, s32[1024]{0:T(1024)}, u32[]{:S(2)}) copy-start(s32[1024]{0:T(1024)} %param.11) | copy-start | bytes 12292
  174.6 4.5 %collective-permute-start.1 = (bf16[512,1024]{1,0:T(8,128)(2,1)S(1)}, bf16[512,1024]{1,0:T(8,128)(2,1)}, u32[]{:S(2)}, u32[]{:S(2)}) collective-permute-start(bf16[512,1024]{1,0:T(8,128)(2,1)S(1)} %bitcast.41), channel_id=1, source_target_pairs={{0,1},{1,0},{2,3},{3,2},{4,5},{5,4},{6,7},{7,6},{8,9},{9,8},{10,11... | collective-permute-start | bytes 3145736 | tf_op jit(solution)/shard_map/ppermute | solution.py:79
  181.3 1.6 copy-start
  203.6 14.0 %all-to-all-start.5 = ((bf16[8,16,1152]{2,1,0:T(8,128)(2,1)}), bf16[8,16,1152]{2,1,0:T(8,128)(2,1)S(1)}, u32[]{:S(2)}, u32[]{:S(2)}) async-start(bf16[8,16,1152]{2,1,0:T(8,128)(2,1)} %pad_maximum_fusion.2), calls=%async_computation.5 | async-start | bytes 589824 | tf_op jit(solution)/shard_map/all_to_all | solution.py:117
  248.6 5.7 %collective-permute-start.2 = (f32[]{:T(128)}, f32[]{:T(128)}, u32[]{:S(2)}, u32[]{:S(2)}) collective-permute-start(f32[]{:T(128)} %fusion.39), channel_id=1, source_target_pairs={{0,1},{1,0},{2,3},{3,2},{4,5},{5,4},{6,7},{7,6},{8,9},{9,8},{10,11... | collective-permute-start | bytes 20 | tf_op jit(solution)/shard_map/ppermute | solution.py:141
  255.7 2.6 collective-permute-start.3
  259.0 4.1 %collective-permute-start.4 = (f32[]{:T(128)}, f32[]{:T(128)}, u32[]{:S(2)}, u32[]{:S(2)}) collective-permute-start(f32[]{:T(128)} %add.133), channel_id=1, source_target_pairs={{0,4},{1,5},{2,6},{3,7},{4,0},{5,1},{6,2},{7,3},{8,12},{9,13},{10,... | collective-permute-start | bytes 20 | tf_op jit(solution)/shard_map/ppermute | solution.py:145
